TPU v7x, 128 devices: a whole 4x4x4 slice. The times are simulated.
128 devices in a mesh: seq: 32 (over x, z_hi, y), exp: 4 (over z_lo, core).
Axes of the slice: x: 4, y: 4, z: 4 (z_hi: 2, z_lo: 2; z = z_hi * 2 + z_lo), core: 2. Of those that a mesh axis runs over, the one named last changes fastest.
Arguments:
- segment_ids: int32 [8192], replicated, may hold values from 0 to 130, as said below
- queries: bfloat16 [8192, 2048], P('seq', 'exp'), may hold values from -8 to 8
- keys: bfloat16 [8192, 2048], P('seq', 'exp'), may hold values from -8 to 8
- values: bfloat16 [8192, 2048], P('seq', 'exp'), may hold values from -6 to 6
- out_weight: bfloat16 [2048, 2048], P('exp'), may hold values from -0.125 to 0.125
- residual: bfloat16 [8192, 2048], P('seq'), may hold values from -16 to 16
- norm_gain: bfloat16 [2048], replicated, may hold values from 0.099609375 to 1.8984375
- shared_in: bfloat16 [2, 2048, 3072], P(None, None, 'exp'), may hold values from -0.125 to 0.125
- shared_out: bfloat16 [3072, 2048], P('exp'), may hold values from -0.109375 to 0.109375
- shared_gate: bfloat16 [2048], replicated, may hold values from -0.125 to 0.125
- expert_in: bfloat16 [64, 2, 2048, 1408], P('seq', None, None, 'exp'), may hold values from -0.125 to 0.125
- expert_out: bfloat16 [64, 1408, 2048], P('seq', 'exp'), may hold values from -0.15625 to 0.15625
- expert_ids: int32 [8192, 4], P('seq'), may hold values from 0 to 59, all different within a row; in each aligned block of 256 rows (0 to 255, 256 to 511, ...) at most 32 rows name the same one
- gate_weights: float32 [8192, 4], P('seq'), may hold values from 0.05 to 0.5
Outputs:
- mixed: bfloat16 [8192, 2048], P(('seq', 'exp'))
- attn_proj: bfloat16 [8192, 2048], P(('seq', 'exp'))
- key_cache: bfloat16 [8192, 2048], P('seq', 'exp')
Inputs may be any that keep to these rules, and one draw needn't show every extreme that they name: `segment_ids`: never falls along the stream, starts at 0 and rises by at most one from a token to the next; there are exactly (2048) // 16 + 3 prompts; one prompt has exactly 6144 tokens, every other fewer. `expert_ids`: each row names 4 different experts; in each aligned block of 256 rows (the rows of one block of the stream) no expert is named by more than 32 rows, a bound that some block reaches.
All inputs are finite; a program needn't handle non-finite values.
Results may differ from a plain program's by a relative error of at most 0.012.
Values may be sent and summed in bfloat16 or wider, within the bound.
No kernel may reach another device: no remote copies, remote signals or barrier semaphores. Data moves between devices by JAX's collectives and lax.ppermute only.
A program may use at most 128 MiB of HBM per device.

v0:
```python
import math

import jax
import jax.numpy as jnp
from jax import lax
from jax.sharding import PartitionSpec as P

HD = 128
TOPK = 4
SLOTS = 64
CAP = 32


rope_base = 1000000.0
neg_fill = -1e30
norm_eps = 1e-06


def token_positions(segment_ids):
    stream_len = segment_ids.shape[0]
    token_index = jnp.arange(stream_len, dtype=jnp.int32)
    boundary = jnp.concatenate([jnp.ones((1,), jnp.bool_), segment_ids[1:] != segment_ids[:-1]])
    seg_start = lax.cummax(jnp.where(boundary, token_index, 0), axis=0)
    return (token_index - seg_start, seg_start)


def rotate(values_in, positions, head_count):
    half_dim = HD // 2
    frequency = rope_base ** (-(2.0 * jnp.arange(half_dim, dtype=jnp.float32)) / HD)
    angle_all = positions.astype(jnp.float32)[:, None] * frequency[None, :]
    cosine = jnp.cos(angle_all)[:, None, :]
    sine_part = jnp.sin(angle_all)[:, None, :]
    shaped = values_in.astype(jnp.float32).reshape(values_in.shape[0], head_count, HD)
    first_half = shaped[..., :half_dim]
    second_half = shaped[..., half_dim:]
    turned = jnp.concatenate(
        [
            first_half * cosine - second_half * sine_part,
            second_half * cosine + first_half * sine_part,
        ],
        axis=-1,
    )
    return turned.reshape(values_in.shape[0], head_count * HD).astype(jnp.bfloat16)


def rms_norm(hidden_in, norm_gain):
    mean_square = jnp.mean(hidden_in * hidden_in, axis=-1, keepdims=True)
    return (hidden_in * lax.rsqrt(mean_square + norm_eps) * norm_gain.astype(jnp.float32)).astype(
        jnp.bfloat16
    )


def expert_parts(incoming, expert_in, expert_out):
    expert_pre = jnp.einsum(
        "nscd,sgde->nscge", incoming, expert_in, preferred_element_type=jnp.float32
    )
    expert_hidden = (jax.nn.silu(expert_pre[..., 0, :]) * expert_pre[..., 1, :]).astype(
        jnp.bfloat16
    )
    return jnp.einsum(
        "nsce,sed->nscd", expert_hidden, expert_out, preferred_element_type=jnp.float32
    ).astype(jnp.bfloat16)


def body(
    segment_ids,
    queries,
    keys,
    values,
    out_weight,
    residual,
    norm_gain,
    shared_in,
    shared_out,
    shared_gate,
    expert_in,
    expert_out,
    expert_ids,
    gate_weights,
):
    seq_count = lax.axis_size("seq")
    exp_count = lax.axis_size("exp")
    seq_place = lax.axis_index("seq")
    exp_place = lax.axis_index("exp")
    block_len = queries.shape[0]
    stream_len = segment_ids.shape[0]
    local_heads = queries.shape[1] // HD
    block_first = seq_place * block_len
    positions, seg_start = token_positions(segment_ids)
    local_pos = lax.dynamic_slice_in_dim(positions, block_first, block_len, 0)
    query_seg = lax.dynamic_slice_in_dim(segment_ids, block_first, block_len, 0)
    rotated_q = rotate(queries, local_pos, local_heads).reshape(block_len, local_heads, HD)
    key_cache = rotate(keys, local_pos, local_heads)
    score_scale = 1.0 / math.sqrt(HD)
    query_pos = block_first + jnp.arange(block_len, dtype=jnp.int32)

    def attend(state_now, key_rows, value_rows, key_first):
        width_keys = key_rows.shape[0]
        run_max, run_sum, run_acc = state_now
        scores = (
            jnp.einsum(
                "qhd,khd->hqk",
                rotated_q,
                key_rows.reshape(width_keys, local_heads, HD),
                preferred_element_type=jnp.float32,
            )
            * score_scale
        )
        key_pos = key_first + jnp.arange(width_keys, dtype=jnp.int32)
        key_seg = lax.dynamic_slice_in_dim(
            segment_ids, jnp.clip(key_first, 0, stream_len - width_keys), width_keys, 0
        )
        visible = (
            True
            & (key_pos[None, :] <= query_pos[:, None])
            & (key_seg[None, :] == query_seg[:, None])
        )
        new_max = jnp.maximum(run_max, jnp.max(jnp.where(visible[None], scores, neg_fill), axis=-1))
        weights_f = jnp.where(visible[None], jnp.exp(scores - new_max[..., None]), 0.0)
        rescale = jnp.exp(run_max - new_max)
        weights_b = weights_f.astype(jnp.bfloat16)
        gathered = jnp.einsum(
            "hqk,khd->hqd",
            weights_b,
            value_rows.reshape(width_keys, local_heads, HD),
            preferred_element_type=jnp.float32,
        )
        return (
            new_max,
            run_sum * rescale + jnp.sum(weights_f, axis=-1),
            run_acc * rescale[..., None] + gathered,
        )

    init_state = (
        jnp.full((local_heads, block_len), neg_fill, jnp.float32),
        jnp.zeros((local_heads, block_len), jnp.float32),
        jnp.zeros((local_heads, block_len, HD), jnp.float32),
    )
    pieces = (
        lax.all_gather(key_cache, "seq", axis=0, tiled=True),
        lax.all_gather(values, "seq", axis=0, tiled=True),
    )
    piece_len = pieces[0].shape[0]
    step_len = math.gcd(piece_len, 512)

    def inner_step(step_id, state_in):
        row_start = step_id * step_len
        key_rows = lax.dynamic_slice_in_dim(pieces[0], row_start, step_len, 0)
        value_rows = lax.dynamic_slice_in_dim(pieces[1], row_start, step_len, 0)
        return attend(state_in, key_rows, value_rows, row_start)

    final_state = lax.fori_loop(0, piece_len // step_len, inner_step, init_state)
    run_max, run_sum, run_acc = final_state
    attended = (
        (run_acc / run_sum[..., None])
        .transpose(1, 0, 2)
        .reshape(block_len, local_heads * HD)
        .astype(jnp.bfloat16)
    )
    attn_part = jnp.dot(attended, out_weight, preferred_element_type=jnp.float32)
    row_count = block_len // exp_count
    row_first = exp_place * row_count
    residual_f = residual.astype(jnp.float32)
    attn_sum = lax.psum(attn_part.astype(jnp.bfloat16), "exp").astype(jnp.float32)
    after_attn = residual_f + attn_sum
    normed = rms_norm(after_attn, norm_gain)
    attn_rows = lax.dynamic_slice_in_dim(attn_sum, row_first, row_count, 0).astype(jnp.bfloat16)
    after_rows = lax.dynamic_slice_in_dim(after_attn, row_first, row_count, 0)
    shared_pre = jnp.einsum("td,gde->tge", normed, shared_in, preferred_element_type=jnp.float32)
    shared_hidden = (jax.nn.silu(shared_pre[:, 0]) * shared_pre[:, 1]).astype(jnp.bfloat16)
    shared_term = jnp.dot(shared_hidden, shared_out, preferred_element_type=jnp.float32)
    shared_factor = jax.nn.sigmoid(jnp.dot(normed, shared_gate, preferred_element_type=jnp.float32))
    flat_ids = expert_ids.reshape(-1)
    one_hot = (flat_ids[:, None] == jnp.arange(SLOTS, dtype=jnp.int32)[None, :]).astype(jnp.int32)
    slot_rank = jnp.sum(jnp.cumsum(one_hot, axis=0) * one_hot, axis=1) - 1
    slot_place = flat_ids * CAP + slot_rank
    owner_row = jnp.arange(flat_ids.shape[0], dtype=jnp.int32) // TOPK
    source_row = jnp.full((SLOTS * CAP,), -1, jnp.int32).at[slot_place].set(owner_row)
    slot_local = SLOTS // seq_count
    model_width = normed.shape[1]
    outgoing = jnp.where(
        (source_row >= 0)[:, None], normed[jnp.maximum(source_row, 0)], jnp.zeros((), jnp.bfloat16)
    ).reshape(seq_count, slot_local, CAP, model_width)
    col_count = model_width // exp_count
    col_first = exp_place * col_count
    outgoing_part = lax.dynamic_slice_in_dim(outgoing, col_first, col_count, 3)
    incoming = lax.all_gather(
        lax.all_to_all(outgoing_part, "seq", split_axis=0, concat_axis=0, tiled=True),
        "exp",
        axis=3,
        tiled=True,
    )
    expert_part = expert_parts(incoming, expert_in, expert_out)
    summed = lax.psum_scatter(
        expert_part.astype(jnp.float32).astype(jnp.bfloat16), "exp", scatter_dimension=3, tiled=True
    ).astype(jnp.float32)
    returned = lax.all_to_all(
        summed.astype(jnp.bfloat16), "seq", split_axis=0, concat_axis=0, tiled=True
    ).astype(summed.dtype)
    picked = returned.reshape(SLOTS * CAP, col_count)[slot_place].reshape(
        block_len, TOPK, col_count
    )
    moe_cols = jnp.sum(gate_weights[:, :, None] * picked, axis=1)
    moe_term = lax.dynamic_update_slice_in_dim(
        jnp.zeros((block_len, model_width), jnp.float32), moe_cols, col_first, 1
    )
    combined = shared_factor[:, None] * shared_term + moe_term
    moe_rows = lax.psum_scatter(
        combined.astype(jnp.bfloat16), "exp", scatter_dimension=0, tiled=True
    ).astype(jnp.float32)
    mixed_out = (after_rows + moe_rows).astype(jnp.bfloat16)
    return (mixed_out, attn_rows, key_cache)


def solution(mesh):
    return jax.shard_map(
        body,
        mesh=mesh,
        in_specs=(
            P(),
            P("seq", "exp"),
            P("seq", "exp"),
            P("seq", "exp"),
            P("exp", None),
            P("seq", None),
            P(),
            P(None, None, "exp"),
            P("exp", None),
            P(),
            P("seq", None, None, "exp"),
            P("seq", "exp", None),
            P("seq", None),
            P("seq", None),
        ),
        out_specs=(P(("seq", "exp"), None), P(("seq", "exp"), None), P("seq", "exp")),
        check_vma=False,
    )
```

profile of v0, /device:TPU:1, one launch (start us, length us, event | category | flops | bytes accessed | tf_op | source)
XLA Modules:
  0.0 834.0 jit_solution(13940769842598370679)
XLA Ops:
  20.9 34.2 %reduce-window.19 = s32[64,8,128]{2,1,0:T(8,128)} reduce-window(s32[64,8,128]{2,1,0:T(8,128)} %fusion.36, s32[]{:T(128)} %constant.119.clone.1), window={size=1x1x128 pad=0_0x0_0x127_0}, to_apply=%region_8.9 | reduce-window | flops 8323072 | bytes 524292 | tf_op jit(solution)/shard_map/reduce-window.2
  63.0 85.7 %all-gather.4.cloned.1.call-done = bf16[8192,512]{0,1:T(8,128)(2,1)} async-done(((bf16[256,512]{0,1:T(8,128)(2,1)}), bf16[8192,512]{0,1:T(8,128)(2,1)}) %all-gather.4.cloned.1.call-update) | async-done | bytes 8388624 | tf_op jit(solution)/shard_map/all_gather | solution.py:140
  148.7 131.5 %all-gather.6.cloned.1.call-done = bf16[8192,512]{0,1:T(8,128)(2,1)} async-done(((bf16[256,512]{0,1:T(8,128)(2,1)}), bf16[8192,512]{0,1:T(8,128)(2,1)}) %all-gather.6.cloned.1.call-update) | async-done | bytes 8388624 | tf_op jit(solution)/shard_map/all_gather | solution.py:141
  280.3 179.6 %while.18 = (s32[]{:T(128)}, f32[4,256]{1,0:T(4,128)S(1)}, f32[4,256]{1,0:T(4,128)S(1)}, f32[4,256,128]{2,1,0:T(8,128)}, s32[8192]{0:T(1024)}, /*index=5*/s32[25...) while((s32[]{:T(128)}, f32[4,256]{1,0:T(4,128)S(1)}, ...), condition=%wide.region_5.6_spmd.clone, body=%wide.region_2.5_spmd.clone.sunk | while | flops 274994944 | bytes 19739916 | solution.py:152
  283.5 2.9 fusion.66
  294.6 2.9 fusion.66
  299.8 2.8 convolution_add_fusion.2
  305.8 2.9 fusion.66
  311.0 2.8 convolution_add_fusion.2
  317.1 2.9 fusion.66
  322.3 2.8 convolution_add_fusion.2
  328.3 2.9 fusion.66
  333.5 2.8 convolution_add_fusion.2
  339.5 2.9 fusion.66
  344.7 2.8 convolution_add_fusion.2
  350.8 2.9 fusion.66
  356.0 2.8 convolution_add_fusion.2
  362.0 2.9 fusion.66
  367.2 2.8 convolution_add_fusion.2
  373.3 2.9 fusion.66
  378.4 2.8 convolution_add_fusion.2
  384.5 2.9 fusion.66
  395.7 2.9 fusion.66
  407.0 2.9 fusion.66
  418.2 2.9 fusion.66
  429.4 2.9 fusion.66
  440.7 2.9 fusion.66
  445.8 2.8 convolution_add_fusion.2
  451.9 2.9 fusion.66
  463.0 3.4 convolution_convert_fusion
  468.2 4.5 scatter_custom_fusion
  472.8 33.6 %all-reduce.2.cloned.1.call-done = bf16[256,2048]{1,0:T(8,128)(2,1)} async-done(((bf16[256,2048]{1,0:T(8,128)(2,1)}), bf16[256,2048]{1,0:T(8,128)(2,1)}) %all-reduce.2.cloned.1.call-update) | async-done | bytes 1048592 | tf_op jit(solution)/shard_map/psum | solution.py:164
  506.4 3.4 convert_add_fusion
  511.4 17.7 %gather_fusion = bf16[2048,2048]{1,0:T(8,128)(2,1)} fusion(bf16[256,2048]{1,0:T(8,128)(2,1)} %multiply_convert_fusion, s32[2048]{0:T(1024)S(1)} %maximum_clamp_fusion), kind=kCustom, calls=%fused_computation | custom fusion | bytes 16785408 | tf_op jit(solution)/shard_map/gather | solution.py:182
  531.0 36.8 %all_to_all.10 = bf16[32,2,32,512]{3,2,1,0:T(8,128)(2,1)S(1)} all-to-all(bf16[32,2,32,512]{3,2,1,0:T(8,128)(2,1)S(1)} %dynamic-slice_select_fusion), channel_id=1, replica_groups=mesh['seq'=32,'exp'=4] {'seq'}, dimensions={0} | all-to-all | bytes 4194304 | tf_op jit(solution)/shard_map/all_to_all | solution.py:188
  569.6 79.5 %all-gather.8.cloned.1.call-done = bf16[32,2,32,2048]{3,2,0,1:T(8,128)(2,1)} async-done(((bf16[32,2,32,512]{3,2,0,1:T(8,128)(2,1)}), bf16[32,2,32,2048]{3,2,0,1:T(8,128)(2,1)}) %all-gather.8.cloned.1.call-update) | async-done | bytes 8388624 | tf_op jit(solution)/shard_map/all_gather | solution.py:187
  649.1 10.1 %fusion.21 = f32[32,2,32,2,352]{4,2,3,0,1:T(8,128)S(1)} fusion(bf16[2,2,2048,352]{2,3,1,0:T(8,128)(2,1)} %param.26, bf16[32,2,32,2048]{3,2,0,1:T(8,128)(2,1)} %all-gather.8.cloned.1.call-done), kind=kOutput, calls=%fused_computation.38 | convolution fusion | flops 5905580032 | bytes 19922944 | tf_op jit(solution)/shard_map/nscd,sgde->nscge/dot_general | solution.py:54
  659.3 6.7 convert_bitcast_fusion
  666.0 80.0 %reduce-scatter.3.cloned.1.call-done = bf16[32,2,32,512]{3,2,0,1:T(8,128)(2,1)} async-done(((bf16[32,2,32,2048]{3,2,0,1:T(8,128)(2,1)}), bf16[32,2,32,512]{3,2,0,1:T(8,128)(2,1)}) %reduce-scatter.3.cloned.1.call-update) | async-done | bytes 2097168 | tf_op jit(solution)/shard_map/reduce_scatter | solution.py:194
  746.0 3.2 copy.56
  749.1 9.4 %all-to-all-start.1 = ((bf16[32,2,32,512]{3,2,1,0:T(8,128)(2,1)}), bf16[32,2,32,512]{3,2,1,0:T(8,128)(2,1)}, u32[]{:S(2)}, u32[]{:S(2)}) async-start(bf16[32,2,32,512]{3,2,1,0:T(8,128)(2,1)} %copy.56), calls=%async_computation.2 | async-start | bytes 4194304 | tf_op jit(solution)/shard_map/all_to_all | solution.py:197
  760.4 4.9 fusion.28
  767.7 19.7 %all-to-all-done.1 = bf16[32,2,32,512]{3,2,1,0:T(8,128)(2,1)} async-done(((bf16[32,2,32,512]{3,2,1,0:T(8,128)(2,1)}), bf16[32,2,32,512]{3,2,1,0:T(8,128)(2,1)}, u32[]{:S(2)}, u32[]{:S(2)}) %all-to-all-start.1) | async-done | bytes 2097184 | tf_op jit(solution)/shard_map/all_to_all | solution.py:197
  787.4 4.1 bitcast_convert_fusion
  791.5 7.5 gather_fusion.1
  799.0 2.9 reshape.255
  801.9 3.1 multiply_reduce_fusion
  808.8 16.5 %reduce-scatter.5.cloned.1.call-done = bf16[64,2048]{1,0:T(8,128)(2,1)} async-done(((bf16[256,2048]{1,0:T(8,128)(2,1)}), bf16[64,2048]{1,0:T(8,128)(2,1)}) %reduce-scatter.5.cloned.1.call-update) | async-done | bytes 262160 | tf_op jit(solution)/shard_map/reduce_scatter | solution.py:208
  (282 shorter events, 148.6 us)
Async XLA Ops:
  7.2 758.1 %copy-start = (bf16[768,2048]{1,0:T(8,128)(2,1)S(1)}, bf16[768,2048]{1,0:T(8,128)(2,1)}, u32[]{:S(2)}) copy-start(bf16[768,2048]{1,0:T(8,128)(2,1)} %param.24) | copy-start | bytes 9437188
  7.2 141.6 %all-gather.4.cloned.1.call-start = ((), (), s32[]{:S(2)}) async-start(), calls=%async_computation.4 | async-start | bytes 8650752 | tf_op jit(solution)/shard_map/all_gather | solution.py:140
  13.3 6.6 copy-start.9
  15.4 264.9 %all-gather.6.cloned.1.call-start = ((), (), s32[]{:S(2)}) async-start(), calls=%async_computation.5 | async-start | bytes 8650752 | tf_op jit(solution)/shard_map/all_gather | solution.py:141
  17.2 489.2 %all-reduce.2.cloned.1.call-start = ((), (), s32[]{:S(2)}) async-start(), calls=%async_computation.6 | async-start | bytes 2097152 | tf_op jit(solution)/shard_map/psum | solution.py:164
  20.0 260.2 %copy-start.6 = (s32[256,4]{1,0:T(8,128)}, s32[256,4]{1,0:T(8,128)S(1)}, u32[]{:S(2)}) copy-start(s32[256,4]{1,0:T(8,128)S(1)} %copy.50) | copy-start | bytes 12292
  286.5 2.2 copy-start.1
  297.6 2.2 copy-start.1
  308.8 2.2 copy-start.1
  320.0 2.2 copy-start.1
  331.3 2.2 copy-start.1
  342.5 2.2 copy-start.1
  353.7 2.2 copy-start.1
  365.0 2.2 copy-start.1
  376.2 2.2 copy-start.1
  387.4 2.2 copy-start.1
  398.7 2.2 copy-start.1
  409.9 2.2 copy-start.1
  421.1 2.2 copy-start.1
  432.4 2.2 copy-start.1
  443.6 2.2 copy-start.1
  454.8 2.2 copy-start.1
  463.0 4.1 copy-start.7
  463.0 4.9 copy-start.10
  463.0 5.1 copy-start.8
  466.4 182.7 %all-gather.8.cloned.1.call-start = ((), (), s32[]{:S(2)}) async-start(), calls=%async_computation.7 | async-start | bytes 10485760 | tf_op jit(solution)/shard_map/all_gather | solution.py:187
  506.4 3.4 copy-start.2
  506.4 3.4 copy-start.3
  569.4 176.6 %reduce-scatter.3.cloned.1.call-start = ((), (), s32[]{:S(2)}) async-start(), calls=%async_computation.8 | async-start | bytes 10485760 | tf_op jit(solution)/shard_map/reduce_scatter | solution.py:194
  649.1 10.2 %copy-start.13 = (bf16[2,352,2048]{2,1,0:T(8,128)(2,1)S(1)}, bf16[2,352,2048]{2,1,0:T(8,128)(2,1)}, u32[]{:S(2)}) copy-start(bf16[2,352,2048]{2,1,0:T(8,128)(2,1)} %param.27) | copy-start | bytes 8650756
  749.1 9.4 %copy-start.11 = (f32[256,4]{0,1:T(4,128)S(1)}, f32[256,4]{0,1:T(4,128)}, u32[]{:S(2)}) copy-start(f32[256,4]{0,1:T(4,128)} %param.29) | copy-start | bytes 12292
  749.1 9.6 %copy-start.12 = (bf16[2048]{0:T(1024)(128)(2,1)S(1)}, bf16[2048]{0:T(1024)(128)(2,1)}, u32[]{:S(2)}) copy-start(bf16[2048]{0:T(1024)(128)(2,1)} %param.25) | copy-start | bytes 12292
  749.1 38.2 %all-to-all-start.1 = ((bf16[32,2,32,512]{3,2,1,0:T(8,128)(2,1)}), bf16[32,2,32,512]{3,2,1,0:T(8,128)(2,1)}, u32[]{:S(2)}, u32[]{:S(2)}) async-start(bf16[32,2,32,512]{3,2,1,0:T(8,128)(2,1)} %copy.56), calls=%async_computation.2 | async-start | bytes 4194304 | tf_op jit(solution)/shard_map/all_to_all | solution.py:197
  758.5 66.7 %reduce-scatter.5.cloned.1.call-start = ((), (), s32[]{:S(2)}) async-start(), calls=%async_computation.9 | async-start | bytes 1310720 | tf_op jit(solution)/shard_map/reduce_scatter | solution.py:208
  801.9 3.1 copy-start.4
  805.1 1.2 copy-start.5
Sparse Core Ops, SparseCore 0:
  15.5 133.2 all-gather.3
  152.1 128.1 all-gather.5
  466.5 39.8 all-reduce.1
  569.5 79.5 all-gather.7
  666.1 79.7 reduce-scatter.2
  806.4 18.8 reduce-scatter.4
where the time goes:
time: 839 us; the launch traced here: 834 us
  waiting for transfers between devices  447 us (53%)
  matrix products  121 us (14%)
  other arithmetic  104 us (12%)
  local copies, waits for them, and re-layouts  102 us (12%)
  blocking collectives  36.8 us (4%)
  between operations  14.5 us (2%)
  starting transfers between devices  9.79 us (1%)
    all_gather x1, waiting for transfers between devices, body(): lax.all_gather(values, 'seq', axis=0, tiled=True)  132 us
    all_gather x1, waiting for transfers between devices, body(): lax.all_gather(key_cache, 'seq', axis=0, tiled=True)  85.7 us
    reduce_scatter x1, waiting for transfers between devices, body(): lax.psum_scatter(expert_part.astype(jnp.float32).astype(jnp.bfloat16), 'e...  80 us
    all_gather x1, waiting for transfers between devices, body(): lax.all_gather(lax.all_to_all(outgoing_part, 'seq', split_axis=0, concat_...  79.5 us
    dot_general x16, matrix products, attend(): jnp.einsum('qhd,khd->hqk', rotated_q, key_rows.reshape(width_keys, local_...  47.1 us
    dot_general x16, matrix products, attend(): jnp.einsum('hqk,khd->hqd', weights_b, value_rows.reshape(width_keys, loca...  44.4 us
    another operation x6, other arithmetic  38.3 us
    all_to_all x1, blocking collectives, body(): lax.all_to_all(outgoing_part, 'seq', split_axis=0, concat_axis=0, tiled=T...  36.8 us
  transfers between devices with their start and end apart: 7, of which 7 were waited for; matrix products, arithmetic and copies ran while one was open for 8% of the time, Pallas kernels for 0%

commit v1 on v0

--- a/solution.py
+++ b/solution.py
@@ -86,9 +86,9 @@
     stream_len = segment_ids.shape[0]
     local_heads = queries.shape[1] // HD
     block_first = seq_place * block_len
-    positions, seg_start = token_positions(segment_ids)
-    local_pos = lax.dynamic_slice_in_dim(positions, block_first, block_len, 0)
     query_seg = lax.dynamic_slice_in_dim(segment_ids, block_first, block_len, 0)
+    local_start = jnp.sum((segment_ids[None, :] < query_seg[:, None]).astype(jnp.int32), axis=1)
+    local_pos = block_first + jnp.arange(block_len, dtype=jnp.int32) - local_start
     rotated_q = rotate(queries, local_pos, local_heads).reshape(block_len, local_heads, HD)
     key_cache = rotate(keys, local_pos, local_heads)
     score_scale = 1.0 / math.sqrt(HD)
@@ -149,7 +149,9 @@
         value_rows = lax.dynamic_slice_in_dim(pieces[1], row_start, step_len, 0)
         return attend(state_in, key_rows, value_rows, row_start)
 
-    final_state = lax.fori_loop(0, piece_len // step_len, inner_step, init_state)
+    first_chunk = local_start[0] // step_len
+    end_chunk = (block_first + block_len + step_len - 1) // step_len
+    final_state = lax.fori_loop(first_chunk, end_chunk, inner_step, init_state)
     run_max, run_sum, run_acc = final_state
     attended = (
         (run_acc / run_sum[..., None])

time: 839 us -> 750 us (0.89)
  matrix products: 121 us -> 31.7 us
  waiting for transfers between devices: 447 us -> 529 us
  local copies, waits for them, and re-layouts: 102 us -> 57.5 us
  other arithmetic: 104 us -> 63.2 us
    psum x1, waiting for transfers between devices: 33.6 us -> 117 us  [body(): lax.psum(attn_part.astype(jnp.bfloat16), 'exp').astype(jnp.float32)]
    dot_general x16 -> x1, matrix products: 47.1 us -> 1.69 us  [attend(): jnp.einsum('qhd,khd->hqk', rotated_q, key_rows.reshape(width_keys, local_...]
    dot_general x16 -> x1, matrix products: 44.4 us -> 0.88 us  [attend(): jnp.einsum('hqk,khd->hqd', weights_b, value_rows.reshape(width_keys, loca...]
    reduce_sum x16 -> x1, other arithmetic: 35.2 us -> 0.46 us  [attend(): jnp.sum(weights_f, axis=-1)]
    dynamic_slice x16 -> x1, local copies, waits for them, and re-layouts: 36.3 us -> 2.24 us  [inner_step(): value_rows = lax.dynamic_slice_in_dim(pieces[1], row_start, step_len, 0)]
    dynamic_slice x16 -> x1, local copies, waits for them, and re-layouts: 12.3 us -> 0.77 us  [attend(): lax.dynamic_slice_in_dim(segment_ids, jnp.clip(key_first, 0, stream_len -...]
    another operation x7 -> x4, other arithmetic: 38.4 us -> 37.1 us
where the time goes in v1:
time: 750 us; the launch traced here: 746 us
  waiting for transfers between devices  529 us (71%)
  other arithmetic  63.2 us (8%)
  local copies, waits for them, and re-layouts  57.5 us (8%)
  blocking collectives  36.8 us (5%)
  matrix products  31.7 us (4%)
  between operations  17.1 us (2%)
  starting transfers between devices  9.81 us (1%)
    all_gather x1, waiting for transfers between devices, body(): lax.all_gather(values, 'seq', axis=0, tiled=True)  132 us
    psum x1, waiting for transfers between devices, body(): lax.psum(attn_part.astype(jnp.bfloat16), 'exp').astype(jnp.float32)  117 us
    all_gather x1, waiting for transfers between devices, body(): lax.all_gather(key_cache, 'seq', axis=0, tiled=True)  85.3 us
    reduce_scatter x1, waiting for transfers between devices, body(): lax.psum_scatter(expert_part.astype(jnp.float32).astype(jnp.bfloat16), 'e...  79.9 us
    all_gather x1, waiting for transfers between devices, body(): lax.all_gather(lax.all_to_all(outgoing_part, 'seq', split_axis=0, concat_...  79.5 us
    another operation x4, other arithmetic  37.1 us
    all_to_all x1, blocking collectives, body(): lax.all_to_all(outgoing_part, 'seq', split_axis=0, concat_axis=0, tiled=T...  36.8 us
    all_to_all x1, waiting for transfers between devices, body(): lax.all_to_all(summed.astype(jnp.bfloat16), 'seq', split_axis=0, concat_a...  19.7 us
  transfers between devices with their start and end apart: 7, of which 7 were waited for; matrix products, arithmetic and copies ran while one was open for 8% of the time, Pallas kernels for 0%

profile of v1, /device:TPU:1, one launch (start us, length us, event | category | flops | bytes accessed | tf_op | source)
XLA Modules:
  0.0 745.5 jit_solution(7431968535885015745)
XLA Ops:
  7.2 0.9 dynamic_slice.21
  8.2 1.7 convert_reduce_fusion
  9.9 1.1 copy.61
  11.8 1.1 copy.62
  13.3 1.2 subtract_convert_fusion
  15.3 1.8 copy.63
  21.0 1.1 copy.64
  23.1 34.1 %reduce-window.6 = s32[64,8,128]{2,1,0:T(8,128)} reduce-window(s32[64,8,128]{2,1,0:T(8,128)} %fusion.35, s32[]{:T(128)} %constant.99.clone.1), window={size=1x1x128 pad=0_0x0_0x127_0}, to_apply=%region_7.8 | reduce-window | flops 8323072 | bytes 524292 | tf_op jit(solution)/shard_map/reduce-window
  57.3 1.8 slice.54
  59.0 1.1 copy.70
  61.5 1.8 broadcast_add_fusion
  63.3 85.3 %all-gather.4.cloned.1.call-done = bf16[8192,512]{0,1:T(8,128)(2,1)} async-done(((bf16[256,512]{0,1:T(8,128)(2,1)}), bf16[8192,512]{0,1:T(8,128)(2,1)}) %all-gather.4.cloned.1.call-update) | async-done | bytes 8388624 | tf_op jit(solution)/shard_map/all_gather | solution.py:140
  148.6 131.5 %all-gather.6.cloned.1.call-done = bf16[8192,512]{0,1:T(8,128)(2,1)} async-done(((bf16[256,512]{0,1:T(8,128)(2,1)}), bf16[8192,512]{0,1:T(8,128)(2,1)}) %all-gather.6.cloned.1.call-update) | async-done | bytes 8388624 | tf_op jit(solution)/shard_map/all_gather | solution.py:141
  280.1 0.8 broadcast_in_dim.48
  281.0 7.2 while.15
  281.0 2.2 constant_dynamic-slice_fusion.3
  284.2 1.7 fusion.63
  286.4 0.9 convolution_add_fusion.2
  288.1 2.0 copy.65
  290.2 1.1 divide_convert_fusion
  291.3 3.3 convolution_convert_fusion
  296.5 4.5 scatter_custom_fusion
  301.1 116.9 %all-reduce.2.cloned.1.call-done = bf16[256,2048]{1,0:T(8,128)(2,1)} async-done(((bf16[256,2048]{1,0:T(8,128)(2,1)}), bf16[256,2048]{1,0:T(8,128)(2,1)}) %all-reduce.2.cloned.1.call-update) | async-done | bytes 1048592 | tf_op jit(solution)/shard_map/psum | solution.py:166
  418.0 3.4 convert_add_fusion
  421.4 1.5 multiply_convert_fusion
  422.9 17.7 %gather_fusion = bf16[2048,2048]{1,0:T(8,128)(2,1)} fusion(bf16[256,2048]{1,0:T(8,128)(2,1)} %multiply_convert_fusion, s32[2048]{0:T(1024)S(1)} %maximum_clamp_fusion), kind=kCustom, calls=%fused_computation | custom fusion | bytes 16785408 | tf_op jit(solution)/shard_map/gather | solution.py:184
  440.6 1.9 dynamic-slice_select_fusion
  442.6 36.8 %all_to_all.10 = bf16[32,2,32,512]{3,2,1,0:T(8,128)(2,1)S(1)} all-to-all(bf16[32,2,32,512]{3,2,1,0:T(8,128)(2,1)S(1)} %dynamic-slice_select_fusion), channel_id=1, replica_groups=mesh['seq'=32,'exp'=4] {'seq'}, dimensions={0} | all-to-all | bytes 4194304 | tf_op jit(solution)/shard_map/all_to_all | solution.py:190
  479.3 1.6 copy.72
  481.2 79.5 %all-gather.8.cloned.1.call-done = bf16[32,2,32,2048]{3,2,0,1:T(8,128)(2,1)} async-done(((bf16[32,2,32,512]{3,2,0,1:T(8,128)(2,1)}), bf16[32,2,32,2048]{3,2,0,1:T(8,128)(2,1)}) %all-gather.8.cloned.1.call-update) | async-done | bytes 8388624 | tf_op jit(solution)/shard_map/all_gather | solution.py:189
  560.7 10.1 %fusion.20 = f32[32,2,32,2,352]{4,2,3,0,1:T(8,128)S(1)} fusion(bf16[2,2,2048,352]{2,3,1,0:T(8,128)(2,1)} %param.26, bf16[32,2,32,2048]{3,2,0,1:T(8,128)(2,1)} %all-gather.8.cloned.1.call-done), kind=kOutput, calls=%fused_computation.36 | convolution fusion | flops 5905580032 | bytes 19922944 | tf_op jit(solution)/shard_map/nscd,sgde->nscge/dot_general | solution.py:54
  570.8 6.7 convert_bitcast_fusion
  577.6 79.9 %reduce-scatter.3.cloned.1.call-done = bf16[32,2,32,512]{3,2,0,1:T(8,128)(2,1)} async-done(((bf16[32,2,32,2048]{3,2,0,1:T(8,128)(2,1)}), bf16[32,2,32,512]{3,2,0,1:T(8,128)(2,1)}) %reduce-scatter.3.cloned.1.call-update) | async-done | bytes 2097168 | tf_op jit(solution)/shard_map/reduce_scatter | solution.py:196
  657.5 3.2 copy.74
  660.7 9.4 %all-to-all-start.1 = ((bf16[32,2,32,512]{3,2,1,0:T(8,128)(2,1)}), bf16[32,2,32,512]{3,2,1,0:T(8,128)(2,1)}, u32[]{:S(2)}, u32[]{:S(2)}) async-start(bf16[32,2,32,512]{3,2,1,0:T(8,128)(2,1)} %copy.74), calls=%async_computation.2 | async-start | bytes 4194304 | tf_op jit(solution)/shard_map/all_to_all | solution.py:199
  670.3 1.6 fusion.43
  671.9 4.9 fusion.27
  676.9 2.4 convolution_multiply_fusion
  679.3 19.7 %all-to-all-done.1 = bf16[32,2,32,512]{3,2,1,0:T(8,128)(2,1)} async-done(((bf16[32,2,32,512]{3,2,1,0:T(8,128)(2,1)}), bf16[32,2,32,512]{3,2,1,0:T(8,128)(2,1)}, u32[]{:S(2)}, u32[]{:S(2)}) %all-to-all-start.1) | async-done | bytes 2097184 | tf_op jit(solution)/shard_map/all_to_all | solution.py:199
  698.9 4.1 bitcast_convert_fusion
  703.0 7.5 %gather_fusion.1 = f32[1024,512]{1,0:T(8,128)} fusion(f32[2048,512]{1,0:T(8,128)} %bitcast_convert_fusion, s32[1024]{0:T(1024)S(1)} %broadcast_clamp_fusion), kind=kCustom, calls=%fused_computation.1 | custom fusion | bytes 4198400 | tf_op jit(solution)/shard_map/gather | solution.py:202
  710.5 2.9 reshape.241
  713.4 3.1 multiply_reduce_fusion
  716.7 1.1 convert_element_type.96
  717.8 0.8 copy.75
  718.7 1.7 dynamic-slice_convert_fusion
  720.3 16.5 %reduce-scatter.5.cloned.1.call-done = bf16[64,2048]{1,0:T(8,128)(2,1)} async-done(((bf16[256,2048]{1,0:T(8,128)(2,1)}), bf16[64,2048]{1,0:T(8,128)(2,1)}) %reduce-scatter.5.cloned.1.call-update) | async-done | bytes 262160 | tf_op jit(solution)/shard_map/reduce_scatter | solution.py:210
  736.8 1.9 add_convert_fusion
  (80 shorter events, 10.5 us)
Async XLA Ops:
  7.2 669.7 %copy-start = (bf16[768,2048]{1,0:T(8,128)(2,1)S(1)}, bf16[768,2048]{1,0:T(8,128)(2,1)}, u32[]{:S(2)}) copy-start(bf16[768,2048]{1,0:T(8,128)(2,1)} %param.24) | copy-start | bytes 9437188
  7.2 141.4 %all-gather.4.cloned.1.call-start = ((), (), s32[]{:S(2)}) async-start(), calls=%async_computation.4 | async-start | bytes 8650752 | tf_op jit(solution)/shard_map/all_gather | solution.py:140
  13.3 8.8 %copy-start.9 = (s32[256,4]{0,1:T(4,128)S(1)}, s32[256,4]{0,1:T(4,128)}, u32[]{:S(2)}) copy-start(s32[256,4]{0,1:T(4,128)} %param.28) | copy-start | bytes 12292
  15.2 264.9 %all-gather.6.cloned.1.call-start = ((), (), s32[]{:S(2)}) async-start(), calls=%async_computation.5 | async-start | bytes 8650752 | tf_op jit(solution)/shard_map/all_gather | solution.py:141
  17.1 400.9 %all-reduce.2.cloned.1.call-start = ((), (), s32[]{:S(2)}) async-start(), calls=%async_computation.6 | async-start | bytes 2097152 | tf_op jit(solution)/shard_map/psum | solution.py:166
  284.2 2.2 copy-start.1
  284.2 2.2 copy-start.6
  287.3 0.8 copy-start.7
  291.2 5.1 copy-start.8
  294.6 266.0 %all-gather.8.cloned.1.call-start = ((), (), s32[]{:S(2)}) async-start(), calls=%async_computation.7 | async-start | bytes 10485760 | tf_op jit(solution)/shard_map/all_gather | solution.py:189
  418.0 3.4 copy-start.2
  418.0 3.4 copy-start.3
  480.9 176.6 %reduce-scatter.3.cloned.1.call-start = ((), (), s32[]{:S(2)}) async-start(), calls=%async_computation.8 | async-start | bytes 10485760 | tf_op jit(solution)/shard_map/reduce_scatter | solution.py:196
  560.7 10.2 %copy-start.12 = (bf16[2,352,2048]{2,1,0:T(8,128)(2,1)S(1)}, bf16[2,352,2048]{2,1,0:T(8,128)(2,1)}, u32[]{:S(2)}) copy-start(bf16[2,352,2048]{2,1,0:T(8,128)(2,1)} %param.27) | copy-start | bytes 8650756
  660.7 9.4 %copy-start.10 = (f32[256,4]{0,1:T(4,128)S(1)}, f32[256,4]{0,1:T(4,128)}, u32[]{:S(2)}) copy-start(f32[256,4]{0,1:T(4,128)} %param.29) | copy-start | bytes 12292
  660.7 9.6 %copy-start.11 = (bf16[2048]{0:T(1024)(128)(2,1)S(1)}, bf16[2048]{0:T(1024)(128)(2,1)}, u32[]{:S(2)}) copy-start(bf16[2048]{0:T(1024)(128)(2,1)} %param.25) | copy-start | bytes 12292
  660.7 38.2 %all-to-all-start.1 = ((bf16[32,2,32,512]{3,2,1,0:T(8,128)(2,1)}), bf16[32,2,32,512]{3,2,1,0:T(8,128)(2,1)}, u32[]{:S(2)}, u32[]{:S(2)}) async-start(bf16[32,2,32,512]{3,2,1,0:T(8,128)(2,1)} %copy.74), calls=%async_computation.2 | async-start | bytes 4194304 | tf_op jit(solution)/shard_map/all_to_all | solution.py:199
  670.1 66.7 %reduce-scatter.5.cloned.1.call-start = ((), (), s32[]{:S(2)}) async-start(), calls=%async_computation.9 | async-start | bytes 1310720 | tf_op jit(solution)/shard_map/reduce_scatter | solution.py:210
  713.4 3.1 copy-start.4
  716.6 1.2 copy-start.5
Sparse Core Ops, SparseCore 0:
  15.3 133.2 all-gather.3
  152.0 128.1 all-gather.5
  294.7 123.1 all-reduce.1
  481.0 79.5 all-gather.7
  577.7 79.7 reduce-scatter.2
  717.9 18.8 reduce-scatter.4

commit v2 on v1

--- a/solution.py
+++ b/solution.py
@@ -3,9 +3,12 @@
 import jax
 import jax.numpy as jnp
 from jax import lax
-from jax.sharding import PartitionSpec as P
+from jax.sharding import Mesh, PartitionSpec as P
+from jax.experimental import pallas as pl
+from jax.experimental.pallas import tpu as pltpu
 
 HD = 128
+HEADS = 16
 TOPK = 4
 SLOTS = 64
 CAP = 32
@@ -14,6 +17,112 @@
 rope_base = 1000000.0
 neg_fill = -1e30
 norm_eps = 1e-06
+
+
+KEY_TILE = 512
+
+
+def flash_kernel(bounds_ref, q_ref, k_ref, v_ref, qseg_ref, kseg_ref, o_ref, m_sc, l_sc, acc_sc):
+    step = pl.program_id(0)
+    first_chunk = bounds_ref[0]
+    end_chunk = bounds_ref[1]
+    query_first = bounds_ref[2]
+    chunk = first_chunk + step
+    rows = q_ref.shape[0]
+    heads = q_ref.shape[1] // HD
+
+    @pl.when(step == 0)
+    def _():
+        m_sc[...] = jnp.full(m_sc.shape, neg_fill, jnp.float32)
+        l_sc[...] = jnp.zeros(l_sc.shape, jnp.float32)
+        acc_sc[...] = jnp.zeros(acc_sc.shape, jnp.float32)
+
+    @pl.when(chunk < end_chunk)
+    def _():
+        key_pos = chunk * KEY_TILE + lax.broadcasted_iota(jnp.int32, (1, KEY_TILE), 1)
+        query_pos = query_first + lax.broadcasted_iota(jnp.int32, (rows, 1), 0)
+        visible = (key_pos <= query_pos) & (kseg_ref[...] == qseg_ref[...])
+        score_scale = 1.0 / math.sqrt(HD)
+        for h in range(heads):
+            cols = slice(h * HD, (h + 1) * HD)
+            scores = (
+                lax.dot_general(
+                    q_ref[:, cols], k_ref[:, cols], (((1,), (1,)), ((), ())),
+                    preferred_element_type=jnp.float32,
+                )
+                * score_scale
+            )
+            m_old = m_sc[h]
+            m_new = jnp.maximum(
+                m_old, jnp.max(jnp.where(visible, scores, neg_fill), axis=1, keepdims=True)
+            )
+            weights_f = jnp.where(visible, jnp.exp(scores - m_new), 0.0)
+            rescale = jnp.exp(m_old - m_new)
+            l_sc[h] = l_sc[h] * rescale + jnp.sum(weights_f, axis=1, keepdims=True)
+            acc_sc[h] = acc_sc[h] * rescale + jnp.dot(
+                weights_f.astype(jnp.bfloat16), v_ref[:, cols], preferred_element_type=jnp.float32
+            )
+            m_sc[h] = m_new
+
+    @pl.when(step == pl.num_programs(0) - 1)
+    def _():
+        for h in range(heads):
+            o_ref[:, h * HD:(h + 1) * HD] = (acc_sc[h] / l_sc[h]).astype(o_ref.dtype)
+
+
+def flash_attention(rotated_q, key_all, value_all, query_seg, segment_ids, query_first, seg_first):
+    rows, width = rotated_q.shape
+    heads = width // HD
+    key_count = key_all.shape[0]
+    chunks = key_count // KEY_TILE
+    first_chunk = seg_first // KEY_TILE
+    end_chunk = (query_first + rows + KEY_TILE - 1) // KEY_TILE
+    bounds = jnp.stack([first_chunk, end_chunk, query_first]).astype(jnp.int32)
+
+    def kv_map(c, b):
+        return (jnp.minimum(b[0] + c, b[1] - 1), 0)
+
+    def kseg_map(c, b):
+        return (0, jnp.minimum(b[0] + c, b[1] - 1))
+
+    grid_spec = pltpu.PrefetchScalarGridSpec(
+        num_scalar_prefetch=1,
+        grid=(chunks,),
+        in_specs=[
+            pl.BlockSpec((rows, width), lambda c, b: (0, 0)),
+            pl.BlockSpec((KEY_TILE, width), kv_map),
+            pl.BlockSpec((KEY_TILE, width), kv_map),
+            pl.BlockSpec((rows, 1), lambda c, b: (0, 0)),
+            pl.BlockSpec((1, KEY_TILE), kseg_map),
+        ],
+        out_specs=pl.BlockSpec((rows, width), lambda c, b: (0, 0)),
+        scratch_shapes=[
+            pltpu.VMEM((heads, rows, 1), jnp.float32),
+            pltpu.VMEM((heads, rows, 1), jnp.float32),
+            pltpu.VMEM((heads, rows, HD), jnp.float32),
+        ],
+    )
+    flops = 4 * rows * key_count * width
+    return pl.pallas_call(
+        flash_kernel,
+        grid_spec=grid_spec,
+        out_shape=jax.ShapeDtypeStruct((rows, width), jnp.bfloat16),
+        compiler_params=pltpu.CompilerParams(
+            dimension_semantics=("arbitrary",), vmem_limit_bytes=48 * 1024 * 1024
+        ),
+        cost_estimate=pl.CostEstimate(
+            flops=flops,
+            transcendentals=rows * key_count * heads,
+            bytes_accessed=2 * key_count * width * 2 + 2 * rows * width * 2,
+        ),
+    )(
+        bounds,
+        rotated_q,
+        key_all,
+        value_all,
+        query_seg.reshape(rows, 1).astype(jnp.int32),
+        segment_ids.reshape(1, key_count).astype(jnp.int32),
+    )
 
 
 def token_positions(segment_ids):
@@ -78,87 +187,35 @@
     expert_ids,
     gate_weights,
 ):
-    seq_count = lax.axis_size("seq")
+    seq_count = lax.axis_size("sh") * lax.axis_size("sl")
     exp_count = lax.axis_size("exp")
-    seq_place = lax.axis_index("seq")
+    group_place = lax.axis_index("sh")
+    sub_count = lax.axis_size("sl")
+    seq_place = group_place * sub_count + lax.axis_index("sl")
     exp_place = lax.axis_index("exp")
     block_len = queries.shape[0]
-    stream_len = segment_ids.shape[0]
     local_heads = queries.shape[1] // HD
     block_first = seq_place * block_len
     query_seg = lax.dynamic_slice_in_dim(segment_ids, block_first, block_len, 0)
     local_start = jnp.sum((segment_ids[None, :] < query_seg[:, None]).astype(jnp.int32), axis=1)
     local_pos = block_first + jnp.arange(block_len, dtype=jnp.int32) - local_start
-    rotated_q = rotate(queries, local_pos, local_heads).reshape(block_len, local_heads, HD)
+    rotated_q = rotate(queries, local_pos, local_heads)
     key_cache = rotate(keys, local_pos, local_heads)
-    score_scale = 1.0 / math.sqrt(HD)
-    query_pos = block_first + jnp.arange(block_len, dtype=jnp.int32)
-
-    def attend(state_now, key_rows, value_rows, key_first):
-        width_keys = key_rows.shape[0]
-        run_max, run_sum, run_acc = state_now
-        scores = (
-            jnp.einsum(
-                "qhd,khd->hqk",
-                rotated_q,
-                key_rows.reshape(width_keys, local_heads, HD),
-                preferred_element_type=jnp.float32,
-            )
-            * score_scale
-        )
-        key_pos = key_first + jnp.arange(width_keys, dtype=jnp.int32)
-        key_seg = lax.dynamic_slice_in_dim(
-            segment_ids, jnp.clip(key_first, 0, stream_len - width_keys), width_keys, 0
-        )
-        visible = (
-            True
-            & (key_pos[None, :] <= query_pos[:, None])
-            & (key_seg[None, :] == query_seg[:, None])
-        )
-        new_max = jnp.maximum(run_max, jnp.max(jnp.where(visible[None], scores, neg_fill), axis=-1))
-        weights_f = jnp.where(visible[None], jnp.exp(scores - new_max[..., None]), 0.0)
-        rescale = jnp.exp(run_max - new_max)
-        weights_b = weights_f.astype(jnp.bfloat16)
-        gathered = jnp.einsum(
-            "hqk,khd->hqd",
-            weights_b,
-            value_rows.reshape(width_keys, local_heads, HD),
-            preferred_element_type=jnp.float32,
-        )
-        return (
-            new_max,
-            run_sum * rescale + jnp.sum(weights_f, axis=-1),
-            run_acc * rescale[..., None] + gathered,
-        )
-
-    init_state = (
-        jnp.full((local_heads, block_len), neg_fill, jnp.float32),
-        jnp.zeros((local_heads, block_len), jnp.float32),
-        jnp.zeros((local_heads, block_len, HD), jnp.float32),
-    )
-    pieces = (
-        lax.all_gather(key_cache, "seq", axis=0, tiled=True),
-        lax.all_gather(values, "seq", axis=0, tiled=True),
-    )
-    piece_len = pieces[0].shape[0]
-    step_len = math.gcd(piece_len, 512)
-
-    def inner_step(step_id, state_in):
-        row_start = step_id * step_len
-        key_rows = lax.dynamic_slice_in_dim(pieces[0], row_start, step_len, 0)
-        value_rows = lax.dynamic_slice_in_dim(pieces[1], row_start, step_len, 0)
-        return attend(state_in, key_rows, value_rows, row_start)
-
-    first_chunk = local_start[0] // step_len
-    end_chunk = (block_first + block_len + step_len - 1) // step_len
-    final_state = lax.fori_loop(first_chunk, end_chunk, inner_step, init_state)
-    run_max, run_sum, run_acc = final_state
-    attended = (
-        (run_acc / run_sum[..., None])
-        .transpose(1, 0, 2)
-        .reshape(block_len, local_heads * HD)
-        .astype(jnp.bfloat16)
-    )
+    stacked = jnp.stack([rotated_q, key_cache, values]).reshape(3, block_len, local_heads, HD)
+    moved = lax.all_to_all(stacked, "sl", split_axis=2, concat_axis=1, tiled=True)
+    span = block_len * sub_count
+    head_q = moved[0].reshape(span, HD)
+    head_kv = moved[1:].reshape(2, span, HD)
+    gathered = lax.all_gather(head_kv, "sh", axis=1, tiled=True)
+    span_first = group_place * span
+    span_seg = lax.dynamic_slice_in_dim(segment_ids, span_first, span, 0)
+    seg_first = jnp.sum((segment_ids < span_seg[0]).astype(jnp.int32))
+    head_out = flash_attention(
+        head_q, gathered[0], gathered[1], span_seg, segment_ids, span_first, seg_first
+    )
+    attended = lax.all_to_all(
+        head_out.reshape(sub_count, block_len, 1, HD), "sl", split_axis=0, concat_axis=2, tiled=True
+    ).reshape(block_len, local_heads * HD)
     attn_part = jnp.dot(attended, out_weight, preferred_element_type=jnp.float32)
     row_count = block_len // exp_count
     row_first = exp_place * row_count
@@ -187,7 +244,7 @@
     col_first = exp_place * col_count
     outgoing_part = lax.dynamic_slice_in_dim(outgoing, col_first, col_count, 3)
     incoming = lax.all_gather(
-        lax.all_to_all(outgoing_part, "seq", split_axis=0, concat_axis=0, tiled=True),
+        lax.all_to_all(outgoing_part, SEQ, split_axis=0, concat_axis=0, tiled=True),
         "exp",
         axis=3,
         tiled=True,
@@ -197,7 +254,7 @@
         expert_part.astype(jnp.float32).astype(jnp.bfloat16), "exp", scatter_dimension=3, tiled=True
     ).astype(jnp.float32)
     returned = lax.all_to_all(
-        summed.astype(jnp.bfloat16), "seq", split_axis=0, concat_axis=0, tiled=True
+        summed.astype(jnp.bfloat16), SEQ, split_axis=0, concat_axis=0, tiled=True
     ).astype(summed.dtype)
     picked = returned.reshape(SLOTS * CAP, col_count)[slot_place].reshape(
         block_len, TOPK, col_count
@@ -214,26 +271,34 @@
     return (mixed_out, attn_rows, key_cache)
 
 
+SEQ = ("sh", "sl")
+
+
 def solution(mesh):
+    exp_count = mesh.shape["exp"]
+    seq_count = mesh.shape["seq"]
+    sub_count = HEADS // exp_count
+    grid = mesh.devices.reshape(seq_count // sub_count, sub_count, exp_count)
+    split_mesh = Mesh(grid, ("sh", "sl", "exp"))
     return jax.shard_map(
         body,
-        mesh=mesh,
+        mesh=split_mesh,
         in_specs=(
             P(),
-            P("seq", "exp"),
-            P("seq", "exp"),
-            P("seq", "exp"),
+            P(SEQ, "exp"),
+            P(SEQ, "exp"),
+            P(SEQ, "exp"),
             P("exp", None),
-            P("seq", None),
+            P(SEQ, None),
             P(),
             P(None, None, "exp"),
             P("exp", None),
             P(),
-            P("seq", None, None, "exp"),
-            P("seq", "exp", None),
-            P("seq", None),
-            P("seq", None),
+            P(SEQ, None, None, "exp"),
+            P(SEQ, "exp", None),
+            P(SEQ, None),
+            P(SEQ, None),
         ),
-        out_specs=(P(("seq", "exp"), None), P(("seq", "exp"), None), P("seq", "exp")),
+        out_specs=(P(("sh", "sl", "exp"), None), P(("sh", "sl", "exp"), None), P(SEQ, "exp")),
         check_vma=False,
     )

time: 750 us -> 526 us (0.70)
  waiting for transfers between devices: 529 us -> 285 us
  blocking collectives: 36.8 us -> 53.3 us
    all_gather x3 -> x2, waiting for transfers between devices: 296 us -> 110 us  [the longest x1 79.5 us: body(): lax.all_gather(lax.all_to_all(outgoing_part, SEQ, split_axis=0, concat_ax...]
    psum x1, waiting for transfers between devices: 117 us -> 54.9 us  [body(): lax.psum(attn_part.astype(jnp.bfloat16), 'exp').astype(jnp.float32)]
    all_to_all x1 -> x2, blocking collectives: 36.8 us -> 53.3 us  [the longest x1 36.8 us: body(): lax.all_to_all(outgoing_part, SEQ, split_axis=0, concat_axis=0, tiled=True)]
    all_to_all x1 -> x2, waiting for transfers between devices: 19.7 us -> 25.2 us  [the longest x1 19.7 us: body(): lax.all_to_all(summed.astype(jnp.bfloat16), SEQ, split_axis=0, concat_axi...]
    another operation x4 -> x5, other arithmetic: 37.1 us -> 33 us
  transfers between devices with their start and end apart: 7 -> 7, of which waited for: 7 -> 7; matrix products, arithmetic and copies ran while one was open for 8% -> 11% of each run, Pallas kernels for 0% -> 0%
where the time goes in v2:
time: 526 us; the launch traced here: 524 us
  waiting for transfers between devices  285 us (54%)
  local copies, waits for them, and re-layouts  61.4 us (12%)
  other arithmetic  59.4 us (11%)
  blocking collectives  53.3 us (10%)
  matrix products  29.2 us (6%)
  between operations  16.8 us (3%)
  starting transfers between devices  13.7 us (3%)
    reduce_scatter x1, waiting for transfers between devices, body(): lax.psum_scatter(expert_part.astype(jnp.float32).astype(jnp.bfloat16), 'e...  80 us
    all_gather x1, waiting for transfers between devices, body(): lax.all_gather(lax.all_to_all(outgoing_part, SEQ, split_axis=0, concat_ax...  79.5 us
    psum x1, waiting for transfers between devices, body(): lax.psum(attn_part.astype(jnp.bfloat16), 'exp').astype(jnp.float32)  54.9 us
    all_to_all x1, blocking collectives, body(): lax.all_to_all(outgoing_part, SEQ, split_axis=0, concat_axis=0, tiled=True)  36.8 us
    another operation x3, other arithmetic  32 us
    all_gather x1, waiting for transfers between devices, body(): gathered = lax.all_gather(head_kv, 'sh', axis=1, tiled=True)  30.6 us
    all_to_all x1, waiting for transfers between devices, body(): lax.all_to_all(summed.astype(jnp.bfloat16), SEQ, split_axis=0, concat_axi...  19.7 us
    gather x1, local copies, waits for them, and re-layouts, body(): normed[jnp.maximum(source_row, 0)]  17.7 us
  transfers between devices with their start and end apart: 7, of which 7 were waited for; matrix products, arithmetic and copies ran while one was open for 11% of the time, Pallas kernels for 0%

profile of v2, /device:TPU:1, one launch (start us, length us, event | category | flops | bytes accessed | tf_op | source)
XLA Modules:
  0.0 523.9 jit_solution(11698251836619388195)
XLA Ops:
  7.3 0.9 dynamic_slice.16
  8.2 1.7 convert_reduce_fusion
  9.9 1.1 copy.74
  11.8 1.1 copy.75
  13.8 1.1 copy.76
  15.2 1.3 fusion.22
  17.2 0.9 pad_maximum_fusion
  18.2 2.3 copy.77
  20.5 16.6 %all_to_all.40 = bf16[3,256,4,128]{3,1,0,2:T(8,128)(2,1)S(1)} all-to-all(bf16[3,256,4,128]{3,1,0,2:T(8,128)(2,1)} %copy.77), channel_id=1, replica_groups=mesh['sh'=8,'sl'=4,'exp'=4] {'sl'}, dimensions={2} | all-to-all | bytes 1572864 | tf_op jit(solution)/shard_map/all_to_all | solution.py:205
  39.4 1.3 convert_reduce_fusion.1
  43.2 1.0 copy.79.qseg_ref
  45.8 31.1 %reduce-window.6 = s32[64,8,128]{2,1,0:T(8,128)S(1)} reduce-window(s32[64,8,128]{2,1,0:T(8,128)} %fusion.21, s32[]{:T(128)} %constant.81.clone.1), window={size=1x1x128 pad=0_0x0_0x127_0}, to_apply=%region_4.5 | reduce-window | flops 8323072 | bytes 524292 | tf_op jit(solution)/shard_map/reduce-window
  77.8 1.1 copy.85
  79.9 1.0 slice.70
  80.9 30.6 %all-gather.3.cloned.1.call-done = bf16[2,8192,128]{2,1,0:T(8,128)(2,1)} async-done(((bf16[2,1024,128]{2,1,0:T(8,128)(2,1)}), bf16[2,8192,128]{2,1,0:T(8,128)(2,1)}) %all-gather.3.cloned.1.call-update) | async-done | bytes 4194320 | tf_op jit(solution)/shard_map/all_gather | solution.py:209
  111.4 2.6 slice_bitcast_fusion.2
  114.0 5.2 shard_map.157
  120.0 1.8 copy.80
  121.7 3.9 all-to-all-start.1
  125.7 5.5 %all-to-all-done.1 = bf16[4,256,1,128]{1,3,2,0:T(8,128)(2,1)S(1)} async-done(((bf16[4,256,1,128]{1,3,2,0:T(8,128)(2,1)}), bf16[4,256,1,128]{1,3,2,0:T(8,128)(2,1)S(1)}, u32[]{:S(2)}, u32[]{:S(2)}) %all-to-all-start.1) | async-done | bytes 262176 | tf_op jit(solution)/shard_map/all_to_all | solution.py:216
  131.9 3.4 convolution_convert_fusion
  137.2 4.5 scatter_custom_fusion
  141.8 54.9 %all-reduce.2.cloned.1.call-done = bf16[256,2048]{1,0:T(8,128)(2,1)} async-done(((bf16[256,2048]{1,0:T(8,128)(2,1)}), bf16[256,2048]{1,0:T(8,128)(2,1)}) %all-reduce.2.cloned.1.call-update) | async-done | bytes 1048592 | tf_op jit(solution)/shard_map/psum | solution.py:223
  196.7 3.4 convert_add_fusion
  200.2 1.5 multiply_convert_fusion
  201.6 17.7 %gather_fusion = bf16[2048,2048]{1,0:T(8,128)(2,1)} fusion(bf16[256,2048]{1,0:T(8,128)(2,1)} %multiply_convert_fusion, s32[2048]{0:T(1024)S(1)} %maximum_clamp_fusion), kind=kCustom, calls=%fused_computation | custom fusion | bytes 16785408 | tf_op jit(solution)/shard_map/gather | solution.py:241
  219.4 1.9 dynamic-slice_select_fusion
  221.3 36.8 %all_to_all.41 = bf16[32,2,32,512]{3,2,1,0:T(8,128)(2,1)S(1)} all-to-all(bf16[32,2,32,512]{3,2,1,0:T(8,128)(2,1)S(1)} %dynamic-slice_select_fusion), channel_id=1, replica_groups=mesh['sh'=8,'sl'=4,'exp'=4] {'sh','sl'}, dimensions={0} | all-to-all | bytes 4194304 | tf_op jit(solution)/shard_map/all_to_all | solution.py:247
  258.1 1.6 copy.87
  259.9 79.5 %all-gather.5.cloned.1.call-done = bf16[32,2,32,2048]{3,2,0,1:T(8,128)(2,1)} async-done(((bf16[32,2,32,512]{3,2,0,1:T(8,128)(2,1)}), bf16[32,2,32,2048]{3,2,0,1:T(8,128)(2,1)}) %all-gather.5.cloned.1.call-update) | async-done | bytes 8388624 | tf_op jit(solution)/shard_map/all_gather | solution.py:246
  339.4 10.1 %fusion.6 = f32[32,2,32,2,352]{4,2,3,0,1:T(8,128)S(1)} fusion(bf16[2,2,2048,352]{2,3,1,0:T(8,128)(2,1)} %param.24, bf16[32,2,32,2048]{3,2,0,1:T(8,128)(2,1)} %all-gather.5.cloned.1.call-done), kind=kOutput, calls=%fused_computation.14 | convolution fusion | flops 5905580032 | bytes 19922944 | tf_op jit(solution)/shard_map/nscd,sgde->nscge/dot_general | solution.py:163
  349.6 6.7 %convert_bitcast_fusion = bf16[32,2,32,2048]{3,2,0,1:T(8,128)(2,1)} fusion(bf16[2,352,2048]{2,1,0:T(8,128)(2,1)S(1)} %copy-done.19, f32[32,2,32,2,352]{4,2,3,0,1:T(8,128)S(1)} %fusion.6), kind=kOutput, calls=%fused_computation.5 | convolution fusion | flops 2961309696 | bytes 17039360 | tf_op jit(solution)/shard_map/nsce,sed->nscd/dot_general | solution.py:169
  356.3 80.0 %reduce-scatter.3.cloned.1.call-done = bf16[32,2,32,512]{3,2,0,1:T(8,128)(2,1)} async-done(((bf16[32,2,32,2048]{3,2,0,1:T(8,128)(2,1)}), bf16[32,2,32,512]{3,2,0,1:T(8,128)(2,1)}) %reduce-scatter.3.cloned.1.call-update) | async-done | bytes 2097168 | tf_op jit(solution)/shard_map/reduce_scatter | solution.py:253
  436.3 3.2 copy.89
  439.4 9.4 %all-to-all-start.3 = ((bf16[32,2,32,512]{3,2,1,0:T(8,128)(2,1)}), bf16[32,2,32,512]{3,2,1,0:T(8,128)(2,1)}, u32[]{:S(2)}, u32[]{:S(2)}) async-start(bf16[32,2,32,512]{3,2,1,0:T(8,128)(2,1)} %copy.89), calls=%async_computation.4 | async-start | bytes 4194304 | tf_op jit(solution)/shard_map/all_to_all | solution.py:256
  449.1 1.6 fusion.31
  450.7 4.9 fusion.13
  455.6 2.4 convolution_multiply_fusion
  458.0 19.7 %all-to-all-done.3 = bf16[32,2,32,512]{3,2,1,0:T(8,128)(2,1)} async-done(((bf16[32,2,32,512]{3,2,1,0:T(8,128)(2,1)}), bf16[32,2,32,512]{3,2,1,0:T(8,128)(2,1)}, u32[]{:S(2)}, u32[]{:S(2)}) %all-to-all-start.3) | async-done | bytes 2097184 | tf_op jit(solution)/shard_map/all_to_all | solution.py:256
  477.7 4.1 bitcast_convert_fusion
  481.8 7.5 %gather_fusion.1 = f32[1024,512]{1,0:T(8,128)} fusion(f32[2048,512]{1,0:T(8,128)} %bitcast_convert_fusion, s32[1024]{0:T(1024)S(1)} %broadcast_clamp_fusion), kind=kCustom, calls=%fused_computation.1 | custom fusion | bytes 4198400 | tf_op jit(solution)/shard_map/gather | solution.py:259
  489.3 2.9 reshape.248
  492.2 3.1 multiply_reduce_fusion
  495.4 1.1 convert_element_type.99
  497.3 1.8 copy.90
  499.1 1.7 dynamic-slice_convert_fusion
  500.8 14.7 %reduce-scatter.5.cloned.1.call-done = bf16[64,2048]{1,0:T(8,128)(2,1)} async-done(((bf16[256,2048]{1,0:T(8,128)(2,1)}), bf16[64,2048]{1,0:T(8,128)(2,1)}) %reduce-scatter.5.cloned.1.call-update) | async-done | bytes 262160 | tf_op jit(solution)/shard_map/reduce_scatter | solution.py:267
  515.5 1.9 add_convert_fusion
  (87 shorter events, 13.0 us)
Async XLA Ops:
  7.2 448.4 %copy-start = (bf16[768,2048]{1,0:T(8,128)(2,1)S(1)}, bf16[768,2048]{1,0:T(8,128)(2,1)}, u32[]{:S(2)}) copy-start(bf16[768,2048]{1,0:T(8,128)(2,1)} %param.22) | copy-start | bytes 9437188
  7.2 104.3 %all-gather.3.cloned.1.call-start = ((), (), s32[]{:S(2)}) async-start(), calls=%async_computation.6 | async-start | bytes 4718592 | tf_op jit(solution)/shard_map/all_gather | solution.py:209
  16.5 0.7 copy-start.10
  16.5 0.7 copy-start.12
  20.5 18.4 %copy-start.3 = (s32[8192]{0:T(1024)S(1)}, s32[8192]{0:T(1024)}, u32[]{:S(2)}) copy-start(s32[8192]{0:T(1024)} %param.14) | copy-start | bytes 98308
  20.5 23.8 %copy-start.16 = (s32[256,4]{0,1:T(4,128)S(1)}, s32[256,4]{0,1:T(4,128)}, u32[]{:S(2)}) copy-start(s32[256,4]{0,1:T(4,128)} %param.26) | copy-start | bytes 12292
  37.0 0.9 copy-start.7
  44.4 0.7 copy-start.8
  111.4 2.6 copy-start.1
  119.2 0.7 copy-start.2
  121.7 9.5 %all-to-all-start.1 = ((bf16[4,256,1,128]{1,3,2,0:T(8,128)(2,1)}), bf16[4,256,1,128]{1,3,2,0:T(8,128)(2,1)S(1)}, u32[]{:S(2)}, u32[]{:S(2)}) async-start(bf16[4,256,1,128]{1,3,2,0:T(8,128)(2,1)} %copy.80), calls=%async_computation.1 | async-start | bytes 524288 | tf_op jit(solution)/shard_map/all_to_all | solution.py:216
  125.7 71.0 %all-reduce.2.cloned.1.call-start = ((), (), s32[]{:S(2)}) async-start(), calls=%async_computation.7 | async-start | bytes 2097152 | tf_op jit(solution)/shard_map/psum | solution.py:223
  131.2 0.7 copy-start.15
  131.9 4.1 copy-start.9
  131.9 5.2 copy-start.14
  135.4 204.0 %all-gather.5.cloned.1.call-start = ((), (), s32[]{:S(2)}) async-start(), calls=%async_computation.8 | async-start | bytes 10485760 | tf_op jit(solution)/shard_map/all_gather | solution.py:246
  196.7 3.4 copy-start.4
  196.7 3.4 copy-start.5
  259.7 176.6 %reduce-scatter.3.cloned.1.call-start = ((), (), s32[]{:S(2)}) async-start(), calls=%async_computation.9 | async-start | bytes 10485760 | tf_op jit(solution)/shard_map/reduce_scatter | solution.py:253
  339.4 10.2 %copy-start.19 = (bf16[2,352,2048]{2,1,0:T(8,128)(2,1)S(1)}, bf16[2,352,2048]{2,1,0:T(8,128)(2,1)}, u32[]{:S(2)}) copy-start(bf16[2,352,2048]{2,1,0:T(8,128)(2,1)} %param.25) | copy-start | bytes 8650756
  439.4 9.4 %copy-start.17 = (f32[256,4]{0,1:T(4,128)S(1)}, f32[256,4]{0,1:T(4,128)}, u32[]{:S(2)}) copy-start(f32[256,4]{0,1:T(4,128)} %param.27) | copy-start | bytes 12292
  439.4 9.6 %copy-start.18 = (bf16[2048]{0:T(1024)(128)(2,1)S(1)}, bf16[2048]{0:T(1024)(128)(2,1)}, u32[]{:S(2)}) copy-start(bf16[2048]{0:T(1024)(128)(2,1)} %param.23) | copy-start | bytes 12292
  439.4 38.2 %all-to-all-start.3 = ((bf16[32,2,32,512]{3,2,1,0:T(8,128)(2,1)}), bf16[32,2,32,512]{3,2,1,0:T(8,128)(2,1)}, u32[]{:S(2)}, u32[]{:S(2)}) async-start(bf16[32,2,32,512]{3,2,1,0:T(8,128)(2,1)} %copy.89), calls=%async_computation.4 | async-start | bytes 4194304 | tf_op jit(solution)/shard_map/all_to_all | solution.py:256
  448.8 66.7 %reduce-scatter.5.cloned.1.call-start = ((), (), s32[]{:S(2)}) async-start(), calls=%async_computation.10 | async-start | bytes 1310720 | tf_op jit(solution)/shard_map/reduce_scatter | solution.py:267
  492.2 3.1 copy-start.6
  495.4 1.2 copy-start.11
  495.4 1.2 copy-start.13
Sparse Core Ops, SparseCore 0:
  38.9 72.4 all-gather.2
  135.5 61.1 all-reduce.1
  259.8 79.5 all-gather.4
  356.4 79.7 reduce-scatter.2
  496.7 18.7 reduce-scatter.4

commit v3 on v2

--- a/solution.py
+++ b/solution.py
@@ -188,11 +188,12 @@
     gate_weights,
 ):
     seq_count = lax.axis_size("sh") * lax.axis_size("sl")
-    exp_count = lax.axis_size("exp")
+    exp_count = lax.axis_size("zl") * lax.axis_size("co")
     group_place = lax.axis_index("sh")
     sub_count = lax.axis_size("sl")
     seq_place = group_place * sub_count + lax.axis_index("sl")
-    exp_place = lax.axis_index("exp")
+    exp_place = lax.axis_index("zl") * lax.axis_size("co") + lax.axis_index("co")
+    quarter_place = lax.axis_index("co") * lax.axis_size("zl") + lax.axis_index("zl")
     block_len = queries.shape[0]
     local_heads = queries.shape[1] // HD
     block_first = seq_place * block_len
@@ -220,7 +221,7 @@
     row_count = block_len // exp_count
     row_first = exp_place * row_count
     residual_f = residual.astype(jnp.float32)
-    attn_sum = lax.psum(attn_part.astype(jnp.bfloat16), "exp").astype(jnp.float32)
+    attn_sum = lax.psum(lax.psum(attn_part.astype(jnp.bfloat16), "co"), "zl").astype(jnp.float32)
     after_attn = residual_f + attn_sum
     normed = rms_norm(after_attn, norm_gain)
     attn_rows = lax.dynamic_slice_in_dim(attn_sum, row_first, row_count, 0).astype(jnp.bfloat16)
@@ -230,8 +231,9 @@
     shared_term = jnp.dot(shared_hidden, shared_out, preferred_element_type=jnp.float32)
     shared_factor = jax.nn.sigmoid(jnp.dot(normed, shared_gate, preferred_element_type=jnp.float32))
     flat_ids = expert_ids.reshape(-1)
-    one_hot = (flat_ids[:, None] == jnp.arange(SLOTS, dtype=jnp.int32)[None, :]).astype(jnp.int32)
-    slot_rank = jnp.sum(jnp.cumsum(one_hot, axis=0) * one_hot, axis=1) - 1
+    flat_index = jnp.arange(flat_ids.shape[0], dtype=jnp.int32)
+    earlier_same = (flat_ids[None, :] == flat_ids[:, None]) & (flat_index[None, :] < flat_index[:, None])
+    slot_rank = jnp.sum(earlier_same.astype(jnp.int32), axis=1)
     slot_place = flat_ids * CAP + slot_rank
     owner_row = jnp.arange(flat_ids.shape[0], dtype=jnp.int32) // TOPK
     source_row = jnp.full((SLOTS * CAP,), -1, jnp.int32).at[slot_place].set(owner_row)
@@ -241,17 +243,25 @@
         (source_row >= 0)[:, None], normed[jnp.maximum(source_row, 0)], jnp.zeros((), jnp.bfloat16)
     ).reshape(seq_count, slot_local, CAP, model_width)
     col_count = model_width // exp_count
-    col_first = exp_place * col_count
+    col_first = quarter_place * col_count
     outgoing_part = lax.dynamic_slice_in_dim(outgoing, col_first, col_count, 3)
     incoming = lax.all_gather(
-        lax.all_to_all(outgoing_part, SEQ, split_axis=0, concat_axis=0, tiled=True),
-        "exp",
+        lax.all_gather(
+            lax.all_to_all(outgoing_part, SEQ, split_axis=0, concat_axis=0, tiled=True),
+            "zl",
+            axis=3,
+            tiled=True,
+        ),
+        "co",
         axis=3,
         tiled=True,
     )
     expert_part = expert_parts(incoming, expert_in, expert_out)
     summed = lax.psum_scatter(
-        expert_part.astype(jnp.float32).astype(jnp.bfloat16), "exp", scatter_dimension=3, tiled=True
+        lax.psum_scatter(expert_part, "co", scatter_dimension=3, tiled=True),
+        "zl",
+        scatter_dimension=3,
+        tiled=True,
     ).astype(jnp.float32)
     returned = lax.all_to_all(
         summed.astype(jnp.bfloat16), SEQ, split_axis=0, concat_axis=0, tiled=True
@@ -265,40 +275,41 @@
     )
     combined = shared_factor[:, None] * shared_term + moe_term
     moe_rows = lax.psum_scatter(
-        combined.astype(jnp.bfloat16), "exp", scatter_dimension=0, tiled=True
+        combined.astype(jnp.bfloat16), EXP, scatter_dimension=0, tiled=True
     ).astype(jnp.float32)
     mixed_out = (after_rows + moe_rows).astype(jnp.bfloat16)
     return (mixed_out, attn_rows, key_cache)
 
 
 SEQ = ("sh", "sl")
+EXP = ("zl", "co")
 
 
 def solution(mesh):
     exp_count = mesh.shape["exp"]
     seq_count = mesh.shape["seq"]
     sub_count = HEADS // exp_count
-    grid = mesh.devices.reshape(seq_count // sub_count, sub_count, exp_count)
-    split_mesh = Mesh(grid, ("sh", "sl", "exp"))
+    grid = mesh.devices.reshape(seq_count // sub_count, sub_count, exp_count // 2, 2)
+    split_mesh = Mesh(grid, ("sh", "sl", "zl", "co"))
     return jax.shard_map(
         body,
         mesh=split_mesh,
         in_specs=(
             P(),
-            P(SEQ, "exp"),
-            P(SEQ, "exp"),
-            P(SEQ, "exp"),
-            P("exp", None),
+            P(SEQ, EXP),
+            P(SEQ, EXP),
+            P(SEQ, EXP),
+            P(EXP, None),
             P(SEQ, None),
             P(),
-            P(None, None, "exp"),
-            P("exp", None),
+            P(None, None, EXP),
+            P(EXP, None),
             P(),
-            P(SEQ, None, None, "exp"),
-            P(SEQ, "exp", None),
+            P(SEQ, None, None, EXP),
+            P(SEQ, EXP, None),
             P(SEQ, None),
             P(SEQ, None),
         ),
-        out_specs=(P(("sh", "sl", "exp"), None), P(("sh", "sl", "exp"), None), P(SEQ, "exp")),
+        out_specs=(P(("sh", "sl", "zl", "co"), None), P(("sh", "sl", "zl", "co"), None), P(SEQ, EXP)),
         check_vma=False,
     )

time: 526 us -> 563 us (1.070)
  waiting for transfers between devices: 285 us -> 355 us
  other arithmetic: 59.4 us -> 25.9 us
  blocking collectives: 53.3 us -> 62.1 us
    psum x1 -> x2, waiting for transfers between devices: 54.9 us -> 91 us  [the longest x1 46.5 us: body(): lax.psum(attn_part.astype(jnp.bfloat16), 'co')]
    all_gather x1, waiting for transfers between devices: 30.6 us -> 66.1 us  [body(): gathered = lax.all_gather(head_kv, 'sh', axis=1, tiled=True)]
    another operation x3 -> x0, other arithmetic: 32 us -> none
    all_gather x0 -> x1, waiting for transfers between devices: none -> 25.4 us  [body(): lax.all_gather(lax.all_gather(lax.all_to_all(outgoing_part, SEQ, split_ax...]
    all_gather x1, waiting for transfers between devices: 79.5 us -> 57.5 us  [body(): lax.all_gather(lax.all_to_all(outgoing_part, SEQ, split_axis=0, concat_ax...]
    all_to_all x0 -> x1, blocking collectives: none -> 9.33 us  [body(): lax.all_to_all(head_out.reshape(sub_count, block_len, 1, HD), 'sl', split...]
    reduce_scatter x2 -> x3, waiting for transfers between devices: 94.7 us -> 96.3 us  [the longest x1 60.3 us: body(): lax.psum_scatter(lax.psum_scatter(expert_part, 'co', scatter_dimension=3,...]
  transfers between devices with their start and end apart: 7 -> 9, of which waited for: 7 -> 9; matrix products, arithmetic and copies ran while one was open for 11% -> 4% of each run, Pallas kernels for 0% -> 0%
where the time goes in v3:
time: 563 us; the launch traced here: 562 us
  waiting for transfers between devices  355 us (63%)
  blocking collectives  62.1 us (11%)
  local copies, waits for them, and re-layouts  57.3 us (10%)
  matrix products  29.1 us (5%)
  other arithmetic  25.9 us (5%)
  between operations  16.8 us (3%)
  starting transfers between devices  9.87 us (2%)
    all_gather x1, waiting for transfers between devices, body(): gathered = lax.all_gather(head_kv, 'sh', axis=1, tiled=True)  66.1 us
    reduce_scatter x1, waiting for transfers between devices, body(): lax.psum_scatter(lax.psum_scatter(expert_part, 'co', scatter_dimension=3,...  60.3 us
    all_gather x1, waiting for transfers between devices, body(): lax.all_gather(lax.all_to_all(outgoing_part, SEQ, split_axis=0, concat_ax...  57.5 us
    psum x1, waiting for transfers between devices, body(): lax.psum(attn_part.astype(jnp.bfloat16), 'co')  46.5 us
    psum x1, waiting for transfers between devices, body(): lax.psum(lax.psum(attn_part.astype(jnp.bfloat16), 'co'), 'zl')  44.5 us
    all_to_all x1, blocking collectives, body(): lax.all_to_all(outgoing_part, SEQ, split_axis=0, concat_axis=0, tiled=True)  36.3 us
    all_gather x1, waiting for transfers between devices, body(): lax.all_gather(lax.all_gather(lax.all_to_all(outgoing_part, SEQ, split_ax...  25.4 us
    reduce_scatter x1, waiting for transfers between devices, body(): lax.psum_scatter(expert_part, 'co', scatter_dimension=3, tiled=True)  20.3 us
  transfers between devices with their start and end apart: 9, of which 9 were waited for; matrix products, arithmetic and copies ran while one was open for 4% of the time, Pallas kernels for 0%

profile of v3, /device:TPU:1, one launch (start us, length us, event | category | flops | bytes accessed | tf_op | source)
XLA Modules:
  0.0 561.6 jit_solution(2346702742244227206)
XLA Ops:
  7.3 0.9 dynamic_slice.16
  8.2 1.7 convert_reduce_fusion
  9.9 1.1 copy.65
  11.8 1.1 copy.66
  13.8 1.1 copy.67
  15.2 1.3 fusion.20
  17.2 1.0 pad_maximum_fusion
  18.2 2.3 copy.68
  20.5 16.6 %all_to_all.40 = bf16[3,256,4,128]{3,1,0,2:T(8,128)(2,1)S(1)} all-to-all(bf16[3,256,4,128]{3,1,0,2:T(8,128)(2,1)} %copy.68), channel_id=1, replica_groups=mesh['sh'=8,'sl'=4,'zl'=2,'co'=2] {'sl'}, dimensions={2} | all-to-all | bytes 1572864 | tf_op jit(solution)/shard_map/all_to_all | solution.py:206
  39.5 1.3 convert_reduce_fusion.2
  43.1 1.0 copy.70.qseg_ref
  44.3 1.0 slice.62
  45.2 66.1 %all-gather.4.cloned.1.call-done = bf16[2,8192,128]{2,1,0:T(8,128)(2,1)} async-done(((bf16[2,1024,128]{2,1,0:T(8,128)(2,1)}), bf16[2,8192,128]{2,1,0:T(8,128)(2,1)}) %all-gather.4.cloned.1.call-update) | async-done | bytes 4194320 | tf_op jit(solution)/shard_map/all_gather | solution.py:210
  111.4 2.6 slice_bitcast_fusion.2
  113.9 5.3 shard_map.157
  119.9 1.1 copy.71
  121.0 9.3 %all_to_all.41 = bf16[4,256,1,128]{1,3,2,0:T(8,128)(2,1)S(1)} all-to-all(bf16[4,256,1,128]{1,3,2,0:T(8,128)(2,1)S(1)} %copy.71), channel_id=1, replica_groups=mesh['sh'=8,'sl'=4,'zl'=2,'co'=2] {'sl'}, dimensions={0} | all-to-all | bytes 524288 | tf_op jit(solution)/shard_map/all_to_all | solution.py:217
  130.3 3.3 convolution_convert_fusion
  133.7 46.5 %all-reduce.3.cloned.1.call-done = bf16[256,2048]{1,0:T(8,128)(2,1)} async-done(((bf16[256,2048]{1,0:T(8,128)(2,1)}), bf16[256,2048]{1,0:T(8,128)(2,1)}) %all-reduce.3.cloned.1.call-update) | async-done | bytes 1048592 | tf_op jit(solution)/shard_map/psum | solution.py:224
  181.4 4.3 scatter_custom_fusion
  185.9 44.5 %all-reduce.5.cloned.1.call-done = bf16[256,2048]{1,0:T(8,128)(2,1)} async-done(((bf16[256,2048]{1,0:T(8,128)(2,1)}), bf16[256,2048]{1,0:T(8,128)(2,1)}) %all-reduce.5.cloned.1.call-update) | async-done | bytes 1048592 | tf_op jit(solution)/shard_map/psum | solution.py:224
  230.4 3.4 convert_add_fusion
  233.7 1.5 multiply_convert_fusion
  235.2 17.7 %gather_fusion = bf16[2048,2048]{1,0:T(8,128)(2,1)} fusion(bf16[256,2048]{1,0:T(8,128)(2,1)} %multiply_convert_fusion, s32[2048]{0:T(1024)S(1)} %maximum_clamp_fusion), kind=kCustom, calls=%fused_computation | custom fusion | bytes 16785408 | tf_op jit(solution)/shard_map/gather | solution.py:243
  253.0 1.9 dynamic-slice_select_fusion
  254.9 36.3 %all_to_all.42 = bf16[32,2,32,512]{3,2,1,0:T(8,128)(2,1)S(1)} all-to-all(bf16[32,2,32,512]{3,2,1,0:T(8,128)(2,1)S(1)} %dynamic-slice_select_fusion), channel_id=1, replica_groups=mesh['sh'=8,'sl'=4,'zl'=2,'co'=2] {'sh','sl'}, dimensions={0} | all-to-all | bytes 4194304 | tf_op jit(solution)/shard_map/all_to_all | solution.py:250
  291.2 1.6 copy.75
  292.8 57.5 %all-gather.6.cloned.1.call-done = bf16[32,2,32,1024]{3,2,0,1:T(8,128)(2,1)} async-done(((bf16[32,2,32,512]{3,2,0,1:T(8,128)(2,1)}), bf16[32,2,32,1024]{3,2,0,1:T(8,128)(2,1)}) %all-gather.6.cloned.1.call-update) | async-done | bytes 4194320 | tf_op jit(solution)/shard_map/all_gather | solution.py:249
  350.6 25.4 %all-gather.8.cloned.1.call-done = bf16[32,2,32,2048]{3,2,0,1:T(8,128)(2,1)} async-done(((bf16[32,2,32,1024]{3,2,0,1:T(8,128)(2,1)}), bf16[32,2,32,2048]{3,2,0,1:T(8,128)(2,1)}) %all-gather.8.cloned.1.call-update) | async-done | bytes 8388624 | tf_op jit(solution)/shard_map/all_gather | solution.py:248
  376.0 10.1 %fusion.7 = f32[32,2,32,2,352]{4,2,3,0,1:T(8,128)S(1)} fusion(bf16[2,2,2048,352]{2,3,1,0:T(8,128)(2,1)} %param.24, bf16[32,2,32,2048]{3,2,0,1:T(8,128)(2,1)} %all-gather.8.cloned.1.call-done), kind=kOutput, calls=%fused_computation.17 | convolution fusion | flops 5905580032 | bytes 19922944 | tf_op jit(solution)/shard_map/nscd,sgde->nscge/dot_general | solution.py:163
  386.1 6.7 %convert_bitcast_fusion = bf16[32,2,32,2048]{3,2,0,1:T(8,128)(2,1)} fusion(bf16[2,352,2048]{2,1,0:T(8,128)(2,1)S(1)} %copy-done.16, f32[32,2,32,2,352]{4,2,3,0,1:T(8,128)S(1)} %fusion.7), kind=kOutput, calls=%fused_computation.5 | convolution fusion | flops 2961309696 | bytes 17039360 | tf_op jit(solution)/shard_map/nsce,sed->nscd/dot_general | solution.py:169
  392.9 20.3 %reduce-scatter.4.cloned.1.call-done = bf16[32,2,32,1024]{3,2,0,1:T(8,128)(2,1)} async-done(((bf16[32,2,32,2048]{3,2,0,1:T(8,128)(2,1)}), bf16[32,2,32,1024]{3,2,0,1:T(8,128)(2,1)}) %reduce-scatter.4.cloned.1.call-update) | async-done | bytes 4194320 | tf_op jit(solution)/shard_map/reduce_scatter | solution.py:261
  413.3 60.3 %reduce-scatter.6.cloned.1.call-done = bf16[32,2,32,512]{3,2,0,1:T(8,128)(2,1)} async-done(((bf16[32,2,32,1024]{3,2,0,1:T(8,128)(2,1)}), bf16[32,2,32,512]{3,2,0,1:T(8,128)(2,1)}) %reduce-scatter.6.cloned.1.call-update) | async-done | bytes 2097168 | tf_op jit(solution)/shard_map/reduce_scatter | solution.py:260
  473.6 3.2 copy.77
  476.7 9.4 %all-to-all-start.3 = ((bf16[32,2,32,512]{3,2,1,0:T(8,128)(2,1)}), bf16[32,2,32,512]{3,2,1,0:T(8,128)(2,1)}, u32[]{:S(2)}, u32[]{:S(2)}) async-start(bf16[32,2,32,512]{3,2,1,0:T(8,128)(2,1)} %copy.77), calls=%async_computation.5 | async-start | bytes 4194304 | tf_op jit(solution)/shard_map/all_to_all | solution.py:266
  486.3 1.6 fusion.29
  488.0 4.9 fusion.14
  492.9 2.4 convolution_multiply_fusion
  495.3 18.8 %all-to-all-done.3 = bf16[32,2,32,512]{3,2,1,0:T(8,128)(2,1)} async-done(((bf16[32,2,32,512]{3,2,1,0:T(8,128)(2,1)}), bf16[32,2,32,512]{3,2,1,0:T(8,128)(2,1)}, u32[]{:S(2)}, u32[]{:S(2)}) %all-to-all-start.3) | async-done | bytes 2097184 | tf_op jit(solution)/shard_map/all_to_all | solution.py:266
  514.1 4.1 bitcast_convert_fusion
  518.2 7.5 %gather_fusion.1 = f32[1024,512]{1,0:T(8,128)} fusion(f32[2048,512]{1,0:T(8,128)} %bitcast_convert_fusion, s32[1024]{0:T(1024)S(1)} %broadcast_clamp_fusion), kind=kCustom, calls=%fused_computation.1 | custom fusion | bytes 4198400 | tf_op jit(solution)/shard_map/gather | solution.py:269
  525.7 2.9 reshape.227
  528.6 3.1 multiply_reduce_fusion
  531.8 1.1 convert_element_type.95
  533.7 1.8 copy.78
  535.5 1.7 dynamic-slice_convert_fusion
  537.2 15.7 %reduce-scatter.8.cloned.1.call-done = bf16[64,2048]{1,0:T(8,128)(2,1)} async-done(((bf16[256,2048]{1,0:T(8,128)(2,1)}), bf16[64,2048]{1,0:T(8,128)(2,1)}) %reduce-scatter.8.cloned.1.call-update) | async-done | bytes 262160 | tf_op jit(solution)/shard_map/reduce_scatter | solution.py:277
  552.9 1.9 add_convert_fusion
  (79 shorter events, 8.7 us)
Async XLA Ops:
  7.2 485.7 %copy-start = (bf16[768,2048]{1,0:T(8,128)(2,1)S(1)}, bf16[768,2048]{1,0:T(8,128)(2,1)}, u32[]{:S(2)}) copy-start(bf16[768,2048]{1,0:T(8,128)(2,1)} %param.22) | copy-start | bytes 9437188
  7.2 104.2 %all-gather.4.cloned.1.call-start = ((), (), s32[]{:S(2)}) async-start(), calls=%async_computation.7 | async-start | bytes 4718592 | tf_op jit(solution)/shard_map/all_gather | solution.py:210
  16.5 0.7 copy-start.8
  16.5 0.7 copy-start.10
  20.5 18.4 %copy-start.3 = (s32[8192]{0:T(1024)S(1)}, s32[8192]{0:T(1024)}, u32[]{:S(2)}) copy-start(s32[8192]{0:T(1024)} %param.14) | copy-start | bytes 98308
  37.1 0.9 copy-start.7
  38.9 141.4 %all-reduce.3.cloned.1.call-start = ((), (), s32[]{:S(2)}) async-start(), calls=%async_computation.8 | async-start | bytes 2097152 | tf_op jit(solution)/shard_map/psum | solution.py:224
  111.4 2.6 copy-start.1
  119.2 0.7 copy-start.2
  130.3 50.0 %copy-start.12 = (s32[256,4]{0,1:T(4,128)S(1)}, s32[256,4]{0,1:T(4,128)}, u32[]{:S(2)}) copy-start(s32[256,4]{0,1:T(4,128)} %param.26) | copy-start | bytes 12292
  130.3 50.2 %copy-start.13 = (bf16[2048]{0:T(1024)(128)(2,1)S(1)}, bf16[2048]{0:T(1024)(128)(2,1)}, u32[]{:S(2)}) copy-start(bf16[2048]{0:T(1024)(128)(2,1)} %param.20) | copy-start | bytes 12292
  133.7 96.7 %all-reduce.5.cloned.1.call-start = ((), (), s32[]{:S(2)}) async-start(), calls=%async_computation.9 | async-start | bytes 2097152 | tf_op jit(solution)/shard_map/psum | solution.py:224
  180.3 170.0 %all-gather.6.cloned.1.call-start = ((), (), s32[]{:S(2)}) async-start(), calls=%async_computation.10 | async-start | bytes 6291456 | tf_op jit(solution)/shard_map/all_gather | solution.py:249
  230.3 3.4 copy-start.4
  230.4 3.4 copy-start.5
  292.8 83.2 %all-gather.8.cloned.1.call-start = ((), (), s32[]{:S(2)}) async-start(), calls=%async_computation.11 | async-start | bytes 12582912 | tf_op jit(solution)/shard_map/all_gather | solution.py:248
  350.3 62.9 %reduce-scatter.4.cloned.1.call-start = ((), (), s32[]{:S(2)}) async-start(), calls=%async_computation.12 | async-start | bytes 12582912 | tf_op jit(solution)/shard_map/reduce_scatter | solution.py:261
  376.0 10.2 %copy-start.16 = (bf16[2,352,2048]{2,1,0:T(8,128)(2,1)S(1)}, bf16[2,352,2048]{2,1,0:T(8,128)(2,1)}, u32[]{:S(2)}) copy-start(bf16[2,352,2048]{2,1,0:T(8,128)(2,1)} %param.25) | copy-start | bytes 8650756
  392.9 80.7 %reduce-scatter.6.cloned.1.call-start = ((), (), s32[]{:S(2)}) async-start(), calls=%async_computation.13 | async-start | bytes 6291456 | tf_op jit(solution)/shard_map/reduce_scatter | solution.py:260
  476.7 9.4 %copy-start.14 = (f32[256,4]{0,1:T(4,128)S(1)}, f32[256,4]{0,1:T(4,128)}, u32[]{:S(2)}) copy-start(f32[256,4]{0,1:T(4,128)} %param.27) | copy-start | bytes 12292
  476.7 9.6 %copy-start.15 = (bf16[2048]{0:T(1024)(128)(2,1)S(1)}, bf16[2048]{0:T(1024)(128)(2,1)}, u32[]{:S(2)}) copy-start(bf16[2048]{0:T(1024)(128)(2,1)} %param.23) | copy-start | bytes 12292
  476.7 37.4 %all-to-all-start.3 = ((bf16[32,2,32,512]{3,2,1,0:T(8,128)(2,1)}), bf16[32,2,32,512]{3,2,1,0:T(8,128)(2,1)}, u32[]{:S(2)}, u32[]{:S(2)}) async-start(bf16[32,2,32,512]{3,2,1,0:T(8,128)(2,1)} %copy.77), calls=%async_computation.5 | async-start | bytes 4194304 | tf_op jit(solution)/shard_map/all_to_all | solution.py:266
  486.1 66.8 %reduce-scatter.8.cloned.1.call-start = ((), (), s32[]{:S(2)}) async-start(), calls=%async_computation.14 | async-start | bytes 1310720 | tf_op jit(solution)/shard_map/reduce_scatter | solution.py:277
  528.6 3.1 copy-start.6
  531.8 1.2 copy-start.9
  531.8 1.2 copy-start.11
Sparse Core Ops, SparseCore 0:
  39.0 72.3 all-gather.3
  133.8 46.3 all-reduce.2
  182.7 47.5 all-reduce.4
  292.9 57.3 all-gather.5
  351.8 24.1 all-gather.7
  393.0 20.2 reduce-scatter.3
  415.7 57.8 reduce-scatter.5
  533.1 19.7 reduce-scatter.7

commit v4 on v3

--- a/solution.py
+++ b/solution.py
@@ -125,6 +125,27 @@
     )
 
 
+def shifted_copies(x, axis_name, count):
+    moved = [x]
+    for shift in range(1, count):
+        pairs = [(i, (i + shift) % count) for i in range(count)]
+        moved.append(lax.ppermute(x, axis_name, pairs))
+    return moved
+
+
+def sum_by_permutes(x, axis_name, count):
+    total = x.astype(jnp.float32)
+    for part in shifted_copies(x, axis_name, count)[1:]:
+        total = total + part.astype(jnp.float32)
+    return total
+
+
+def gather_by_permutes(x, axis_name, count, place):
+    moved = shifted_copies(x, axis_name, count)
+    reverse = jnp.stack([moved[0]] + moved[1:][::-1])
+    return jnp.roll(reverse, place, axis=0)
+
+
 def token_positions(segment_ids):
     stream_len = segment_ids.shape[0]
     token_index = jnp.arange(stream_len, dtype=jnp.int32)
@@ -193,7 +214,6 @@
     sub_count = lax.axis_size("sl")
     seq_place = group_place * sub_count + lax.axis_index("sl")
     exp_place = lax.axis_index("zl") * lax.axis_size("co") + lax.axis_index("co")
-    quarter_place = lax.axis_index("co") * lax.axis_size("zl") + lax.axis_index("zl")
     block_len = queries.shape[0]
     local_heads = queries.shape[1] // HD
     block_first = seq_place * block_len
@@ -207,7 +227,9 @@
     span = block_len * sub_count
     head_q = moved[0].reshape(span, HD)
     head_kv = moved[1:].reshape(2, span, HD)
-    gathered = lax.all_gather(head_kv, "sh", axis=1, tiled=True)
+    group_count = lax.axis_size("sh")
+    gathered = gather_by_permutes(head_kv, "sh", group_count, group_place)
+    gathered = jnp.moveaxis(gathered, 0, 1).reshape(2, group_count * span, HD)
     span_first = group_place * span
     span_seg = lax.dynamic_slice_in_dim(segment_ids, span_first, span, 0)
     seg_first = jnp.sum((segment_ids < span_seg[0]).astype(jnp.int32))
@@ -221,7 +243,7 @@
     row_count = block_len // exp_count
     row_first = exp_place * row_count
     residual_f = residual.astype(jnp.float32)
-    attn_sum = lax.psum(lax.psum(attn_part.astype(jnp.bfloat16), "co"), "zl").astype(jnp.float32)
+    attn_sum = sum_by_permutes(attn_part.astype(jnp.bfloat16), EXP, exp_count)
     after_attn = residual_f + attn_sum
     normed = rms_norm(after_attn, norm_gain)
     attn_rows = lax.dynamic_slice_in_dim(attn_sum, row_first, row_count, 0).astype(jnp.bfloat16)
@@ -243,26 +265,18 @@
         (source_row >= 0)[:, None], normed[jnp.maximum(source_row, 0)], jnp.zeros((), jnp.bfloat16)
     ).reshape(seq_count, slot_local, CAP, model_width)
     col_count = model_width // exp_count
-    col_first = quarter_place * col_count
+    col_first = exp_place * col_count
     outgoing_part = lax.dynamic_slice_in_dim(outgoing, col_first, col_count, 3)
     incoming = lax.all_gather(
-        lax.all_gather(
-            lax.all_to_all(outgoing_part, SEQ, split_axis=0, concat_axis=0, tiled=True),
-            "zl",
-            axis=3,
-            tiled=True,
-        ),
-        "co",
+        lax.all_to_all(outgoing_part, SEQ, split_axis=0, concat_axis=0, tiled=True),
+        EXP,
         axis=3,
         tiled=True,
     )
     expert_part = expert_parts(incoming, expert_in, expert_out)
-    summed = lax.psum_scatter(
-        lax.psum_scatter(expert_part, "co", scatter_dimension=3, tiled=True),
-        "zl",
-        scatter_dimension=3,
-        tiled=True,
-    ).astype(jnp.float32)
+    summed = lax.psum_scatter(expert_part, EXP, scatter_dimension=3, tiled=True).astype(
+        jnp.float32
+    )
     returned = lax.all_to_all(
         summed.astype(jnp.bfloat16), SEQ, split_axis=0, concat_axis=0, tiled=True
     ).astype(summed.dtype)

time: 563 us -> 527 us (0.936)
  waiting for transfers between devices: 355 us -> 276 us
  starting transfers between devices: 9.87 us -> 27.8 us
  blocking collectives: 62.1 us -> 76.5 us
  local copies, waits for them, and re-layouts: 57.3 us -> 64.6 us
    all_gather x2 -> x0, waiting for transfers between devices: 91.5 us -> none  [the longest x1 66.1 us: body(): gathered = lax.all_gather(head_kv, 'sh', axis=1, tiled=True)]
    psum x2 -> x0, waiting for transfers between devices: 91 us -> none  [the longest x1 46.5 us: body(): lax.psum(attn_part.astype(jnp.bfloat16), 'co')]
    ppermute x0 -> x10, waiting for transfers between devices: none -> 79.6 us  [shifted_copies(): moved.append(lax.ppermute(x, axis_name, pairs))]
    all_gather x1, waiting for transfers between devices: 57.5 us -> 82 us  [body(): lax.all_gather(lax.all_to_all(outgoing_part, SEQ, split_axis=0, concat_ax...]
    ppermute x0 -> x10, starting transfers between devices: none -> 18.2 us  [shifted_copies(): moved.append(lax.ppermute(x, axis_name, pairs))]
    all_to_all x1, blocking collectives: 36.3 us -> 51.1 us  [body(): lax.all_to_all(outgoing_part, SEQ, split_axis=0, concat_axis=0, tiled=True)]
    unnamed x41 -> x50, local copies, waits for them, and re-layouts: 7.65 us -> 17.1 us
    reduce_scatter x2 -> x1, waiting for transfers between devices: 80.6 us -> 79.9 us  [body(): lax.psum_scatter(expert_part, EXP, scatter_dimension=3, tiled=True)]
  transfers between devices with their start and end apart: 9 -> 14, of which waited for: 9 -> 11; matrix products, arithmetic and copies ran while one was open for 4% -> 5% of each run, Pallas kernels for 0% -> 0%
where the time goes in v4:
time: 527 us; the launch traced here: 525 us
  waiting for transfers between devices  276 us (52%)
  blocking collectives  76.5 us (15%)
  local copies, waits for them, and re-layouts  64.6 us (12%)
  other arithmetic  29.9 us (6%)
  matrix products  29.1 us (6%)
  starting transfers between devices  27.8 us (5%)
  between operations  16.5 us (3%)
    all_gather x1, waiting for transfers between devices, body(): lax.all_gather(lax.all_to_all(outgoing_part, SEQ, split_axis=0, concat_ax...  82 us
    reduce_scatter x1, waiting for transfers between devices, body(): lax.psum_scatter(expert_part, EXP, scatter_dimension=3, tiled=True)  79.9 us
    ppermute x10, waiting for transfers between devices, shifted_copies(): moved.append(lax.ppermute(x, axis_name, pairs))  79.6 us
    all_to_all x1, blocking collectives, body(): lax.all_to_all(outgoing_part, SEQ, split_axis=0, concat_axis=0, tiled=True)  51.1 us
    all_to_all x1, waiting for transfers between devices, body(): lax.all_to_all(summed.astype(jnp.bfloat16), SEQ, split_axis=0, concat_axi...  19.4 us
    ppermute x10, starting transfers between devices, shifted_copies(): moved.append(lax.ppermute(x, axis_name, pairs))  18.2 us
    gather x1, local copies, waits for them, and re-layouts, body(): normed[jnp.maximum(source_row, 0)]  17.7 us
    unnamed x50, local copies, waits for them, and re-layouts  17.1 us
  transfers between devices with their start and end apart: 14, of which 11 were waited for; matrix products, arithmetic and copies ran while one was open for 5% of the time, Pallas kernels for 0%

profile of v4, /device:TPU:1, one launch (start us, length us, event | category | flops | bytes accessed | tf_op | source)
XLA Modules:
  0.0 525.4 jit_solution(11950502814498170510)
XLA Ops:
  7.2 1.9 copy.102
  11.9 1.7 convert_reduce_fusion
  17.0 1.9 pad_maximum_fusion
  18.9 2.3 copy.103
  21.2 16.4 %all_to_all.40 = bf16[3,256,4,128]{3,1,0,2:T(8,128)(2,1)S(1)} all-to-all(bf16[3,256,4,128]{3,1,0,2:T(8,128)(2,1)} %copy.103), channel_id=1, replica_groups=mesh['sh'=8,'sl'=4,'zl'=2,'co'=2] {'sl'}, dimensions={2} | all-to-all | bytes 1572864 | tf_op jit(solution)/shard_map/all_to_all | solution.py:226
  39.4 5.8 %collective-permute-start = (bf16[2,1024,128]{2,1,0:T(8,128)(2,1)}, bf16[2,1024,128]{2,1,0:T(8,128)(2,1)}, u32[]{:S(2)}, u32[]{:S(2)}) collective-permute-start(bf16[2,1024,128]{2,1,0:T(8,128)(2,1)} %bitcast.18), channel_id=1, source_target_pairs={{0,112},{16,0},{32,16},{48,32},{64,48},{80,64},{96,80},{112,96},{1... | collective-permute-start | bytes 1572872 | tf_op jit(solution)/shard_map/ppermute | solution.py:132
  53.1 2.5 collective-permute-start.3
  55.6 1.5 collective-permute-start.4
  57.2 1.4 collective-permute-start.5
  59.6 7.3 %collective-permute-done.1 = bf16[2,1024,128]{2,1,0:T(8,128)(2,1)} collective-permute-done((bf16[2,1024,128]{2,1,0:T(8,128)(2,1)}, bf16[2,1024,128]{2,1,0:T(8,128)(2,1)}, u32[]{:S(2)}, u32[]{:S(2)}) %collective-permute-start.1) | collective-permute-done | bytes 524320 | tf_op jit(solution)/shard_map/ppermute | solution.py:132
  68.1 11.1 %collective-permute-done.3 = bf16[2,1024,128]{2,1,0:T(8,128)(2,1)S(1)} collective-permute-done((bf16[2,1024,128]{2,1,0:T(8,128)(2,1)}, bf16[2,1024,128]{2,1,0:T(8,128)(2,1)S(1)}, u32[]{:S(2)}, u32[]{:S(2)}) %collective-permute-start.3) | collective-permute-done | bytes 524320 | tf_op jit(solution)/shard_map/ppermute | solution.py:132
  79.3 11.2 %collective-permute-done.4 = bf16[2,1024,128]{2,1,0:T(8,128)(2,1)S(1)} collective-permute-done((bf16[2,1024,128]{2,1,0:T(8,128)(2,1)}, bf16[2,1024,128]{2,1,0:T(8,128)(2,1)S(1)}, u32[]{:S(2)}, u32[]{:S(2)}) %collective-permute-start.4) | collective-permute-done | bytes 524320 | tf_op jit(solution)/shard_map/ppermute | solution.py:132
  90.6 11.3 %collective-permute-done.5 = bf16[2,1024,128]{2,1,0:T(8,128)(2,1)S(1)} collective-permute-done((bf16[2,1024,128]{2,1,0:T(8,128)(2,1)}, bf16[2,1024,128]{2,1,0:T(8,128)(2,1)S(1)}, u32[]{:S(2)}, u32[]{:S(2)}) %collective-permute-start.5) | collective-permute-done | bytes 524320 | tf_op jit(solution)/shard_map/ppermute | solution.py:132
  107.1 5.2 shard_map.157
  113.2 8.9 %all_to_all.41 = bf16[4,256,1,128]{1,3,2,0:T(8,128)(2,1)S(1)} all-to-all(bf16[4,256,1,128]{1,3,2,0:T(8,128)(2,1)} %copy.106), channel_id=1, replica_groups=mesh['sh'=8,'sl'=4,'zl'=2,'co'=2] {'sl'}, dimensions={0} | all-to-all | bytes 524288 | tf_op jit(solution)/shard_map/all_to_all | solution.py:239
  122.1 3.3 convolution_convert_fusion
  125.4 4.8 collective-permute-start.9
  133.0 4.3 scatter_custom_fusion
  137.4 16.9 %collective-permute-done.9 = bf16[256,2048]{1,0:T(8,128)(2,1)} collective-permute-done((bf16[256,2048]{1,0:T(8,128)(2,1)}, bf16[256,2048]{1,0:T(8,128)(2,1)}, u32[]{:S(2)}, u32[]{:S(2)}) %collective-permute-start.9) | collective-permute-done | bytes 1048608 | tf_op jit(solution)/shard_map/ppermute | solution.py:132
  154.3 1.4 collective-permute-done.8
  155.7 20.5 %collective-permute-done.7 = bf16[256,2048]{1,0:T(8,128)(2,1)} collective-permute-done((bf16[256,2048]{1,0:T(8,128)(2,1)}, bf16[256,2048]{1,0:T(8,128)(2,1)}, u32[]{:S(2)}, u32[]{:S(2)}) %collective-permute-start.7) | collective-permute-done | bytes 1048608 | tf_op jit(solution)/shard_map/ppermute | solution.py:132
  176.2 4.3 multiply_reduce_fusion.1
  180.5 1.4 copy-done.3
  181.9 1.3 multiply_convert_fusion
  183.1 17.7 %gather_fusion = bf16[2048,2048]{1,0:T(8,128)(2,1)} fusion(bf16[256,2048]{1,0:T(8,128)(2,1)} %multiply_convert_fusion, s32[2048]{0:T(1024)S(1)} %maximum_clamp_fusion), kind=kCustom, calls=%fused_computation | custom fusion | bytes 16785408 | tf_op jit(solution)/shard_map/gather | solution.py:265
  200.9 1.9 dynamic-slice_select_fusion
  202.8 51.1 %all_to_all.42 = bf16[32,2,32,512]{3,2,1,0:T(8,128)(2,1)S(1)} all-to-all(bf16[32,2,32,512]{3,2,1,0:T(8,128)(2,1)S(1)} %dynamic-slice_select_fusion), channel_id=1, replica_groups=mesh['sh'=8,'sl'=4,'zl'=2,'co'=2] {'sh','sl'}, dimensions={0} | all-to-all | bytes 4194304 | tf_op jit(solution)/shard_map/all_to_all | solution.py:271
  254.0 1.6 copy.110
  255.6 82.0 %all-gather.2.cloned.1.call-done = bf16[32,2,32,2048]{3,2,0,1:T(8,128)(2,1)} async-done(((bf16[32,2,32,512]{3,2,0,1:T(8,128)(2,1)}), bf16[32,2,32,2048]{3,2,0,1:T(8,128)(2,1)}) %all-gather.2.cloned.1.call-update) | async-done | bytes 8388624 | tf_op jit(solution)/shard_map/all_gather | solution.py:270
  337.7 10.1 %fusion.7 = f32[32,2,32,2,352]{4,2,3,0,1:T(8,128)S(1)} fusion(bf16[2,2,2048,352]{2,3,1,0:T(8,128)(2,1)} %param.24, bf16[32,2,32,2048]{3,2,0,1:T(8,128)(2,1)} %all-gather.2.cloned.1.call-done), kind=kOutput, calls=%fused_computation.18 | convolution fusion | flops 5905580032 | bytes 19922944 | tf_op jit(solution)/shard_map/nscd,sgde->nscge/dot_general | solution.py:184
  347.8 6.7 %convert_bitcast_fusion = bf16[32,2,32,2048]{3,2,0,1:T(8,128)(2,1)} fusion(bf16[2,352,2048]{2,1,0:T(8,128)(2,1)S(1)} %copy-done.13, f32[32,2,32,2,352]{4,2,3,0,1:T(8,128)S(1)} %fusion.7), kind=kOutput, calls=%fused_computation.5 | convolution fusion | flops 2961309696 | bytes 17039360 | tf_op jit(solution)/shard_map/nsce,sed->nscd/dot_general | solution.py:190
  354.6 79.9 %reduce-scatter.3.cloned.1.call-done = bf16[32,2,32,512]{3,2,0,1:T(8,128)(2,1)} async-done(((bf16[32,2,32,2048]{3,2,0,1:T(8,128)(2,1)}), bf16[32,2,32,512]{3,2,0,1:T(8,128)(2,1)}) %reduce-scatter.3.cloned.1.call-update) | async-done | bytes 2097168 | tf_op jit(solution)/shard_map/reduce_scatter | solution.py:277
  434.5 3.2 copy.112
  437.7 9.2 %all-to-all-start.3 = ((bf16[32,2,32,512]{3,2,1,0:T(8,128)(2,1)}), bf16[32,2,32,512]{3,2,1,0:T(8,128)(2,1)}, u32[]{:S(2)}, u32[]{:S(2)}) async-start(bf16[32,2,32,512]{3,2,1,0:T(8,128)(2,1)} %copy.112), calls=%async_computation.4 | async-start | bytes 4194304 | tf_op jit(solution)/shard_map/all_to_all | solution.py:280
  447.4 1.6 fusion.30
  449.0 4.9 fusion.14
  454.0 2.4 convolution_multiply_fusion
  456.4 19.4 %all-to-all-done.3 = bf16[32,2,32,512]{3,2,1,0:T(8,128)(2,1)} async-done(((bf16[32,2,32,512]{3,2,1,0:T(8,128)(2,1)}), bf16[32,2,32,512]{3,2,1,0:T(8,128)(2,1)}, u32[]{:S(2)}, u32[]{:S(2)}) %all-to-all-start.3) | async-done | bytes 2097184 | tf_op jit(solution)/shard_map/all_to_all | solution.py:280
  475.8 4.2 bitcast_convert_fusion
  479.9 7.5 %gather_fusion.1 = f32[1024,512]{1,0:T(8,128)} fusion(f32[2048,512]{1,0:T(8,128)} %bitcast_convert_fusion, s32[1024]{0:T(1024)S(1)} %broadcast_clamp_fusion), kind=kCustom, calls=%fused_computation.1 | custom fusion | bytes 4198400 | tf_op jit(solution)/shard_map/gather | solution.py:283
  487.4 2.9 reshape.233
  490.3 3.0 multiply_reduce_fusion
  493.3 2.0 add_dynamic-update-slice_fusion
  495.3 2.7 convert_element_type.107
  498.8 1.8 copy.113
  500.6 1.7 dynamic-slice_convert_fusion
  502.3 14.7 %reduce-scatter.5.cloned.1.call-done = bf16[64,2048]{1,0:T(8,128)(2,1)} async-done(((bf16[256,2048]{1,0:T(8,128)(2,1)}), bf16[64,2048]{1,0:T(8,128)(2,1)}) %reduce-scatter.5.cloned.1.call-update) | async-done | bytes 262160 | tf_op jit(solution)/shard_map/reduce_scatter | solution.py:291
  517.0 1.9 add_convert_fusion
  (95 shorter events, 25.9 us)
Async XLA Ops:
  7.2 446.8 %copy-start = (bf16[768,2048]{1,0:T(8,128)(2,1)S(1)}, bf16[768,2048]{1,0:T(8,128)(2,1)}, u32[]{:S(2)}) copy-start(bf16[768,2048]{1,0:T(8,128)(2,1)} %param.22) | copy-start | bytes 9437188
  7.2 330.5 %all-gather.2.cloned.1.call-start = ((), (), s32[]{:S(2)}) async-start(), calls=%async_computation.6 | async-start | bytes 10485760 | tf_op jit(solution)/shard_map/all_gather | solution.py:270
  15.1 30.2 %copy-start.2 = (s32[8192]{0:T(1024)S(1)}, s32[8192]{0:T(1024)}, u32[]{:S(2)}) copy-start(s32[8192]{0:T(1024)} %param.14) | copy-start | bytes 98308
  16.3 0.7 copy-start.5
  16.3 0.7 copy-start.7
  37.7 0.9 copy-start.4
  39.4 17.7 %collective-permute-start = (bf16[2,1024,128]{2,1,0:T(8,128)(2,1)}, bf16[2,1024,128]{2,1,0:T(8,128)(2,1)}, u32[]{:S(2)}, u32[]{:S(2)}) collective-permute-start(bf16[2,1024,128]{2,1,0:T(8,128)(2,1)} %bitcast.18), channel_id=1, source_target_pairs={{0,112},{16,0},{32,16},{48,32},{64,48},{80,64},{96,80},{112,96},{1... | collective-permute-start | bytes 1572872 | tf_op jit(solution)/shard_map/ppermute | solution.py:132
  45.8 21.1 %collective-permute-start.1 = (bf16[2,1024,128]{2,1,0:T(8,128)(2,1)}, bf16[2,1024,128]{2,1,0:T(8,128)(2,1)}, u32[]{:S(2)}, u32[]{:S(2)}) collective-permute-start(bf16[2,1024,128]{2,1,0:T(8,128)(2,1)} %bitcast.18), channel_id=1, source_target_pairs={{0,96},{16,112},{32,0},{48,16},{64,32},{80,48},{96,64},{112,80},{1... | collective-permute-start | bytes 1572872 | tf_op jit(solution)/shard_map/ppermute | solution.py:132
  51.0 17.0 %collective-permute-start.2 = (bf16[2,1024,128]{2,1,0:T(8,128)(2,1)}, bf16[2,1024,128]{2,1,0:T(8,128)(2,1)S(1)}, u32[]{:S(2)}, u32[]{:S(2)}) collective-permute-start(bf16[2,1024,128]{2,1,0:T(8,128)(2,1)} %bitcast.18), channel_id=1, source_target_pairs={{0,80},{16,96},{32,112},{48,0},{64,16},{80,32},{96,48},{112,64},{1... | collective-permute-start | bytes 1572872 | tf_op jit(solution)/shard_map/ppermute | solution.py:132
  53.1 26.1 %collective-permute-start.3 = (bf16[2,1024,128]{2,1,0:T(8,128)(2,1)}, bf16[2,1024,128]{2,1,0:T(8,128)(2,1)S(1)}, u32[]{:S(2)}, u32[]{:S(2)}) collective-permute-start(bf16[2,1024,128]{2,1,0:T(8,128)(2,1)} %bitcast.18), channel_id=1, source_target_pairs={{0,64},{16,80},{32,96},{48,112},{64,0},{80,16},{96,32},{112,48},{1... | collective-permute-start | bytes 1572872 | tf_op jit(solution)/shard_map/ppermute | solution.py:132
  55.6 34.9 %collective-permute-start.4 = (bf16[2,1024,128]{2,1,0:T(8,128)(2,1)}, bf16[2,1024,128]{2,1,0:T(8,128)(2,1)S(1)}, u32[]{:S(2)}, u32[]{:S(2)}) collective-permute-start(bf16[2,1024,128]{2,1,0:T(8,128)(2,1)} %bitcast.18), channel_id=1, source_target_pairs={{0,48},{16,64},{32,80},{48,96},{64,112},{80,0},{96,16},{112,32},{1... | collective-permute-start | bytes 1572872 | tf_op jit(solution)/shard_map/ppermute | solution.py:132
  57.2 44.7 %collective-permute-start.5 = (bf16[2,1024,128]{2,1,0:T(8,128)(2,1)}, bf16[2,1024,128]{2,1,0:T(8,128)(2,1)S(1)}, u32[]{:S(2)}, u32[]{:S(2)}) collective-permute-start(bf16[2,1024,128]{2,1,0:T(8,128)(2,1)} %bitcast.18), channel_id=1, source_target_pairs={{0,32},{16,48},{32,64},{48,80},{64,96},{80,112},{96,0},{112,16},{1... | collective-permute-start | bytes 1572872 | tf_op jit(solution)/shard_map/ppermute | solution.py:132
  66.9 35.0 %collective-permute-start.6 = (bf16[2,1024,128]{2,1,0:T(8,128)(2,1)}, bf16[2,1024,128]{2,1,0:T(8,128)(2,1)S(1)}, u32[]{:S(2)}, u32[]{:S(2)}) collective-permute-start(bf16[2,1024,128]{2,1,0:T(8,128)(2,1)} %bitcast.18), channel_id=1, source_target_pairs={{0,16},{16,32},{32,48},{48,64},{64,80},{80,96},{96,112},{112,0},{1... | collective-permute-start | bytes 1572872 | tf_op jit(solution)/shard_map/ppermute | solution.py:132
  106.0 1.0 copy-start.1
  112.3 19.5 %copy-start.9 = (s32[256,4]{0,1:T(4,128)S(1)}, s32[256,4]{0,1:T(4,128)}, u32[]{:S(2)}) copy-start(s32[256,4]{0,1:T(4,128)} %param.26) | copy-start | bytes 12292
  112.3 19.7 %copy-start.10 = (bf16[2048]{0:T(1024)(128)(2,1)S(1)}, bf16[2048]{0:T(1024)(128)(2,1)}, u32[]{:S(2)}) copy-start(bf16[2048]{0:T(1024)(128)(2,1)} %param.20) | copy-start | bytes 12292
  125.4 29.0 %collective-permute-start.9 = (bf16[256,2048]{1,0:T(8,128)(2,1)}, bf16[256,2048]{1,0:T(8,128)(2,1)}, u32[]{:S(2)}, u32[]{:S(2)}) collective-permute-start(bf16[256,2048]{1,0:T(8,128)(2,1)} %convolution_convert_fusion), channel_id=1, source_target_pairs={{0,3},{1,0},{2,1},{3,2},{4,7},{5,4},{6,5},{7,6},{8,11},{9,8},{10,9... | collective-permute-start | bytes 3145736 | tf_op jit(solution)/shard_map/ppermute | solution.py:132
  130.2 25.5 %collective-permute-start.8 = (bf16[256,2048]{1,0:T(8,128)(2,1)}, bf16[256,2048]{1,0:T(8,128)(2,1)}, u32[]{:S(2)}, u32[]{:S(2)}) collective-permute-start(bf16[256,2048]{1,0:T(8,128)(2,1)} %convolution_convert_fusion), channel_id=1, source_target_pairs={{0,2},{1,3},{2,0},{3,1},{4,6},{5,7},{6,4},{7,5},{8,10},{9,11},{10,... | collective-permute-start | bytes 3145736 | tf_op jit(solution)/shard_map/ppermute | solution.py:132
  131.0 45.2 %collective-permute-start.7 = (bf16[256,2048]{1,0:T(8,128)(2,1)}, bf16[256,2048]{1,0:T(8,128)(2,1)}, u32[]{:S(2)}, u32[]{:S(2)}) collective-permute-start(bf16[256,2048]{1,0:T(8,128)(2,1)} %convolution_convert_fusion), channel_id=1, source_target_pairs={{0,1},{1,2},{2,3},{3,0},{4,5},{5,6},{6,7},{7,4},{8,9},{9,10},{10,1... | collective-permute-start | bytes 3145736 | tf_op jit(solution)/shard_map/ppermute | solution.py:132
  180.5 1.4 copy-start.3
  255.6 178.9 %reduce-scatter.3.cloned.1.call-start = ((), (), s32[]{:S(2)}) async-start(), calls=%async_computation.7 | async-start | bytes 10485760 | tf_op jit(solution)/shard_map/reduce_scatter | solution.py:277
  337.7 10.2 %copy-start.13 = (bf16[2,352,2048]{2,1,0:T(8,128)(2,1)S(1)}, bf16[2,352,2048]{2,1,0:T(8,128)(2,1)}, u32[]{:S(2)}) copy-start(bf16[2,352,2048]{2,1,0:T(8,128)(2,1)} %param.25) | copy-start | bytes 8650756
  354.6 92.6 %copy-start.11 = (bf16[2048]{0:T(1024)(128)(2,1)S(1)}, bf16[2048]{0:T(1024)(128)(2,1)}, u32[]{:S(2)}) copy-start(bf16[2048]{0:T(1024)(128)(2,1)} %param.23) | copy-start | bytes 12292
  354.6 92.6 %copy-start.12 = (f32[256,4]{0,1:T(4,128)S(1)}, f32[256,4]{0,1:T(4,128)}, u32[]{:S(2)}) copy-start(f32[256,4]{0,1:T(4,128)} %param.27) | copy-start | bytes 12292
  437.7 38.1 %all-to-all-start.3 = ((bf16[32,2,32,512]{3,2,1,0:T(8,128)(2,1)}), bf16[32,2,32,512]{3,2,1,0:T(8,128)(2,1)}, u32[]{:S(2)}, u32[]{:S(2)}) async-start(bf16[32,2,32,512]{3,2,1,0:T(8,128)(2,1)} %copy.112), calls=%async_computation.4 | async-start | bytes 4194304 | tf_op jit(solution)/shard_map/all_to_all | solution.py:280
  446.9 70.0 %reduce-scatter.5.cloned.1.call-start = ((), (), s32[]{:S(2)}) async-start(), calls=%async_computation.8 | async-start | bytes 1310720 | tf_op jit(solution)/shard_map/reduce_scatter | solution.py:291
  490.3 7.8 %copy-start.6 = (bf16[256,4,64]{0,2,1:T(8,128)(2,1)S(1)}, bf16[256,4,64]{0,2,1:T(8,128)(2,1)}, u32[]{:S(2)}) copy-start(bf16[256,4,64]{0,2,1:T(8,128)(2,1)} %copy-done.5) | copy-start | bytes 393220
  490.3 7.8 %copy-start.8 = (bf16[256,4,64]{0,2,1:T(8,128)(2,1)S(1)}, bf16[256,4,64]{0,2,1:T(8,128)(2,1)}, u32[]{:S(2)}) copy-start(bf16[256,4,64]{0,2,1:T(8,128)(2,1)} %copy-done.7) | copy-start | bytes 393220
Sparse Core Ops, SparseCore 0:
  255.7 81.9 all-gather.1
  354.7 79.7 reduce-scatter.2
  498.2 18.7 reduce-scatter.4

commit v5 on v4

--- a/solution.py
+++ b/solution.py
@@ -257,16 +257,19 @@
     earlier_same = (flat_ids[None, :] == flat_ids[:, None]) & (flat_index[None, :] < flat_index[:, None])
     slot_rank = jnp.sum(earlier_same.astype(jnp.int32), axis=1)
     slot_place = flat_ids * CAP + slot_rank
-    owner_row = jnp.arange(flat_ids.shape[0], dtype=jnp.int32) // TOPK
-    source_row = jnp.full((SLOTS * CAP,), -1, jnp.int32).at[slot_place].set(owner_row)
     slot_local = SLOTS // seq_count
     model_width = normed.shape[1]
-    outgoing = jnp.where(
-        (source_row >= 0)[:, None], normed[jnp.maximum(source_row, 0)], jnp.zeros((), jnp.bfloat16)
-    ).reshape(seq_count, slot_local, CAP, model_width)
     col_count = model_width // exp_count
     col_first = exp_place * col_count
-    outgoing_part = lax.dynamic_slice_in_dim(outgoing, col_first, col_count, 3)
+    slot_rows = jnp.arange(SLOTS * CAP, dtype=jnp.int32)
+    place_hit = (slot_place[None, :] == slot_rows[:, None]).reshape(SLOTS * CAP, block_len, TOPK)
+    dispatch = jnp.any(place_hit, axis=2).astype(jnp.bfloat16)
+    normed_part = lax.dynamic_slice_in_dim(normed, col_first, col_count, 1)
+    outgoing_part = (
+        jnp.dot(dispatch, normed_part, preferred_element_type=jnp.float32)
+        .astype(jnp.bfloat16)
+        .reshape(seq_count, slot_local, CAP, col_count)
+    )
     incoming = lax.all_gather(
         lax.all_to_all(outgoing_part, SEQ, split_axis=0, concat_axis=0, tiled=True),
         EXP,
@@ -280,9 +283,12 @@
     returned = lax.all_to_all(
         summed.astype(jnp.bfloat16), SEQ, split_axis=0, concat_axis=0, tiled=True
     ).astype(summed.dtype)
-    picked = returned.reshape(SLOTS * CAP, col_count)[slot_place].reshape(
-        block_len, TOPK, col_count
-    )
+    select_rows = (slot_place[:, None] == slot_rows[None, :]).astype(jnp.bfloat16)
+    picked = jnp.dot(
+        select_rows,
+        returned.reshape(SLOTS * CAP, col_count).astype(jnp.bfloat16),
+        preferred_element_type=jnp.float32,
+    ).reshape(block_len, TOPK, col_count)
     moe_cols = jnp.sum(gate_weights[:, :, None] * picked, axis=1)
     moe_term = lax.dynamic_update_slice_in_dim(
         jnp.zeros((block_len, model_width), jnp.float32), moe_cols, col_first, 1

time: 527 us -> 489 us (0.928)
  local copies, waits for them, and re-layouts: 64.6 us -> 31 us
  other arithmetic: 29.9 us -> 18.9 us
    gather x2 -> x0, local copies, waits for them, and re-layouts: 25.2 us -> none  [the longest x1 17.7 us: body(): normed[jnp.maximum(source_row, 0)]]
    unnamed x50 -> x53, local copies, waits for them, and re-layouts: 17.1 us -> 16.2 us
where the time goes in v5:
time: 489 us; the launch traced here: 488 us
  waiting for transfers between devices  278 us (57%)
  blocking collectives  76.1 us (16%)
  matrix products  34 us (7%)
  local copies, waits for them, and re-layouts  31 us (6%)
  starting transfers between devices  28 us (6%)
  other arithmetic  18.9 us (4%)
  between operations  16.9 us (3%)
  Pallas kernels  5.23 us (1%)
    all_gather x1, waiting for transfers between devices, body(): lax.all_gather(lax.all_to_all(outgoing_part, SEQ, split_axis=0, concat_ax...  82 us
    ppermute x10, waiting for transfers between devices, shifted_copies(): moved.append(lax.ppermute(x, axis_name, pairs))  81.3 us
    reduce_scatter x1, waiting for transfers between devices, body(): lax.psum_scatter(expert_part, EXP, scatter_dimension=3, tiled=True)  79.9 us
    all_to_all x1, blocking collectives, body(): lax.all_to_all(outgoing_part, SEQ, split_axis=0, concat_axis=0, tiled=True)  50.8 us
    all_to_all x1, waiting for transfers between devices, body(): lax.all_to_all(summed.astype(jnp.bfloat16), SEQ, split_axis=0, concat_axi...  19.6 us
    ppermute x10, starting transfers between devices, shifted_copies(): moved.append(lax.ppermute(x, axis_name, pairs))  18.4 us
    all_to_all x1, blocking collectives, body(): lax.all_to_all(stacked, 'sl', split_axis=2, concat_axis=1, tiled=True)  16.4 us
    unnamed x53, local copies, waits for them, and re-layouts  16.2 us
  transfers between devices with their start and end apart: 14, of which 11 were waited for; matrix products, arithmetic and copies ran while one was open for 5% of the time, Pallas kernels for 0%

profile of v5, /device:TPU:1, one launch (start us, length us, event | category | flops | bytes accessed | tf_op | source)
XLA Modules:
  0.0 487.8 jit_solution(4287683067888270926)
XLA Ops:
  7.2 1.9 copy.121
  11.9 1.7 convert_reduce_fusion
  15.1 1.2 fusion.28
  17.0 1.9 pad_maximum_fusion
  18.9 2.3 copy.122
  21.2 16.4 %all_to_all.40 = bf16[3,256,4,128]{3,1,0,2:T(8,128)(2,1)S(1)} all-to-all(bf16[3,256,4,128]{3,1,0,2:T(8,128)(2,1)} %copy.122), channel_id=1, replica_groups=mesh['sh'=8,'sl'=4,'zl'=2,'co'=2] {'sl'}, dimensions={2} | all-to-all | bytes 1572864 | tf_op jit(solution)/shard_map/all_to_all | solution.py:226
  39.4 5.8 %collective-permute-start = (bf16[2,1024,128]{2,1,0:T(8,128)(2,1)}, bf16[2,1024,128]{2,1,0:T(8,128)(2,1)}, u32[]{:S(2)}, u32[]{:S(2)}) collective-permute-start(bf16[2,1024,128]{2,1,0:T(8,128)(2,1)} %bitcast.18), channel_id=1, source_target_pairs={{0,112},{16,0},{32,16},{48,32},{64,48},{80,64},{96,80},{112,96},{1... | collective-permute-start | bytes 1572872 | tf_op jit(solution)/shard_map/ppermute | solution.py:132
  46.3 1.3 convert_reduce_fusion.2
  51.4 1.1 constant_dynamic-update-slice_fusion.1
  53.5 2.5 collective-permute-start.3
  56.0 1.5 collective-permute-start.4
  57.5 1.4 collective-permute-start.5
  58.8 1.1 bitcast_dynamic-update-slice_fusion.12
  59.9 7.1 %collective-permute-done.1 = bf16[2,1024,128]{2,1,0:T(8,128)(2,1)} collective-permute-done((bf16[2,1024,128]{2,1,0:T(8,128)(2,1)}, bf16[2,1024,128]{2,1,0:T(8,128)(2,1)}, u32[]{:S(2)}, u32[]{:S(2)}) %collective-permute-start.1) | collective-permute-done | bytes 524320 | tf_op jit(solution)/shard_map/ppermute | solution.py:132
  67.0 1.1 bitcast_dynamic-update-slice_fusion.10
  68.2 11.0 %collective-permute-done.3 = bf16[2,1024,128]{2,1,0:T(8,128)(2,1)S(1)} collective-permute-done((bf16[2,1024,128]{2,1,0:T(8,128)(2,1)}, bf16[2,1024,128]{2,1,0:T(8,128)(2,1)S(1)}, u32[]{:S(2)}, u32[]{:S(2)}) %collective-permute-start.3) | collective-permute-done | bytes 524320 | tf_op jit(solution)/shard_map/ppermute | solution.py:132
  79.3 11.2 %collective-permute-done.4 = bf16[2,1024,128]{2,1,0:T(8,128)(2,1)S(1)} collective-permute-done((bf16[2,1024,128]{2,1,0:T(8,128)(2,1)}, bf16[2,1024,128]{2,1,0:T(8,128)(2,1)S(1)}, u32[]{:S(2)}, u32[]{:S(2)}) %collective-permute-start.4) | collective-permute-done | bytes 524320 | tf_op jit(solution)/shard_map/ppermute | solution.py:132
  90.5 11.5 %collective-permute-done.5 = bf16[2,1024,128]{2,1,0:T(8,128)(2,1)S(1)} collective-permute-done((bf16[2,1024,128]{2,1,0:T(8,128)(2,1)}, bf16[2,1024,128]{2,1,0:T(8,128)(2,1)S(1)}, u32[]{:S(2)}, u32[]{:S(2)}) %collective-permute-start.5) | collective-permute-done | bytes 524320 | tf_op jit(solution)/shard_map/ppermute | solution.py:132
  102.1 1.1 constant_dynamic-update-slice_fusion
  103.3 1.1 bitcast_dynamic-update-slice_fusion.13
  104.4 1.1 bitcast_dynamic-update-slice_fusion.11
  107.3 5.2 %shard_map.157 = bf16[1024,128]{1,0:T(8,128)(2,1)S(1)} custom-call(s32[3]{0:T(128)S(1)} %pad_add_fusion.bounds_ref, bf16[1024,128]{1,0:T(8,128)(2,1)S(1)} %bitcast.129, bf16[8192,128]{1,0:T(8,128)(2,1)S(1)} %bitcast.128, bf16[8192,128]{1,0:T(8,128)(2,1)S(1)} %bitcast.127, s32[1024,1]{1,0:T(8,128)S(1)} %copy-done.1, s32[1,8192]{1,0:T(1,128)S(1)} %bitcast.131), custom_call_target="tpu_custom_call" | custom-call | flops 4294967296 | bytes 4718592 | tf_op jit(solution)/shard_map/pallas_call | solution.py:106
  113.4 8.9 %all_to_all.41 = bf16[4,256,1,128]{1,3,2,0:T(8,128)(2,1)S(1)} all-to-all(bf16[4,256,1,128]{1,3,2,0:T(8,128)(2,1)} %copy.125), channel_id=1, replica_groups=mesh['sh'=8,'sl'=4,'zl'=2,'co'=2] {'sl'}, dimensions={0} | all-to-all | bytes 524288 | tf_op jit(solution)/shard_map/all_to_all | solution.py:239
  122.3 3.3 convolution_convert_fusion.1
  125.6 5.0 %collective-permute-start.9 = (bf16[256,2048]{1,0:T(8,128)(2,1)}, bf16[256,2048]{1,0:T(8,128)(2,1)}, u32[]{:S(2)}, u32[]{:S(2)}) collective-permute-start(bf16[256,2048]{1,0:T(8,128)(2,1)} %convolution_convert_fusion.1), channel_id=1, source_target_pairs={{0,3},{1,0},{2,1},{3,2},{4,7},{5,4},{6,5},{7,6},{8,11},{9,8},{10,9... | collective-permute-start | bytes 3145736 | tf_op jit(solution)/shard_map/ppermute | solution.py:132
  133.3 2.6 fusion.5
  135.9 18.8 %collective-permute-done.9 = bf16[256,2048]{1,0:T(8,128)(2,1)} collective-permute-done((bf16[256,2048]{1,0:T(8,128)(2,1)}, bf16[256,2048]{1,0:T(8,128)(2,1)}, u32[]{:S(2)}, u32[]{:S(2)}) %collective-permute-start.9) | collective-permute-done | bytes 1048608 | tf_op jit(solution)/shard_map/ppermute | solution.py:132
  154.7 1.4 collective-permute-done.8
  156.1 20.5 %collective-permute-done.7 = bf16[256,2048]{1,0:T(8,128)(2,1)} collective-permute-done((bf16[256,2048]{1,0:T(8,128)(2,1)}, bf16[256,2048]{1,0:T(8,128)(2,1)}, u32[]{:S(2)}, u32[]{:S(2)}) %collective-permute-start.7) | collective-permute-done | bytes 1048608 | tf_op jit(solution)/shard_map/ppermute | solution.py:132
  176.6 4.3 multiply_reduce_fusion.1
  182.4 50.8 %all_to_all.42 = bf16[32,2,32,512]{3,2,1,0:T(8,128)(2,1)S(1)} all-to-all(bf16[32,2,32,512]{3,2,1,0:T(8,128)(2,1)S(1)} %bitcast.134), channel_id=1, replica_groups=mesh['sh'=8,'sl'=4,'zl'=2,'co'=2] {'sh','sl'}, dimensions={0} | all-to-all | bytes 4194304 | tf_op jit(solution)/shard_map/all_to_all | solution.py:274
  233.1 1.6 copy.128
  234.8 82.0 %all-gather.2.cloned.1.call-done = bf16[32,2,32,2048]{3,2,0,1:T(8,128)(2,1)} async-done(((bf16[32,2,32,512]{3,2,0,1:T(8,128)(2,1)}), bf16[32,2,32,2048]{3,2,0,1:T(8,128)(2,1)}) %all-gather.2.cloned.1.call-update) | async-done | bytes 8388624 | tf_op jit(solution)/shard_map/all_gather | solution.py:273
  316.8 10.1 %fusion.12 = f32[32,2,32,2,352]{4,2,3,0,1:T(8,128)S(1)} fusion(bf16[2,2,2048,352]{2,3,1,0:T(8,128)(2,1)} %param.24, bf16[32,2,32,2048]{3,2,0,1:T(8,128)(2,1)} %all-gather.2.cloned.1.call-done), kind=kOutput, calls=%fused_computation.22 | convolution fusion | flops 5905580032 | bytes 19922944 | tf_op jit(solution)/shard_map/nscd,sgde->nscge/dot_general | solution.py:184
  327.0 6.7 %convert_bitcast_fusion = bf16[32,2,32,2048]{3,2,0,1:T(8,128)(2,1)} fusion(bf16[2,352,2048]{2,1,0:T(8,128)(2,1)S(1)} %copy-done.14, f32[32,2,32,2,352]{4,2,3,0,1:T(8,128)S(1)} %fusion.12), kind=kOutput, calls=%fused_computation.2 | convolution fusion | flops 2961309696 | bytes 17039360 | tf_op jit(solution)/shard_map/nsce,sed->nscd/dot_general | solution.py:190
  333.7 79.9 %reduce-scatter.3.cloned.1.call-done = bf16[32,2,32,512]{3,2,0,1:T(8,128)(2,1)} async-done(((bf16[32,2,32,2048]{3,2,0,1:T(8,128)(2,1)}), bf16[32,2,32,512]{3,2,0,1:T(8,128)(2,1)}) %reduce-scatter.3.cloned.1.call-update) | async-done | bytes 2097168 | tf_op jit(solution)/shard_map/reduce_scatter | solution.py:280
  413.7 3.2 copy.130
  416.9 9.2 %all-to-all-start.3 = ((bf16[32,2,32,512]{3,2,1,0:T(8,128)(2,1)}), bf16[32,2,32,512]{3,2,1,0:T(8,128)(2,1)}, u32[]{:S(2)}, u32[]{:S(2)}) async-start(bf16[32,2,32,512]{3,2,1,0:T(8,128)(2,1)} %copy.130), calls=%async_computation.4 | async-start | bytes 4194304 | tf_op jit(solution)/shard_map/all_to_all | solution.py:283
  426.4 1.6 fusion.34
  428.0 4.9 %fusion.21 = f32[256,2,768]{2,0,1:T(8,128)S(1)} fusion(bf16[2,2048,768]{2,1,0:T(8,128)(2,1)} %param.21, bf16[256,2048]{1,0:T(8,128)(2,1)} %copy-done.4), kind=kOutput, calls=%fused_computation.30 | convolution fusion | flops 1610612736 | bytes 8912896 | tf_op jit(solution)/shard_map/td,gde->tge/dot_general | solution.py:251
  433.0 2.4 convolution_multiply_fusion
  435.4 19.6 %all-to-all-done.3 = bf16[32,2,32,512]{3,2,1,0:T(8,128)(2,1)} async-done(((bf16[32,2,32,512]{3,2,1,0:T(8,128)(2,1)}), bf16[32,2,32,512]{3,2,1,0:T(8,128)(2,1)}, u32[]{:S(2)}, u32[]{:S(2)}) %all-to-all-start.3) | async-done | bytes 2097184 | tf_op jit(solution)/shard_map/all_to_all | solution.py:283
  455.0 4.2 multiply_reduce_fusion
  459.3 1.1 convert_element_type.118
  461.2 1.8 copy.131
  463.0 1.7 dynamic-slice_convert_fusion
  464.6 14.8 %reduce-scatter.5.cloned.1.call-done = bf16[64,2048]{1,0:T(8,128)(2,1)} async-done(((bf16[256,2048]{1,0:T(8,128)(2,1)}), bf16[64,2048]{1,0:T(8,128)(2,1)}) %reduce-scatter.5.cloned.1.call-update) | async-done | bytes 262160 | tf_op jit(solution)/shard_map/reduce_scatter | solution.py:297
  479.4 1.9 add_convert_fusion
  (88 shorter events, 18.1 us)
Async XLA Ops:
  7.2 425.8 %copy-start = (bf16[768,2048]{1,0:T(8,128)(2,1)S(1)}, bf16[768,2048]{1,0:T(8,128)(2,1)}, u32[]{:S(2)}) copy-start(bf16[768,2048]{1,0:T(8,128)(2,1)} %param.22) | copy-start | bytes 9437188
  7.2 309.6 %all-gather.2.cloned.1.call-start = ((), (), s32[]{:S(2)}) async-start(), calls=%async_computation.6 | async-start | bytes 10485760 | tf_op jit(solution)/shard_map/all_gather | solution.py:273
  15.1 30.1 %copy-start.2 = (s32[8192]{0:T(1024)S(1)}, s32[8192]{0:T(1024)}, u32[]{:S(2)}) copy-start(s32[8192]{0:T(1024)} %param.14) | copy-start | bytes 98308
  16.3 0.7 copy-start.7
  16.3 0.7 copy-start.9
  37.7 0.9 copy-start.6
  39.4 18.1 %collective-permute-start = (bf16[2,1024,128]{2,1,0:T(8,128)(2,1)}, bf16[2,1024,128]{2,1,0:T(8,128)(2,1)}, u32[]{:S(2)}, u32[]{:S(2)}) collective-permute-start(bf16[2,1024,128]{2,1,0:T(8,128)(2,1)} %bitcast.18), channel_id=1, source_target_pairs={{0,112},{16,0},{32,16},{48,32},{64,48},{80,64},{96,80},{112,96},{1... | collective-permute-start | bytes 1572872 | tf_op jit(solution)/shard_map/ppermute | solution.py:132
  45.7 21.3 %collective-permute-start.1 = (bf16[2,1024,128]{2,1,0:T(8,128)(2,1)}, bf16[2,1024,128]{2,1,0:T(8,128)(2,1)}, u32[]{:S(2)}, u32[]{:S(2)}) collective-permute-start(bf16[2,1024,128]{2,1,0:T(8,128)(2,1)} %bitcast.18), channel_id=1, source_target_pairs={{0,96},{16,112},{32,0},{48,16},{64,32},{80,48},{96,64},{112,80},{1... | collective-permute-start | bytes 1572872 | tf_op jit(solution)/shard_map/ppermute | solution.py:132
  51.4 16.8 %collective-permute-start.2 = (bf16[2,1024,128]{2,1,0:T(8,128)(2,1)}, bf16[2,1024,128]{2,1,0:T(8,128)(2,1)S(1)}, u32[]{:S(2)}, u32[]{:S(2)}) collective-permute-start(bf16[2,1024,128]{2,1,0:T(8,128)(2,1)} %bitcast.18), channel_id=1, source_target_pairs={{0,80},{16,96},{32,112},{48,0},{64,16},{80,32},{96,48},{112,64},{1... | collective-permute-start | bytes 1572872 | tf_op jit(solution)/shard_map/ppermute | solution.py:132
  53.5 25.8 %collective-permute-start.3 = (bf16[2,1024,128]{2,1,0:T(8,128)(2,1)}, bf16[2,1024,128]{2,1,0:T(8,128)(2,1)S(1)}, u32[]{:S(2)}, u32[]{:S(2)}) collective-permute-start(bf16[2,1024,128]{2,1,0:T(8,128)(2,1)} %bitcast.18), channel_id=1, source_target_pairs={{0,64},{16,80},{32,96},{48,112},{64,0},{80,16},{96,32},{112,48},{1... | collective-permute-start | bytes 1572872 | tf_op jit(solution)/shard_map/ppermute | solution.py:132
  56.0 34.5 %collective-permute-start.4 = (bf16[2,1024,128]{2,1,0:T(8,128)(2,1)}, bf16[2,1024,128]{2,1,0:T(8,128)(2,1)S(1)}, u32[]{:S(2)}, u32[]{:S(2)}) collective-permute-start(bf16[2,1024,128]{2,1,0:T(8,128)(2,1)} %bitcast.18), channel_id=1, source_target_pairs={{0,48},{16,64},{32,80},{48,96},{64,112},{80,0},{96,16},{112,32},{1... | collective-permute-start | bytes 1572872 | tf_op jit(solution)/shard_map/ppermute | solution.py:132
  57.5 44.5 %collective-permute-start.5 = (bf16[2,1024,128]{2,1,0:T(8,128)(2,1)}, bf16[2,1024,128]{2,1,0:T(8,128)(2,1)S(1)}, u32[]{:S(2)}, u32[]{:S(2)}) collective-permute-start(bf16[2,1024,128]{2,1,0:T(8,128)(2,1)} %bitcast.18), channel_id=1, source_target_pairs={{0,32},{16,48},{32,64},{48,80},{64,96},{80,112},{96,0},{112,16},{1... | collective-permute-start | bytes 1572872 | tf_op jit(solution)/shard_map/ppermute | solution.py:132
  67.0 35.0 %collective-permute-start.6 = (bf16[2,1024,128]{2,1,0:T(8,128)(2,1)}, bf16[2,1024,128]{2,1,0:T(8,128)(2,1)S(1)}, u32[]{:S(2)}, u32[]{:S(2)}) collective-permute-start(bf16[2,1024,128]{2,1,0:T(8,128)(2,1)} %bitcast.18), channel_id=1, source_target_pairs={{0,16},{16,32},{32,48},{48,64},{64,80},{80,96},{96,112},{112,0},{1... | collective-permute-start | bytes 1572872 | tf_op jit(solution)/shard_map/ppermute | solution.py:132
  106.3 1.0 copy-start.1
  112.6 19.7 %copy-start.12 = (bf16[2048]{0:T(1024)(128)(2,1)S(1)}, bf16[2048]{0:T(1024)(128)(2,1)}, u32[]{:S(2)}) copy-start(bf16[2048]{0:T(1024)(128)(2,1)} %param.20) | copy-start | bytes 12292
  112.6 19.7 %copy-start.11 = (s32[256,4]{0,1:T(4,128)S(1)}, s32[256,4]{0,1:T(4,128)}, u32[]{:S(2)}) copy-start(s32[256,4]{0,1:T(4,128)} %param.26) | copy-start | bytes 12292
  125.6 29.1 %collective-permute-start.9 = (bf16[256,2048]{1,0:T(8,128)(2,1)}, bf16[256,2048]{1,0:T(8,128)(2,1)}, u32[]{:S(2)}, u32[]{:S(2)}) collective-permute-start(bf16[256,2048]{1,0:T(8,128)(2,1)} %convolution_convert_fusion.1), channel_id=1, source_target_pairs={{0,3},{1,0},{2,1},{3,2},{4,7},{5,4},{6,5},{7,6},{8,11},{9,8},{10,9... | collective-permute-start | bytes 3145736 | tf_op jit(solution)/shard_map/ppermute | solution.py:132
  130.6 25.5 %collective-permute-start.8 = (bf16[256,2048]{1,0:T(8,128)(2,1)}, bf16[256,2048]{1,0:T(8,128)(2,1)}, u32[]{:S(2)}, u32[]{:S(2)}) collective-permute-start(bf16[256,2048]{1,0:T(8,128)(2,1)} %convolution_convert_fusion.1), channel_id=1, source_target_pairs={{0,2},{1,3},{2,0},{3,1},{4,6},{5,7},{6,4},{7,5},{8,10},{9,11},{10,... | collective-permute-start | bytes 3145736 | tf_op jit(solution)/shard_map/ppermute | solution.py:132
  131.4 45.2 %collective-permute-start.7 = (bf16[256,2048]{1,0:T(8,128)(2,1)}, bf16[256,2048]{1,0:T(8,128)(2,1)}, u32[]{:S(2)}, u32[]{:S(2)}) collective-permute-start(bf16[256,2048]{1,0:T(8,128)(2,1)} %convolution_convert_fusion.1), channel_id=1, source_target_pairs={{0,1},{1,2},{2,3},{3,0},{4,5},{5,6},{6,7},{7,4},{8,9},{9,10},{10,1... | collective-permute-start | bytes 3145736 | tf_op jit(solution)/shard_map/ppermute | solution.py:132
  180.9 52.2 %copy-start.3 = (f32[256,2048]{1,0:T(8,128)}, f32[256,2048]{1,0:T(8,128)S(1)}, u32[]{:S(2)}) copy-start(f32[256,2048]{1,0:T(8,128)S(1)} %get-tuple-element.13) | copy-start | bytes 6291460
  181.2 1.2 copy-start.4
  234.8 178.9 %reduce-scatter.3.cloned.1.call-start = ((), (), s32[]{:S(2)}) async-start(), calls=%async_computation.7 | async-start | bytes 10485760 | tf_op jit(solution)/shard_map/reduce_scatter | solution.py:280
  316.8 10.2 %copy-start.14 = (bf16[2,352,2048]{2,1,0:T(8,128)(2,1)S(1)}, bf16[2,352,2048]{2,1,0:T(8,128)(2,1)}, u32[]{:S(2)}) copy-start(bf16[2,352,2048]{2,1,0:T(8,128)(2,1)} %param.25) | copy-start | bytes 8650756
  333.7 92.6 %copy-start.13 = (bf16[2048]{0:T(1024)(128)(2,1)S(1)}, bf16[2048]{0:T(1024)(128)(2,1)}, u32[]{:S(2)}) copy-start(bf16[2048]{0:T(1024)(128)(2,1)} %param.23) | copy-start | bytes 12292
  416.9 38.1 %all-to-all-start.3 = ((bf16[32,2,32,512]{3,2,1,0:T(8,128)(2,1)}), bf16[32,2,32,512]{3,2,1,0:T(8,128)(2,1)}, u32[]{:S(2)}, u32[]{:S(2)}) async-start(bf16[32,2,32,512]{3,2,1,0:T(8,128)(2,1)} %copy.130), calls=%async_computation.4 | async-start | bytes 4194304 | tf_op jit(solution)/shard_map/all_to_all | solution.py:283
  426.1 53.3 %reduce-scatter.5.cloned.1.call-start = ((), (), s32[]{:S(2)}) async-start(), calls=%async_computation.8 | async-start | bytes 1310720 | tf_op jit(solution)/shard_map/reduce_scatter | solution.py:297
  433.0 22.0 %copy-start.15 = (f32[256,4]{0,1:T(4,128)S(1)}, f32[256,4]{0,1:T(4,128)}, u32[]{:S(2)}) copy-start(f32[256,4]{0,1:T(4,128)} %param.27) | copy-start | bytes 12292
  454.9 4.2 copy-start.5
  459.1 1.3 copy-start.8
  459.1 1.3 copy-start.10
Sparse Core Ops, SparseCore 0:
  234.9 81.8 all-gather.1
  333.9 79.7 reduce-scatter.2
  460.5 18.7 reduce-scatter.4

commit v6 on v5

--- a/solution.py
+++ b/solution.py
@@ -270,19 +270,24 @@
         .astype(jnp.bfloat16)
         .reshape(seq_count, slot_local, CAP, col_count)
     )
-    incoming = lax.all_gather(
-        lax.all_to_all(outgoing_part, SEQ, split_axis=0, concat_axis=0, tiled=True),
-        EXP,
-        axis=3,
-        tiled=True,
-    )
-    expert_part = expert_parts(incoming, expert_in, expert_out)
-    summed = lax.psum_scatter(expert_part, EXP, scatter_dimension=3, tiled=True).astype(
-        jnp.float32
-    )
-    returned = lax.all_to_all(
-        summed.astype(jnp.bfloat16), SEQ, split_axis=0, concat_axis=0, tiled=True
-    ).astype(summed.dtype)
+    returned_parts = []
+    for slot_id in range(slot_local):
+        incoming = lax.all_gather(
+            lax.all_to_all(
+                outgoing_part[:, slot_id:slot_id + 1], SEQ, split_axis=0, concat_axis=0, tiled=True
+            ),
+            EXP,
+            axis=3,
+            tiled=True,
+        )
+        expert_part = expert_parts(
+            incoming, expert_in[slot_id:slot_id + 1], expert_out[slot_id:slot_id + 1]
+        )
+        summed = lax.psum_scatter(expert_part, EXP, scatter_dimension=3, tiled=True)
+        returned_parts.append(
+            lax.all_to_all(summed, SEQ, split_axis=0, concat_axis=0, tiled=True)
+        )
+    returned = jnp.concatenate(returned_parts, axis=1)
     select_rows = (slot_place[:, None] == slot_rows[None, :]).astype(jnp.bfloat16)
     picked = jnp.dot(
         select_rows,

time: 489 us -> 495 us (1.012)
  waiting for transfers between devices: 278 us -> 261 us
  blocking collectives: 76.1 us -> 87.8 us
  starting transfers between devices: 28 us -> 36.5 us
    all_to_all x1 -> x2, blocking collectives: 50.8 us -> 62.5 us  [body(): lax.all_to_all(outgoing_part[:, slot_id:slot_id + 1], SEQ, split_axis=0,...]
    all_gather x1 -> x2, waiting for transfers between devices: 82 us -> 70.6 us  [body(): lax.all_gather(lax.all_to_all(outgoing_part[:, slot_id:slot_id + 1], SEQ,...]
    all_to_all x1 -> x2, waiting for transfers between devices: 19.6 us -> 9.09 us  [body(): lax.all_to_all(summed, SEQ, split_axis=0, concat_axis=0, tiled=True)]
    all_to_all x1 -> x2, starting transfers between devices: 9.23 us -> 17.6 us  [body(): lax.all_to_all(summed, SEQ, split_axis=0, concat_axis=0, tiled=True)]
    reduce_scatter x1 -> x2, waiting for transfers between devices: 79.9 us -> 85.2 us  [body(): summed = lax.psum_scatter(expert_part, EXP, scatter_dimension=3, tiled=True)]
    dot_general x1 -> x2, matrix products: 10.1 us -> 12.8 us  [expert_parts(): jnp.einsum('nscd,sgde->nscge', incoming, expert_in, preferred_element_typ...]
    unnamed x53 -> x55, local copies, waits for them, and re-layouts: 16.2 us -> 16.8 us
  transfers between devices with their start and end apart: 14 -> 17, of which waited for: 11 -> 13; matrix products, arithmetic and copies ran while one was open for 5% -> 9% of each run, Pallas kernels for 0% -> 0%
where the time goes in v6:
time: 495 us; the launch traced here: 493 us
  waiting for transfers between devices  261 us (53%)
  blocking collectives  87.8 us (18%)
  matrix products  36.9 us (7%)
  starting transfers between devices  36.5 us (7%)
  local copies, waits for them, and re-layouts  28.1 us (6%)
  other arithmetic  20.8 us (4%)
  between operations  17.1 us (3%)
  Pallas kernels  5.23 us (1%)
    reduce_scatter x2, waiting for transfers between devices, body(): summed = lax.psum_scatter(expert_part, EXP, scatter_dimension=3, tiled=True)  85.2 us
    ppermute x10, waiting for transfers between devices, shifted_copies(): moved.append(lax.ppermute(x, axis_name, pairs))  81.3 us
    all_gather x2, waiting for transfers between devices, body(): lax.all_gather(lax.all_to_all(outgoing_part[:, slot_id:slot_id + 1], SEQ,...  70.6 us
    all_to_all x2, blocking collectives, body(): lax.all_to_all(outgoing_part[:, slot_id:slot_id + 1], SEQ, split_axis=0,...  62.5 us
    ppermute x10, starting transfers between devices, shifted_copies(): moved.append(lax.ppermute(x, axis_name, pairs))  18.5 us
    all_to_all x2, starting transfers between devices, body(): lax.all_to_all(summed, SEQ, split_axis=0, concat_axis=0, tiled=True)  17.6 us
    unnamed x55, local copies, waits for them, and re-layouts  16.8 us
    all_to_all x1, blocking collectives, body(): lax.all_to_all(stacked, 'sl', split_axis=2, concat_axis=1, tiled=True)  16.4 us
  transfers between devices with their start and end apart: 17, of which 13 were waited for; matrix products, arithmetic and copies ran while one was open for 9% of the time, Pallas kernels for 0%

profile of v6, /device:TPU:1, one launch (start us, length us, event | category | flops | bytes accessed | tf_op | source)
XLA Modules:
  0.0 493.2 jit_solution(8735823572404616301)
XLA Ops:
  7.2 1.9 copy.124
  11.9 1.7 convert_reduce_fusion
  15.1 1.2 fusion.43
  17.0 1.9 pad_maximum_fusion.1
  18.9 2.3 copy.125
  21.2 16.4 %all_to_all.50 = bf16[3,256,4,128]{3,1,0,2:T(8,128)(2,1)S(1)} all-to-all(bf16[3,256,4,128]{3,1,0,2:T(8,128)(2,1)} %copy.125), channel_id=1, replica_groups=mesh['sh'=8,'sl'=4,'zl'=2,'co'=2] {'sl'}, dimensions={2} | all-to-all | bytes 1572864 | tf_op jit(solution)/shard_map/all_to_all | solution.py:226
  39.4 5.8 %collective-permute-start = (bf16[2,1024,128]{2,1,0:T(8,128)(2,1)}, bf16[2,1024,128]{2,1,0:T(8,128)(2,1)}, u32[]{:S(2)}, u32[]{:S(2)}) collective-permute-start(bf16[2,1024,128]{2,1,0:T(8,128)(2,1)} %bitcast.18), channel_id=1, source_target_pairs={{0,112},{16,0},{32,16},{48,32},{64,48},{80,64},{96,80},{112,96},{1... | collective-permute-start | bytes 1572872 | tf_op jit(solution)/shard_map/ppermute | solution.py:132
  46.3 1.3 convert_reduce_fusion.2
  53.6 2.5 collective-permute-start.3
  56.1 1.5 collective-permute-start.4
  57.6 1.4 collective-permute-start.5
  60.1 7.0 %collective-permute-done.1 = bf16[2,1024,128]{2,1,0:T(8,128)(2,1)} collective-permute-done((bf16[2,1024,128]{2,1,0:T(8,128)(2,1)}, bf16[2,1024,128]{2,1,0:T(8,128)(2,1)}, u32[]{:S(2)}, u32[]{:S(2)}) %collective-permute-start.1) | collective-permute-done | bytes 524320 | tf_op jit(solution)/shard_map/ppermute | solution.py:132
  68.2 11.0 %collective-permute-done.3 = bf16[2,1024,128]{2,1,0:T(8,128)(2,1)S(1)} collective-permute-done((bf16[2,1024,128]{2,1,0:T(8,128)(2,1)}, bf16[2,1024,128]{2,1,0:T(8,128)(2,1)S(1)}, u32[]{:S(2)}, u32[]{:S(2)}) %collective-permute-start.3) | collective-permute-done | bytes 524320 | tf_op jit(solution)/shard_map/ppermute | solution.py:132
  79.3 11.2 %collective-permute-done.4 = bf16[2,1024,128]{2,1,0:T(8,128)(2,1)S(1)} collective-permute-done((bf16[2,1024,128]{2,1,0:T(8,128)(2,1)}, bf16[2,1024,128]{2,1,0:T(8,128)(2,1)S(1)}, u32[]{:S(2)}, u32[]{:S(2)}) %collective-permute-start.4) | collective-permute-done | bytes 524320 | tf_op jit(solution)/shard_map/ppermute | solution.py:132
  90.5 11.5 %collective-permute-done.5 = bf16[2,1024,128]{2,1,0:T(8,128)(2,1)S(1)} collective-permute-done((bf16[2,1024,128]{2,1,0:T(8,128)(2,1)}, bf16[2,1024,128]{2,1,0:T(8,128)(2,1)S(1)}, u32[]{:S(2)}, u32[]{:S(2)}) %collective-permute-start.5) | collective-permute-done | bytes 524320 | tf_op jit(solution)/shard_map/ppermute | solution.py:132
  107.3 5.2 %shard_map.157 = bf16[1024,128]{1,0:T(8,128)(2,1)S(1)} custom-call(s32[3]{0:T(128)S(1)} %pad_add_fusion.bounds_ref, bf16[1024,128]{1,0:T(8,128)(2,1)S(1)} %bitcast.162, bf16[8192,128]{1,0:T(8,128)(2,1)S(1)} %bitcast.161, bf16[8192,128]{1,0:T(8,128)(2,1)S(1)} %bitcast.160, s32[1024,1]{1,0:T(8,128)S(1)} %copy-done.1, s32[1,8192]{1,0:T(1,128)S(1)} %bitcast.164), custom_call_target="tpu_custom_call" | custom-call | flops 4294967296 | bytes 4718592 | tf_op jit(solution)/shard_map/pallas_call | solution.py:106
  113.4 8.9 %all_to_all.51 = bf16[4,256,1,128]{1,3,2,0:T(8,128)(2,1)S(1)} all-to-all(bf16[4,256,1,128]{1,3,2,0:T(8,128)(2,1)} %copy.128), channel_id=1, replica_groups=mesh['sh'=8,'sl'=4,'zl'=2,'co'=2] {'sl'}, dimensions={0} | all-to-all | bytes 524288 | tf_op jit(solution)/shard_map/all_to_all | solution.py:239
  122.3 3.3 convolution_convert_fusion.1
  125.6 5.1 %collective-permute-start.9 = (bf16[256,2048]{1,0:T(8,128)(2,1)}, bf16[256,2048]{1,0:T(8,128)(2,1)}, u32[]{:S(2)}, u32[]{:S(2)}) collective-permute-start(bf16[256,2048]{1,0:T(8,128)(2,1)} %convolution_convert_fusion.1), channel_id=1, source_target_pairs={{0,3},{1,0},{2,1},{3,2},{4,7},{5,4},{6,5},{7,6},{8,11},{9,8},{10,9... | collective-permute-start | bytes 3145736 | tf_op jit(solution)/shard_map/ppermute | solution.py:132
  133.3 2.6 fusion.3
  136.0 18.8 %collective-permute-done.9 = bf16[256,2048]{1,0:T(8,128)(2,1)} collective-permute-done((bf16[256,2048]{1,0:T(8,128)(2,1)}, bf16[256,2048]{1,0:T(8,128)(2,1)}, u32[]{:S(2)}, u32[]{:S(2)}) %collective-permute-start.9) | collective-permute-done | bytes 1048608 | tf_op jit(solution)/shard_map/ppermute | solution.py:132
  154.8 1.4 collective-permute-done.8
  156.2 20.5 %collective-permute-done.7 = bf16[256,2048]{1,0:T(8,128)(2,1)} collective-permute-done((bf16[256,2048]{1,0:T(8,128)(2,1)}, bf16[256,2048]{1,0:T(8,128)(2,1)}, u32[]{:S(2)}, u32[]{:S(2)}) %collective-permute-start.7) | collective-permute-done | bytes 1048608 | tf_op jit(solution)/shard_map/ppermute | solution.py:132
  176.6 4.4 multiply_reduce_fusion.1
  181.3 1.2 copy-done.4
  183.2 1.2 fusion.50
  184.4 40.3 %all_to_all.52 = bf16[32,1,32,512]{3,2,1,0:T(8,128)(2,1)} all-to-all(bf16[32,1,32,512]{3,2,1,0:T(8,128)(2,1)S(1)} %get-tuple-element.18), channel_id=1, replica_groups=mesh['sh'=8,'sl'=4,'zl'=2,'co'=2] {'sh','sl'}, dimensions={0} | all-to-all | bytes 2097152 | tf_op jit(solution)/shard_map/all_to_all | solution.py:276
  224.8 22.1 %all_to_all.53 = bf16[32,1,32,512]{3,2,1,0:T(8,128)(2,1)} all-to-all(bf16[32,1,32,512]{3,2,1,0:T(8,128)(2,1)} %get-tuple-element.17), channel_id=1, replica_groups=mesh['sh'=8,'sl'=4,'zl'=2,'co'=2] {'sh','sl'}, dimensions={0} | all-to-all | bytes 2097152 | tf_op jit(solution)/shard_map/all_to_all | solution.py:276
  247.0 33.1 %all-gather.5.cloned.1.call-done = bf16[32,1,32,2048]{3,2,0,1:T(8,128)(2,1)} async-done(((bf16[32,1,32,512]{3,2,0,1:T(8,128)(2,1)}), bf16[32,1,32,2048]{3,2,0,1:T(8,128)(2,1)}) %all-gather.5.cloned.1.call-update) | async-done | bytes 4194320 | tf_op jit(solution)/shard_map/all_gather | solution.py:275
  280.1 6.4 %fusion.19 = f32[32,1,32,2,352]{4,2,3,0,1:T(8,128)S(1)} fusion(bf16[2,2,2048,352]{2,3,1,0:T(8,128)(2,1)} %param.24, bf16[32,1,32,2048]{3,2,0,1:T(8,128)(2,1)} %all-gather.5.cloned.1.call-done), kind=kOutput, calls=%fused_computation.31 | convolution fusion | flops 2952790016 | bytes 9961472 | tf_op jit(solution)/shard_map/nscd,sgde->nscge/dot_general | solution.py:184
  286.5 4.4 convert_bitcast_fusion
  291.2 37.6 %all-gather.3.cloned.1.call-done = bf16[32,1,32,2048]{3,2,0,1:T(8,128)(2,1)} async-done(((bf16[32,1,32,512]{3,2,0,1:T(8,128)(2,1)}), bf16[32,1,32,2048]{3,2,0,1:T(8,128)(2,1)}) %all-gather.3.cloned.1.call-update) | async-done | bytes 4194320 | tf_op jit(solution)/shard_map/all_gather | solution.py:275
  328.7 6.4 %fusion.14 = f32[32,1,32,2,352]{4,2,3,0,1:T(8,128)S(1)} fusion(bf16[2,2,2048,352]{2,3,1,0:T(8,128)(2,1)} %param.24, bf16[32,1,32,2048]{3,2,0,1:T(8,128)(2,1)} %all-gather.3.cloned.1.call-done), kind=kOutput, calls=%fused_computation.30 | convolution fusion | flops 2952790016 | bytes 9961472 | tf_op jit(solution)/shard_map/nscd,sgde->nscge/dot_general | solution.py:184
  335.2 4.3 convert_bitcast_fusion.1
  339.5 37.8 %reduce-scatter.6.cloned.1.call-done = bf16[32,1,32,512]{3,2,0,1:T(8,128)(2,1)} async-done(((bf16[32,1,32,2048]{3,2,0,1:T(8,128)(2,1)}), bf16[32,1,32,512]{3,2,0,1:T(8,128)(2,1)}) %reduce-scatter.6.cloned.1.call-update) | async-done | bytes 1048592 | tf_op jit(solution)/shard_map/reduce_scatter | solution.py:286
  377.3 9.2 %all-to-all-start.5 = ((bf16[32,1,32,512]{3,2,1,0:T(8,128)(2,1)}), bf16[32,1,32,512]{3,2,1,0:T(8,128)(2,1)}, u32[]{:S(2)}, u32[]{:S(2)}) async-start(bf16[32,1,32,512]{3,2,1,0:T(8,128)(2,1)} %bitcast.176), calls=%async_computation.7 | async-start | bytes 2097152 | tf_op jit(solution)/shard_map/all_to_all | solution.py:288
  386.6 1.6 fusion.51
  388.2 47.4 %reduce-scatter.4.cloned.1.call-done = bf16[32,1,32,512]{3,2,0,1:T(8,128)(2,1)} async-done(((bf16[32,1,32,2048]{3,2,0,1:T(8,128)(2,1)}), bf16[32,1,32,512]{3,2,0,1:T(8,128)(2,1)}) %reduce-scatter.4.cloned.1.call-update) | async-done | bytes 1048592 | tf_op jit(solution)/shard_map/reduce_scatter | solution.py:286
  435.6 8.4 %all-to-all-start.3 = ((bf16[32,1,32,512]{3,2,1,0:T(8,128)(2,1)}), bf16[32,1,32,512]{3,2,1,0:T(8,128)(2,1)}, u32[]{:S(2)}, u32[]{:S(2)}) async-start(bf16[32,1,32,512]{3,2,1,0:T(8,128)(2,1)} %bitcast.175), calls=%async_computation.4 | async-start | bytes 2097152 | tf_op jit(solution)/shard_map/all_to_all | solution.py:288
  444.0 4.9 fusion.32
  448.9 2.4 convolution_multiply_fusion
  451.3 9.1 %all-to-all-done.3 = bf16[32,1,32,512]{3,2,1,0:T(8,128)(2,1)} async-done(((bf16[32,1,32,512]{3,2,1,0:T(8,128)(2,1)}), bf16[32,1,32,512]{3,2,1,0:T(8,128)(2,1)}, u32[]{:S(2)}, u32[]{:S(2)}) %all-to-all-start.3) | async-done | bytes 1048608 | tf_op jit(solution)/shard_map/all_to_all | solution.py:288
  460.4 1.7 pad_maximum_fusion
  462.2 2.4 multiply_reduce_fusion
  466.6 1.8 copy.135
  468.4 1.7 dynamic-slice_convert_fusion
  470.1 14.7 %reduce-scatter.8.cloned.1.call-done = bf16[64,2048]{1,0:T(8,128)(2,1)} async-done(((bf16[256,2048]{1,0:T(8,128)(2,1)}), bf16[64,2048]{1,0:T(8,128)(2,1)}) %reduce-scatter.8.cloned.1.call-update) | async-done | bytes 262160 | tf_op jit(solution)/shard_map/reduce_scatter | solution.py:302
  484.8 1.9 add_convert_fusion
  (101 shorter events, 25.4 us)
Async XLA Ops:
  7.2 441.7 %copy-start = (bf16[768,2048]{1,0:T(8,128)(2,1)S(1)}, bf16[768,2048]{1,0:T(8,128)(2,1)}, u32[]{:S(2)}) copy-start(bf16[768,2048]{1,0:T(8,128)(2,1)} %param.22) | copy-start | bytes 9437188
  7.2 272.9 %all-gather.5.cloned.1.call-start = ((), (), s32[]{:S(2)}) async-start(), calls=%async_computation.11 | async-start | bytes 5242880 | tf_op jit(solution)/shard_map/all_gather | solution.py:275
  16.3 0.7 copy-start.7
  16.3 0.7 copy-start.9
  18.9 26.3 %copy-start.2 = (s32[8192]{0:T(1024)S(1)}, s32[8192]{0:T(1024)}, u32[]{:S(2)}) copy-start(s32[8192]{0:T(1024)} %param.14) | copy-start | bytes 98308
  37.7 0.9 copy-start.6
  39.4 18.2 %collective-permute-start = (bf16[2,1024,128]{2,1,0:T(8,128)(2,1)}, bf16[2,1024,128]{2,1,0:T(8,128)(2,1)}, u32[]{:S(2)}, u32[]{:S(2)}) collective-permute-start(bf16[2,1024,128]{2,1,0:T(8,128)(2,1)} %bitcast.18), channel_id=1, source_target_pairs={{0,112},{16,0},{32,16},{48,32},{64,48},{80,64},{96,80},{112,96},{1... | collective-permute-start | bytes 1572872 | tf_op jit(solution)/shard_map/ppermute | solution.py:132
  45.7 21.3 %collective-permute-start.1 = (bf16[2,1024,128]{2,1,0:T(8,128)(2,1)}, bf16[2,1024,128]{2,1,0:T(8,128)(2,1)}, u32[]{:S(2)}, u32[]{:S(2)}) collective-permute-start(bf16[2,1024,128]{2,1,0:T(8,128)(2,1)} %bitcast.18), channel_id=1, source_target_pairs={{0,96},{16,112},{32,0},{48,16},{64,32},{80,48},{96,64},{112,80},{1... | collective-permute-start | bytes 1572872 | tf_op jit(solution)/shard_map/ppermute | solution.py:132
  51.5 16.7 %collective-permute-start.2 = (bf16[2,1024,128]{2,1,0:T(8,128)(2,1)}, bf16[2,1024,128]{2,1,0:T(8,128)(2,1)S(1)}, u32[]{:S(2)}, u32[]{:S(2)}) collective-permute-start(bf16[2,1024,128]{2,1,0:T(8,128)(2,1)} %bitcast.18), channel_id=1, source_target_pairs={{0,80},{16,96},{32,112},{48,0},{64,16},{80,32},{96,48},{112,64},{1... | collective-permute-start | bytes 1572872 | tf_op jit(solution)/shard_map/ppermute | solution.py:132
  53.6 25.7 %collective-permute-start.3 = (bf16[2,1024,128]{2,1,0:T(8,128)(2,1)}, bf16[2,1024,128]{2,1,0:T(8,128)(2,1)S(1)}, u32[]{:S(2)}, u32[]{:S(2)}) collective-permute-start(bf16[2,1024,128]{2,1,0:T(8,128)(2,1)} %bitcast.18), channel_id=1, source_target_pairs={{0,64},{16,80},{32,96},{48,112},{64,0},{80,16},{96,32},{112,48},{1... | collective-permute-start | bytes 1572872 | tf_op jit(solution)/shard_map/ppermute | solution.py:132
  56.1 34.4 %collective-permute-start.4 = (bf16[2,1024,128]{2,1,0:T(8,128)(2,1)}, bf16[2,1024,128]{2,1,0:T(8,128)(2,1)S(1)}, u32[]{:S(2)}, u32[]{:S(2)}) collective-permute-start(bf16[2,1024,128]{2,1,0:T(8,128)(2,1)} %bitcast.18), channel_id=1, source_target_pairs={{0,48},{16,64},{32,80},{48,96},{64,112},{80,0},{96,16},{112,32},{1... | collective-permute-start | bytes 1572872 | tf_op jit(solution)/shard_map/ppermute | solution.py:132
  57.6 44.4 %collective-permute-start.5 = (bf16[2,1024,128]{2,1,0:T(8,128)(2,1)}, bf16[2,1024,128]{2,1,0:T(8,128)(2,1)S(1)}, u32[]{:S(2)}, u32[]{:S(2)}) collective-permute-start(bf16[2,1024,128]{2,1,0:T(8,128)(2,1)} %bitcast.18), channel_id=1, source_target_pairs={{0,32},{16,48},{32,64},{48,80},{64,96},{80,112},{96,0},{112,16},{1... | collective-permute-start | bytes 1572872 | tf_op jit(solution)/shard_map/ppermute | solution.py:132
  67.0 35.1 %collective-permute-start.6 = (bf16[2,1024,128]{2,1,0:T(8,128)(2,1)}, bf16[2,1024,128]{2,1,0:T(8,128)(2,1)S(1)}, u32[]{:S(2)}, u32[]{:S(2)}) collective-permute-start(bf16[2,1024,128]{2,1,0:T(8,128)(2,1)} %bitcast.18), channel_id=1, source_target_pairs={{0,16},{16,32},{32,48},{48,64},{64,80},{80,96},{96,112},{112,0},{1... | collective-permute-start | bytes 1572872 | tf_op jit(solution)/shard_map/ppermute | solution.py:132
  106.2 1.0 copy-start.1
  112.5 19.8 %copy-start.12 = (bf16[2048]{0:T(1024)(128)(2,1)S(1)}, bf16[2048]{0:T(1024)(128)(2,1)}, u32[]{:S(2)}) copy-start(bf16[2048]{0:T(1024)(128)(2,1)} %param.20) | copy-start | bytes 12292
  112.5 19.8 %copy-start.11 = (s32[256,4]{0,1:T(4,128)S(1)}, s32[256,4]{0,1:T(4,128)}, u32[]{:S(2)}) copy-start(s32[256,4]{0,1:T(4,128)} %param.26) | copy-start | bytes 12292
  125.6 29.2 %collective-permute-start.9 = (bf16[256,2048]{1,0:T(8,128)(2,1)}, bf16[256,2048]{1,0:T(8,128)(2,1)}, u32[]{:S(2)}, u32[]{:S(2)}) collective-permute-start(bf16[256,2048]{1,0:T(8,128)(2,1)} %convolution_convert_fusion.1), channel_id=1, source_target_pairs={{0,3},{1,0},{2,1},{3,2},{4,7},{5,4},{6,5},{7,6},{8,11},{9,8},{10,9... | collective-permute-start | bytes 3145736 | tf_op jit(solution)/shard_map/ppermute | solution.py:132
  130.7 25.5 %collective-permute-start.8 = (bf16[256,2048]{1,0:T(8,128)(2,1)}, bf16[256,2048]{1,0:T(8,128)(2,1)}, u32[]{:S(2)}, u32[]{:S(2)}) collective-permute-start(bf16[256,2048]{1,0:T(8,128)(2,1)} %convolution_convert_fusion.1), channel_id=1, source_target_pairs={{0,2},{1,3},{2,0},{3,1},{4,6},{5,7},{6,4},{7,5},{8,10},{9,11},{10,... | collective-permute-start | bytes 3145736 | tf_op jit(solution)/shard_map/ppermute | solution.py:132
  131.4 45.2 %collective-permute-start.7 = (bf16[256,2048]{1,0:T(8,128)(2,1)}, bf16[256,2048]{1,0:T(8,128)(2,1)}, u32[]{:S(2)}, u32[]{:S(2)}) collective-permute-start(bf16[256,2048]{1,0:T(8,128)(2,1)} %convolution_convert_fusion.1), channel_id=1, source_target_pairs={{0,1},{1,2},{2,3},{3,0},{4,5},{5,6},{6,7},{7,4},{8,9},{9,10},{10,1... | collective-permute-start | bytes 3145736 | tf_op jit(solution)/shard_map/ppermute | solution.py:132
  181.0 3.4 copy-start.3
  181.2 1.2 copy-start.4
  224.7 104.0 %all-gather.3.cloned.1.call-start = ((), (), s32[]{:S(2)}) async-start(), calls=%async_computation.9 | async-start | bytes 5242880 | tf_op jit(solution)/shard_map/all_gather | solution.py:275
  247.0 130.3 %reduce-scatter.6.cloned.1.call-start = ((), (), s32[]{:S(2)}) async-start(), calls=%async_computation.12 | async-start | bytes 5242880 | tf_op jit(solution)/shard_map/reduce_scatter | solution.py:286
  280.1 6.4 %copy-start.14 = (bf16[2,352,2048]{2,1,0:T(8,128)(2,1)S(1)}, bf16[2,352,2048]{2,1,0:T(8,128)(2,1)}, u32[]{:S(2)}) copy-start(bf16[2,352,2048]{2,1,0:T(8,128)(2,1)} %param.25) | copy-start | bytes 8650756
  290.9 144.6 %reduce-scatter.4.cloned.1.call-start = ((), (), s32[]{:S(2)}) async-start(), calls=%async_computation.10 | async-start | bytes 5242880 | tf_op jit(solution)/shard_map/reduce_scatter | solution.py:286
  328.7 6.4 %copy-start.15 = (bf16[2,352,2048]{2,1,0:T(8,128)(2,1)S(1)}, bf16[2,352,2048]{2,1,0:T(8,128)(2,1)}, u32[]{:S(2)}) copy-start(bf16[2,352,2048]{2,1,0:T(8,128)(2,1)} %param.25) | copy-start | bytes 8650756
  339.5 47.0 %copy-start.13 = (bf16[2048]{0:T(1024)(128)(2,1)S(1)}, bf16[2048]{0:T(1024)(128)(2,1)}, u32[]{:S(2)}) copy-start(bf16[2048]{0:T(1024)(128)(2,1)} %param.23) | copy-start | bytes 12292
  377.3 58.3 %all-to-all-start.5 = ((bf16[32,1,32,512]{3,2,1,0:T(8,128)(2,1)}), bf16[32,1,32,512]{3,2,1,0:T(8,128)(2,1)}, u32[]{:S(2)}, u32[]{:S(2)}) async-start(bf16[32,1,32,512]{3,2,1,0:T(8,128)(2,1)} %bitcast.176), calls=%async_computation.7 | async-start | bytes 2097152 | tf_op jit(solution)/shard_map/all_to_all | solution.py:288
  435.6 24.9 %all-to-all-start.3 = ((bf16[32,1,32,512]{3,2,1,0:T(8,128)(2,1)}), bf16[32,1,32,512]{3,2,1,0:T(8,128)(2,1)}, u32[]{:S(2)}, u32[]{:S(2)}) async-start(bf16[32,1,32,512]{3,2,1,0:T(8,128)(2,1)} %bitcast.175), calls=%async_computation.4 | async-start | bytes 2097152 | tf_op jit(solution)/shard_map/all_to_all | solution.py:288
  443.9 40.9 %reduce-scatter.8.cloned.1.call-start = ((), (), s32[]{:S(2)}) async-start(), calls=%async_computation.13 | async-start | bytes 1310720 | tf_op jit(solution)/shard_map/reduce_scatter | solution.py:302
  451.3 10.8 %copy-start.16 = (f32[256,4]{0,1:T(4,128)S(1)}, f32[256,4]{0,1:T(4,128)}, u32[]{:S(2)}) copy-start(f32[256,4]{0,1:T(4,128)} %param.27) | copy-start | bytes 12292
  462.2 2.4 copy-start.5
  464.6 1.3 copy-start.8
  464.6 1.3 copy-start.10
Sparse Core Ops, SparseCore 0:
  224.9 55.1 all-gather.4
  281.7 46.9 all-gather.2
  331.1 46.0 reduce-scatter.5
  379.5 55.9 reduce-scatter.3
  466.0 18.7 reduce-scatter.7

commit v7 on v5

--- a/solution.py
+++ b/solution.py
@@ -259,8 +259,9 @@
     slot_place = flat_ids * CAP + slot_rank
     slot_local = SLOTS // seq_count
     model_width = normed.shape[1]
-    col_count = model_width // exp_count
-    col_first = exp_place * col_count
+    core_count = lax.axis_size("co")
+    col_count = model_width // core_count
+    col_first = lax.axis_index("co") * col_count
     slot_rows = jnp.arange(SLOTS * CAP, dtype=jnp.int32)
     place_hit = (slot_place[None, :] == slot_rows[:, None]).reshape(SLOTS * CAP, block_len, TOPK)
     dispatch = jnp.any(place_hit, axis=2).astype(jnp.bfloat16)
@@ -272,12 +273,12 @@
     )
     incoming = lax.all_gather(
         lax.all_to_all(outgoing_part, SEQ, split_axis=0, concat_axis=0, tiled=True),
-        EXP,
+        "co",
         axis=3,
         tiled=True,
     )
     expert_part = expert_parts(incoming, expert_in, expert_out)
-    summed = lax.psum_scatter(expert_part, EXP, scatter_dimension=3, tiled=True).astype(
+    summed = lax.psum_scatter(expert_part, "co", scatter_dimension=3, tiled=True).astype(
         jnp.float32
     )
     returned = lax.all_to_all(

time: 489 us -> 437 us (0.89)
  waiting for transfers between devices: 278 us -> 193 us
  blocking collectives: 76.1 us -> 101 us
    all_gather x1, waiting for transfers between devices: 82 us -> 22.3 us  [body(): lax.all_gather(lax.all_to_all(outgoing_part, SEQ, split_axis=0, concat_ax...]
    reduce_scatter x1, waiting for transfers between devices: 79.9 us -> 20.4 us  [body(): lax.psum_scatter(expert_part, 'co', scatter_dimension=3, tiled=True)]
    all_to_all x1, waiting for transfers between devices: 19.6 us -> 51.8 us  [body(): lax.all_to_all(summed.astype(jnp.bfloat16), SEQ, split_axis=0, concat_axi...]
    all_to_all x1, blocking collectives: 50.8 us -> 75.9 us  [body(): lax.all_to_all(outgoing_part, SEQ, split_axis=0, concat_axis=0, tiled=True)]
  transfers between devices with their start and end apart: 14 -> 14, of which waited for: 11 -> 11; matrix products, arithmetic and copies ran while one was open for 5% -> 6% of each run, Pallas kernels for 0% -> 0%
where the time goes in v7:
time: 437 us; the launch traced here: 436 us
  waiting for transfers between devices  193 us (44%)
  blocking collectives  101 us (23%)
  matrix products  37.6 us (9%)
  local copies, waits for them, and re-layouts  34.4 us (8%)
  starting transfers between devices  28.3 us (6%)
  other arithmetic  19.1 us (4%)
  between operations  16.9 us (4%)
  Pallas kernels  5.23 us (1%)
    ppermute x10, waiting for transfers between devices, shifted_copies(): moved.append(lax.ppermute(x, axis_name, pairs))  81.3 us
    all_to_all x1, blocking collectives, body(): lax.all_to_all(outgoing_part, SEQ, split_axis=0, concat_axis=0, tiled=True)  75.9 us
    all_to_all x1, waiting for transfers between devices, body(): lax.all_to_all(summed.astype(jnp.bfloat16), SEQ, split_axis=0, concat_axi...  51.8 us
    all_gather x1, waiting for transfers between devices, body(): lax.all_gather(lax.all_to_all(outgoing_part, SEQ, split_axis=0, concat_ax...  22.3 us
    reduce_scatter x1, waiting for transfers between devices, body(): lax.psum_scatter(expert_part, 'co', scatter_dimension=3, tiled=True)  20.4 us
    ppermute x10, starting transfers between devices, shifted_copies(): moved.append(lax.ppermute(x, axis_name, pairs))  18.4 us
    reduce_scatter x1, waiting for transfers between devices, body(): lax.psum_scatter(combined.astype(jnp.bfloat16), EXP, scatter_dimension=0,...  17.4 us
    unnamed x53, local copies, waits for them, and re-layouts  16.9 us
  transfers between devices with their start and end apart: 14, of which 11 were waited for; matrix products, arithmetic and copies ran while one was open for 6% of the time, Pallas kernels for 0%

profile of v7, /device:TPU:1, one launch (start us, length us, event | category | flops | bytes accessed | tf_op | source)
XLA Modules:
  0.0 436.0 jit_solution(6154760679558342792)
XLA Ops:
  7.2 1.9 copy.121
  11.9 1.7 convert_reduce_fusion
  15.1 1.2 fusion.28
  17.0 1.9 pad_maximum_fusion
  18.9 2.3 copy.122
  21.2 16.4 %all_to_all.40 = bf16[3,256,4,128]{3,1,0,2:T(8,128)(2,1)S(1)} all-to-all(bf16[3,256,4,128]{3,1,0,2:T(8,128)(2,1)} %copy.122), channel_id=1, replica_groups=mesh['sh'=8,'sl'=4,'zl'=2,'co'=2] {'sl'}, dimensions={2} | all-to-all | bytes 1572864 | tf_op jit(solution)/shard_map/all_to_all | solution.py:226
  39.4 5.8 %collective-permute-start = (bf16[2,1024,128]{2,1,0:T(8,128)(2,1)}, bf16[2,1024,128]{2,1,0:T(8,128)(2,1)}, u32[]{:S(2)}, u32[]{:S(2)}) collective-permute-start(bf16[2,1024,128]{2,1,0:T(8,128)(2,1)} %bitcast.18), channel_id=1, source_target_pairs={{0,112},{16,0},{32,16},{48,32},{64,48},{80,64},{96,80},{112,96},{1... | collective-permute-start | bytes 1572872 | tf_op jit(solution)/shard_map/ppermute | solution.py:132
  46.3 1.3 convert_reduce_fusion.2
  53.5 2.5 collective-permute-start.3
  56.0 1.5 collective-permute-start.4
  57.5 1.4 collective-permute-start.5
  59.9 7.1 %collective-permute-done.1 = bf16[2,1024,128]{2,1,0:T(8,128)(2,1)} collective-permute-done((bf16[2,1024,128]{2,1,0:T(8,128)(2,1)}, bf16[2,1024,128]{2,1,0:T(8,128)(2,1)}, u32[]{:S(2)}, u32[]{:S(2)}) %collective-permute-start.1) | collective-permute-done | bytes 524320 | tf_op jit(solution)/shard_map/ppermute | solution.py:132
  67.0 1.1 bitcast_dynamic-update-slice_fusion.10
  68.2 11.0 %collective-permute-done.3 = bf16[2,1024,128]{2,1,0:T(8,128)(2,1)S(1)} collective-permute-done((bf16[2,1024,128]{2,1,0:T(8,128)(2,1)}, bf16[2,1024,128]{2,1,0:T(8,128)(2,1)S(1)}, u32[]{:S(2)}, u32[]{:S(2)}) %collective-permute-start.3) | collective-permute-done | bytes 524320 | tf_op jit(solution)/shard_map/ppermute | solution.py:132
  79.3 11.2 %collective-permute-done.4 = bf16[2,1024,128]{2,1,0:T(8,128)(2,1)S(1)} collective-permute-done((bf16[2,1024,128]{2,1,0:T(8,128)(2,1)}, bf16[2,1024,128]{2,1,0:T(8,128)(2,1)S(1)}, u32[]{:S(2)}, u32[]{:S(2)}) %collective-permute-start.4) | collective-permute-done | bytes 524320 | tf_op jit(solution)/shard_map/ppermute | solution.py:132
  90.5 11.5 %collective-permute-done.5 = bf16[2,1024,128]{2,1,0:T(8,128)(2,1)S(1)} collective-permute-done((bf16[2,1024,128]{2,1,0:T(8,128)(2,1)}, bf16[2,1024,128]{2,1,0:T(8,128)(2,1)S(1)}, u32[]{:S(2)}, u32[]{:S(2)}) %collective-permute-start.5) | collective-permute-done | bytes 524320 | tf_op jit(solution)/shard_map/ppermute | solution.py:132
  102.1 1.1 constant_dynamic-update-slice_fusion
  103.3 1.1 bitcast_dynamic-update-slice_fusion.13
  104.4 1.1 bitcast_dynamic-update-slice_fusion.11
  107.2 5.2 %shard_map.157 = bf16[1024,128]{1,0:T(8,128)(2,1)S(1)} custom-call(s32[3]{0:T(128)S(1)} %pad_add_fusion.bounds_ref, bf16[1024,128]{1,0:T(8,128)(2,1)S(1)} %bitcast.129, bf16[8192,128]{1,0:T(8,128)(2,1)S(1)} %bitcast.128, bf16[8192,128]{1,0:T(8,128)(2,1)S(1)} %bitcast.127, s32[1024,1]{1,0:T(8,128)S(1)} %copy-done.1, s32[1,8192]{1,0:T(1,128)S(1)} %bitcast.131), custom_call_target="tpu_custom_call" | custom-call | flops 4294967296 | bytes 4718592 | tf_op jit(solution)/shard_map/pallas_call | solution.py:106
  113.3 8.9 %all_to_all.41 = bf16[4,256,1,128]{1,3,2,0:T(8,128)(2,1)S(1)} all-to-all(bf16[4,256,1,128]{1,3,2,0:T(8,128)(2,1)} %copy.125), channel_id=1, replica_groups=mesh['sh'=8,'sl'=4,'zl'=2,'co'=2] {'sl'}, dimensions={0} | all-to-all | bytes 524288 | tf_op jit(solution)/shard_map/all_to_all | solution.py:239
  122.2 3.3 convolution_convert_fusion.1
  125.5 5.0 %collective-permute-start.9 = (bf16[256,2048]{1,0:T(8,128)(2,1)}, bf16[256,2048]{1,0:T(8,128)(2,1)}, u32[]{:S(2)}, u32[]{:S(2)}) collective-permute-start(bf16[256,2048]{1,0:T(8,128)(2,1)} %convolution_convert_fusion.1), channel_id=1, source_target_pairs={{0,3},{1,0},{2,1},{3,2},{4,7},{5,4},{6,5},{7,6},{8,11},{9,8},{10,9... | collective-permute-start | bytes 3145736 | tf_op jit(solution)/shard_map/ppermute | solution.py:132
  133.2 2.6 fusion.5
  135.9 18.8 %collective-permute-done.9 = bf16[256,2048]{1,0:T(8,128)(2,1)} collective-permute-done((bf16[256,2048]{1,0:T(8,128)(2,1)}, bf16[256,2048]{1,0:T(8,128)(2,1)}, u32[]{:S(2)}, u32[]{:S(2)}) %collective-permute-start.9) | collective-permute-done | bytes 1048608 | tf_op jit(solution)/shard_map/ppermute | solution.py:132
  154.7 1.4 collective-permute-done.8
  156.1 20.5 %collective-permute-done.7 = bf16[256,2048]{1,0:T(8,128)(2,1)} collective-permute-done((bf16[256,2048]{1,0:T(8,128)(2,1)}, bf16[256,2048]{1,0:T(8,128)(2,1)}, u32[]{:S(2)}, u32[]{:S(2)}) %collective-permute-start.7) | collective-permute-done | bytes 1048608 | tf_op jit(solution)/shard_map/ppermute | solution.py:132
  176.5 4.4 %multiply_reduce_fusion.1 = (f32[256]{0:T(256)S(1)}, f32[256,2048]{1,0:T(8,128)S(1)}, bf16[256,2048]{1,0:T(8,128)(2,1)}) fusion(bf16[256,2048]{1,0:T(8,128)(2,1)} %param.19, bf16[256,2048]{1,0:T(8,128)(2,1)} %collective-permute-done.9, bf16[256,2048]{1,0:T(8,128)(2,1)} %collective-permute-done.8, bf16[256,2048]{1,0:T(8,128)(2,1)} %collective-permute-done.7, ...), kind=kLoop, calls=%fused_computation.26 | loop fusion | flops 6291200 | bytes 8389632 | tf_op jit(solution)/shard_map/reduce_sum | solution.py:177
  180.9 1.3 copy-done.3
  182.5 1.3 convolution_convert_fusion
  183.8 75.9 %all_to_all.42 = bf16[32,2,32,1024]{3,2,1,0:T(8,128)(2,1)S(1)} all-to-all(bf16[32,2,32,1024]{3,2,1,0:T(8,128)(2,1)S(1)} %bitcast.132), channel_id=1, replica_groups=mesh['sh'=8,'sl'=4,'zl'=2,'co'=2] {'sh','sl'}, dimensions={0} | all-to-all | bytes 8388608 | tf_op jit(solution)/shard_map/all_to_all | solution.py:275
  259.7 2.4 copy.128
  262.2 22.3 %all-gather.2.cloned.1.call-done = bf16[32,2,32,2048]{3,2,0,1:T(8,128)(2,1)} async-done(((bf16[32,2,32,1024]{3,2,0,1:T(8,128)(2,1)}), bf16[32,2,32,2048]{3,2,0,1:T(8,128)(2,1)}) %all-gather.2.cloned.1.call-update) | async-done | bytes 8388624 | tf_op jit(solution)/shard_map/all_gather | solution.py:274
  284.5 10.1 %fusion.12 = f32[32,2,32,2,352]{4,2,3,0,1:T(8,128)S(1)} fusion(bf16[2,2,2048,352]{2,3,1,0:T(8,128)(2,1)} %param.24, bf16[32,2,32,2048]{3,2,0,1:T(8,128)(2,1)} %all-gather.2.cloned.1.call-done), kind=kOutput, calls=%fused_computation.23 | convolution fusion | flops 5905580032 | bytes 19922944 | tf_op jit(solution)/shard_map/nscd,sgde->nscge/dot_general | solution.py:184
  294.6 6.7 %convert_bitcast_fusion = bf16[32,2,32,2048]{3,2,0,1:T(8,128)(2,1)} fusion(bf16[2,352,2048]{2,1,0:T(8,128)(2,1)S(1)} %copy-done.14, f32[32,2,32,2,352]{4,2,3,0,1:T(8,128)S(1)} %fusion.12), kind=kOutput, calls=%fused_computation.2 | convolution fusion | flops 2961309696 | bytes 17039360 | tf_op jit(solution)/shard_map/nsce,sed->nscd/dot_general | solution.py:190
  301.4 20.4 %reduce-scatter.3.cloned.1.call-done = bf16[32,2,32,1024]{3,2,0,1:T(8,128)(2,1)} async-done(((bf16[32,2,32,2048]{3,2,0,1:T(8,128)(2,1)}), bf16[32,2,32,1024]{3,2,0,1:T(8,128)(2,1)}) %reduce-scatter.3.cloned.1.call-update) | async-done | bytes 4194320 | tf_op jit(solution)/shard_map/reduce_scatter | solution.py:281
  321.8 5.0 %copy.130 = bf16[32,2,32,1024]{3,2,1,0:T(8,128)(2,1)} copy(bf16[32,2,32,1024]{3,2,0,1:T(8,128)(2,1)} %reduce-scatter.3.cloned.1.call-done) | data formatting | bytes 8388608 | tf_op jit(solution)/shard_map/reduce_scatter | solution.py:281
  326.8 9.8 %all-to-all-start.3 = ((bf16[32,2,32,1024]{3,2,1,0:T(8,128)(2,1)}), bf16[32,2,32,1024]{3,2,1,0:T(8,128)(2,1)}, u32[]{:S(2)}, u32[]{:S(2)}) async-start(bf16[32,2,32,1024]{3,2,1,0:T(8,128)(2,1)} %copy.130), calls=%async_computation.4 | async-start | bytes 8388608 | tf_op jit(solution)/shard_map/all_to_all | solution.py:284
  336.6 1.6 fusion.34
  338.2 4.9 %fusion.21 = f32[256,2,768]{2,0,1:T(8,128)S(1)} fusion(bf16[2,2048,768]{2,1,0:T(8,128)(2,1)} %param.21, bf16[256,2048]{1,0:T(8,128)(2,1)} %copy-done.4), kind=kOutput, calls=%fused_computation.30 | convolution fusion | flops 1610612736 | bytes 8912896 | tf_op jit(solution)/shard_map/td,gde->tge/dot_general | solution.py:251
  343.2 2.4 convolution_multiply_fusion
  345.6 51.8 %all-to-all-done.3 = bf16[32,2,32,1024]{3,2,1,0:T(8,128)(2,1)} async-done(((bf16[32,2,32,1024]{3,2,1,0:T(8,128)(2,1)}), bf16[32,2,32,1024]{3,2,1,0:T(8,128)(2,1)}, u32[]{:S(2)}, u32[]{:S(2)}) %all-to-all-start.3) | async-done | bytes 4194336 | tf_op jit(solution)/shard_map/all_to_all | solution.py:284
  397.5 7.2 %multiply_reduce_fusion = f32[256,1024]{1,0:T(8,128)S(1)} fusion(f32[256,4]{0,1:T(4,128)S(1)} %copy-done.15, bf16[2048,1024,1]{1,0,2:T(8,128)(2,1)} %bitcast.52, s32[256,4]{0,1:T(4,128)S(1)} %multiply_add_fusion), kind=kOutput, calls=%fused_computation.10 | convolution fusion | flops 4298899456 | bytes 5251072 | tf_op jit(solution)/shard_map/dot_general | solution.py:288
  404.9 1.1 convert_element_type.118
  406.8 1.8 copy.131
  408.6 1.7 dynamic-slice_convert_fusion
  410.3 17.4 %reduce-scatter.5.cloned.1.call-done = bf16[64,2048]{1,0:T(8,128)(2,1)} async-done(((bf16[256,2048]{1,0:T(8,128)(2,1)}), bf16[64,2048]{1,0:T(8,128)(2,1)}) %reduce-scatter.5.cloned.1.call-update) | async-done | bytes 262160 | tf_op jit(solution)/shard_map/reduce_scatter | solution.py:298
  427.6 1.9 add_convert_fusion
  (88 shorter events, 18.9 us)
Async XLA Ops:
  7.2 336.0 %copy-start = (bf16[768,2048]{1,0:T(8,128)(2,1)S(1)}, bf16[768,2048]{1,0:T(8,128)(2,1)}, u32[]{:S(2)}) copy-start(bf16[768,2048]{1,0:T(8,128)(2,1)} %param.22) | copy-start | bytes 9437188
  7.2 277.3 %all-gather.2.cloned.1.call-start = ((), (), s32[]{:S(2)}) async-start(), calls=%async_computation.6 | async-start | bytes 12582912 | tf_op jit(solution)/shard_map/all_gather | solution.py:274
  15.1 30.1 %copy-start.2 = (s32[8192]{0:T(1024)S(1)}, s32[8192]{0:T(1024)}, u32[]{:S(2)}) copy-start(s32[8192]{0:T(1024)} %param.14) | copy-start | bytes 98308
  16.3 0.7 copy-start.7
  16.3 0.7 copy-start.9
  37.7 0.9 copy-start.6
  39.4 18.1 %collective-permute-start = (bf16[2,1024,128]{2,1,0:T(8,128)(2,1)}, bf16[2,1024,128]{2,1,0:T(8,128)(2,1)}, u32[]{:S(2)}, u32[]{:S(2)}) collective-permute-start(bf16[2,1024,128]{2,1,0:T(8,128)(2,1)} %bitcast.18), channel_id=1, source_target_pairs={{0,112},{16,0},{32,16},{48,32},{64,48},{80,64},{96,80},{112,96},{1... | collective-permute-start | bytes 1572872 | tf_op jit(solution)/shard_map/ppermute | solution.py:132
  45.7 21.3 %collective-permute-start.1 = (bf16[2,1024,128]{2,1,0:T(8,128)(2,1)}, bf16[2,1024,128]{2,1,0:T(8,128)(2,1)}, u32[]{:S(2)}, u32[]{:S(2)}) collective-permute-start(bf16[2,1024,128]{2,1,0:T(8,128)(2,1)} %bitcast.18), channel_id=1, source_target_pairs={{0,96},{16,112},{32,0},{48,16},{64,32},{80,48},{96,64},{112,80},{1... | collective-permute-start | bytes 1572872 | tf_op jit(solution)/shard_map/ppermute | solution.py:132
  51.4 16.8 %collective-permute-start.2 = (bf16[2,1024,128]{2,1,0:T(8,128)(2,1)}, bf16[2,1024,128]{2,1,0:T(8,128)(2,1)S(1)}, u32[]{:S(2)}, u32[]{:S(2)}) collective-permute-start(bf16[2,1024,128]{2,1,0:T(8,128)(2,1)} %bitcast.18), channel_id=1, source_target_pairs={{0,80},{16,96},{32,112},{48,0},{64,16},{80,32},{96,48},{112,64},{1... | collective-permute-start | bytes 1572872 | tf_op jit(solution)/shard_map/ppermute | solution.py:132
  53.5 25.8 %collective-permute-start.3 = (bf16[2,1024,128]{2,1,0:T(8,128)(2,1)}, bf16[2,1024,128]{2,1,0:T(8,128)(2,1)S(1)}, u32[]{:S(2)}, u32[]{:S(2)}) collective-permute-start(bf16[2,1024,128]{2,1,0:T(8,128)(2,1)} %bitcast.18), channel_id=1, source_target_pairs={{0,64},{16,80},{32,96},{48,112},{64,0},{80,16},{96,32},{112,48},{1... | collective-permute-start | bytes 1572872 | tf_op jit(solution)/shard_map/ppermute | solution.py:132
  56.0 34.5 %collective-permute-start.4 = (bf16[2,1024,128]{2,1,0:T(8,128)(2,1)}, bf16[2,1024,128]{2,1,0:T(8,128)(2,1)S(1)}, u32[]{:S(2)}, u32[]{:S(2)}) collective-permute-start(bf16[2,1024,128]{2,1,0:T(8,128)(2,1)} %bitcast.18), channel_id=1, source_target_pairs={{0,48},{16,64},{32,80},{48,96},{64,112},{80,0},{96,16},{112,32},{1... | collective-permute-start | bytes 1572872 | tf_op jit(solution)/shard_map/ppermute | solution.py:132
  57.5 44.5 %collective-permute-start.5 = (bf16[2,1024,128]{2,1,0:T(8,128)(2,1)}, bf16[2,1024,128]{2,1,0:T(8,128)(2,1)S(1)}, u32[]{:S(2)}, u32[]{:S(2)}) collective-permute-start(bf16[2,1024,128]{2,1,0:T(8,128)(2,1)} %bitcast.18), channel_id=1, source_target_pairs={{0,32},{16,48},{32,64},{48,80},{64,96},{80,112},{96,0},{112,16},{1... | collective-permute-start | bytes 1572872 | tf_op jit(solution)/shard_map/ppermute | solution.py:132
  67.0 35.0 %collective-permute-start.6 = (bf16[2,1024,128]{2,1,0:T(8,128)(2,1)}, bf16[2,1024,128]{2,1,0:T(8,128)(2,1)S(1)}, u32[]{:S(2)}, u32[]{:S(2)}) collective-permute-start(bf16[2,1024,128]{2,1,0:T(8,128)(2,1)} %bitcast.18), channel_id=1, source_target_pairs={{0,16},{16,32},{32,48},{48,64},{64,80},{80,96},{96,112},{112,0},{1... | collective-permute-start | bytes 1572872 | tf_op jit(solution)/shard_map/ppermute | solution.py:132
  106.2 1.0 copy-start.1
  112.5 19.7 %copy-start.12 = (bf16[2048]{0:T(1024)(128)(2,1)S(1)}, bf16[2048]{0:T(1024)(128)(2,1)}, u32[]{:S(2)}) copy-start(bf16[2048]{0:T(1024)(128)(2,1)} %param.20) | copy-start | bytes 12292
  112.5 19.7 %copy-start.11 = (s32[256,4]{0,1:T(4,128)S(1)}, s32[256,4]{0,1:T(4,128)}, u32[]{:S(2)}) copy-start(s32[256,4]{0,1:T(4,128)} %param.26) | copy-start | bytes 12292
  125.5 29.1 %collective-permute-start.9 = (bf16[256,2048]{1,0:T(8,128)(2,1)}, bf16[256,2048]{1,0:T(8,128)(2,1)}, u32[]{:S(2)}, u32[]{:S(2)}) collective-permute-start(bf16[256,2048]{1,0:T(8,128)(2,1)} %convolution_convert_fusion.1), channel_id=1, source_target_pairs={{0,3},{1,0},{2,1},{3,2},{4,7},{5,4},{6,5},{7,6},{8,11},{9,8},{10,9... | collective-permute-start | bytes 3145736 | tf_op jit(solution)/shard_map/ppermute | solution.py:132
  130.6 25.5 %collective-permute-start.8 = (bf16[256,2048]{1,0:T(8,128)(2,1)}, bf16[256,2048]{1,0:T(8,128)(2,1)}, u32[]{:S(2)}, u32[]{:S(2)}) collective-permute-start(bf16[256,2048]{1,0:T(8,128)(2,1)} %convolution_convert_fusion.1), channel_id=1, source_target_pairs={{0,2},{1,3},{2,0},{3,1},{4,6},{5,7},{6,4},{7,5},{8,10},{9,11},{10,... | collective-permute-start | bytes 3145736 | tf_op jit(solution)/shard_map/ppermute | solution.py:132
  131.3 45.2 %collective-permute-start.7 = (bf16[256,2048]{1,0:T(8,128)(2,1)}, bf16[256,2048]{1,0:T(8,128)(2,1)}, u32[]{:S(2)}, u32[]{:S(2)}) collective-permute-start(bf16[256,2048]{1,0:T(8,128)(2,1)} %convolution_convert_fusion.1), channel_id=1, source_target_pairs={{0,1},{1,2},{2,3},{3,0},{4,5},{5,6},{6,7},{7,4},{8,9},{9,10},{10,1... | collective-permute-start | bytes 3145736 | tf_op jit(solution)/shard_map/ppermute | solution.py:132
  180.9 1.3 copy-start.3
  182.5 1.3 copy-start.4
  262.1 59.7 %reduce-scatter.3.cloned.1.call-start = ((), (), s32[]{:S(2)}) async-start(), calls=%async_computation.7 | async-start | bytes 12582912 | tf_op jit(solution)/shard_map/reduce_scatter | solution.py:281
  284.5 10.2 %copy-start.14 = (bf16[2,352,2048]{2,1,0:T(8,128)(2,1)S(1)}, bf16[2,352,2048]{2,1,0:T(8,128)(2,1)}, u32[]{:S(2)}) copy-start(bf16[2,352,2048]{2,1,0:T(8,128)(2,1)} %param.25) | copy-start | bytes 8650756
  326.7 9.8 %copy-start.13 = (bf16[2048]{0:T(1024)(128)(2,1)S(1)}, bf16[2048]{0:T(1024)(128)(2,1)}, u32[]{:S(2)}) copy-start(bf16[2048]{0:T(1024)(128)(2,1)} %param.23) | copy-start | bytes 12292
  326.8 70.7 %all-to-all-start.3 = ((bf16[32,2,32,1024]{3,2,1,0:T(8,128)(2,1)}), bf16[32,2,32,1024]{3,2,1,0:T(8,128)(2,1)}, u32[]{:S(2)}, u32[]{:S(2)}) async-start(bf16[32,2,32,1024]{3,2,1,0:T(8,128)(2,1)} %copy.130), calls=%async_computation.4 | async-start | bytes 8388608 | tf_op jit(solution)/shard_map/all_to_all | solution.py:284
  336.5 91.1 %reduce-scatter.5.cloned.1.call-start = ((), (), s32[]{:S(2)}) async-start(), calls=%async_computation.8 | async-start | bytes 1310720 | tf_op jit(solution)/shard_map/reduce_scatter | solution.py:298
  343.2 54.3 %copy-start.15 = (f32[256,4]{0,1:T(4,128)S(1)}, f32[256,4]{0,1:T(4,128)}, u32[]{:S(2)}) copy-start(f32[256,4]{0,1:T(4,128)} %param.27) | copy-start | bytes 12292
  397.5 7.2 %copy-start.5 = (f32[256,2048]{1,0:T(8,128)S(1)}, f32[256,2048]{1,0:T(8,128)}, u32[]{:S(2)}) copy-start(f32[256,2048]{1,0:T(8,128)} %convolution_multiply_fusion) | copy-start | bytes 6291460
  404.7 1.4 copy-start.8
  404.7 1.4 copy-start.10
Sparse Core Ops, SparseCore 0:
  262.2 22.1 all-gather.1
  301.5 20.2 reduce-scatter.2
  406.2 21.3 reduce-scatter.4

commit v8 on v7

--- a/solution.py
+++ b/solution.py
@@ -9,6 +9,7 @@
 
 HD = 128
 HEADS = 16
+MOST = 6144
 TOPK = 4
 SLOTS = 64
 CAP = 32
@@ -140,8 +141,32 @@
     return total
 
 
-def gather_by_permutes(x, axis_name, count, place):
-    moved = shifted_copies(x, axis_name, count)
+def causal_copies(x, axis_name, count, reach):
+    moved = [x]
+    for shift in range(1, count):
+        pairs = [(i, i + shift) for i in range(count - shift)] if shift <= reach else []
+        moved.append(lax.ppermute(x, axis_name, pairs) if pairs else jnp.zeros_like(x))
+    return moved
+
+
+def sum_over_chip_pairs(x):
+    half = x.shape[1] // 2
+    core = lax.axis_index("co")
+    swap = [(0, 1), (1, 0)]
+    pair = x.astype(jnp.float32) + lax.ppermute(x, "co", swap).astype(jnp.float32)
+    mine = lax.dynamic_slice_in_dim(pair, core * half, half, 1).astype(jnp.bfloat16)
+    done = (mine.astype(jnp.float32) + lax.ppermute(mine, "zl", swap).astype(jnp.float32)).astype(
+        jnp.bfloat16
+    )
+    other = lax.ppermute(done, "co", swap)
+    whole = jnp.where(
+        core == 0, jnp.concatenate([done, other], axis=1), jnp.concatenate([other, done], axis=1)
+    )
+    return whole.astype(jnp.float32)
+
+
+def gather_by_permutes(x, axis_name, count, place, reach):
+    moved = causal_copies(x, axis_name, count, reach)
     reverse = jnp.stack([moved[0]] + moved[1:][::-1])
     return jnp.roll(reverse, place, axis=0)
 
@@ -228,7 +253,8 @@
     head_q = moved[0].reshape(span, HD)
     head_kv = moved[1:].reshape(2, span, HD)
     group_count = lax.axis_size("sh")
-    gathered = gather_by_permutes(head_kv, "sh", group_count, group_place)
+    reach = -(-(MOST + span - 1) // span) - 1
+    gathered = gather_by_permutes(head_kv, "sh", group_count, group_place, reach)
     gathered = jnp.moveaxis(gathered, 0, 1).reshape(2, group_count * span, HD)
     span_first = group_place * span
     span_seg = lax.dynamic_slice_in_dim(segment_ids, span_first, span, 0)
@@ -243,7 +269,7 @@
     row_count = block_len // exp_count
     row_first = exp_place * row_count
     residual_f = residual.astype(jnp.float32)
-    attn_sum = sum_by_permutes(attn_part.astype(jnp.bfloat16), EXP, exp_count)
+    attn_sum = sum_over_chip_pairs(attn_part.astype(jnp.bfloat16))
     after_attn = residual_f + attn_sum
     normed = rms_norm(after_attn, norm_gain)
     attn_rows = lax.dynamic_slice_in_dim(attn_sum, row_first, row_count, 0).astype(jnp.bfloat16)

time: 437 us -> 414 us (0.947)
  waiting for transfers between devices: 193 us -> 145 us
  starting transfers between devices: 28.3 us -> 43.9 us
  blocking collectives: 101 us -> 107 us
  other arithmetic: 19.1 us -> 23.5 us
    ppermute x10 -> x9, waiting for transfers between devices: 81.3 us -> 34.2 us  [the longest x6 19.2 us: causal_copies(): lax.ppermute(x, axis_name, pairs)]
    ppermute x10 -> x9, starting transfers between devices: 18.4 us -> 33.9 us  [the longest x6 28.1 us: causal_copies(): lax.ppermute(x, axis_name, pairs)]
    convert_element_type x0 -> x3, other arithmetic: none -> 6.37 us  [the longest x1 2.23 us: sum_over_chip_pairs(): (mine.astype(jnp.float32) + lax.ppermute(mine, 'zl', swap).astype(jnp.flo...]
    all_to_all x1, blocking collectives: 75.9 us -> 82.2 us  [body(): lax.all_to_all(outgoing_part, SEQ, split_axis=0, concat_axis=0, tiled=True)]
  transfers between devices with their start and end apart: 14 -> 13, of which waited for: 11 -> 8; matrix products, arithmetic and copies ran while one was open for 6% -> 6% of each run, Pallas kernels for 0% -> 0%
where the time goes in v8:
time: 414 us; the launch traced here: 413 us
  waiting for transfers between devices  145 us (35%)
  blocking collectives  107 us (26%)
  starting transfers between devices  43.9 us (11%)
  matrix products  37.6 us (9%)
  local copies, waits for them, and re-layouts  33.6 us (8%)
  other arithmetic  23.5 us (6%)
  between operations  16.8 us (4%)
  Pallas kernels  5.23 us (1%)
    all_to_all x1, blocking collectives, body(): lax.all_to_all(outgoing_part, SEQ, split_axis=0, concat_axis=0, tiled=True)  82.2 us
    all_to_all x1, waiting for transfers between devices, body(): lax.all_to_all(summed.astype(jnp.bfloat16), SEQ, split_axis=0, concat_axi...  51.8 us
    ppermute x6, starting transfers between devices, causal_copies(): lax.ppermute(x, axis_name, pairs)  28.1 us
    all_gather x1, waiting for transfers between devices, body(): lax.all_gather(lax.all_to_all(outgoing_part, SEQ, split_axis=0, concat_ax...  22.7 us
    reduce_scatter x1, waiting for transfers between devices, body(): lax.psum_scatter(expert_part, 'co', scatter_dimension=3, tiled=True)  20.4 us
    ppermute x6, waiting for transfers between devices, causal_copies(): lax.ppermute(x, axis_name, pairs)  19.2 us
    unnamed x53, local copies, waits for them, and re-layouts  17 us
    all_to_all x1, blocking collectives, body(): lax.all_to_all(stacked, 'sl', split_axis=2, concat_axis=1, tiled=True)  16.4 us
  transfers between devices with their start and end apart: 13, of which 8 were waited for; matrix products, arithmetic and copies ran while one was open for 6% of the time, Pallas kernels for 0%

profile of v8, /device:TPU:1, one launch (start us, length us, event | category | flops | bytes accessed | tf_op | source)
XLA Modules:
  0.0 413.4 jit_solution(6422812360183647660)
XLA Ops:
  7.2 1.9 copy.115
  11.9 1.7 convert_reduce_fusion
  15.1 1.2 fusion.29
  17.0 1.9 pad_maximum_fusion
  18.9 2.3 copy.116
  21.2 16.4 %all_to_all.40 = bf16[3,256,4,128]{3,1,0,2:T(8,128)(2,1)S(1)} all-to-all(bf16[3,256,4,128]{3,1,0,2:T(8,128)(2,1)} %copy.116), channel_id=1, replica_groups=mesh['sh'=8,'sl'=4,'zl'=2,'co'=2] {'sl'}, dimensions={2} | all-to-all | bytes 1572864 | tf_op jit(solution)/shard_map/all_to_all | solution.py:251
  39.4 5.2 %collective-permute-start = (bf16[2,1024,128]{2,1,0:T(8,128)(2,1)}, bf16[2,1024,128]{2,1,0:T(8,128)(2,1)}, u32[]{:S(2)}, u32[]{:S(2)}) collective-permute-start(bf16[2,1024,128]{2,1,0:T(8,128)(2,1)} %bitcast.18), channel_id=1, source_target_pairs={{0,96},{16,112},{1,97},{17,113},{2,98},{18,114},{3,99},{19,115},{4... | collective-permute-start | bytes 1572872 | tf_op jit(solution)/shard_map/ppermute | solution.py:148
  45.2 1.3 convert_reduce_fusion.2
  48.9 5.0 %collective-permute-start.1 = (bf16[2,1024,128]{2,1,0:T(8,128)(2,1)}, bf16[2,1024,128]{2,1,0:T(8,128)(2,1)}, u32[]{:S(2)}, u32[]{:S(2)}) collective-permute-start(bf16[2,1024,128]{2,1,0:T(8,128)(2,1)} %bitcast.18), channel_id=1, source_target_pairs={{0,80},{16,96},{32,112},{1,81},{17,97},{33,113},{2,82},{18,98},{34... | collective-permute-start | bytes 1572872 | tf_op jit(solution)/shard_map/ppermute | solution.py:148
  55.1 1.3 collective-permute-start.2
  58.6 1.3 collective-permute-start.3
  59.9 2.1 collective-permute-start.4
  62.0 13.1 %collective-permute-start.5 = (bf16[2,1024,128]{2,1,0:T(8,128)(2,1)}, bf16[2,1024,128]{2,1,0:T(8,128)(2,1)S(1)}, u32[]{:S(2)}, u32[]{:S(2)}) collective-permute-start(bf16[2,1024,128]{2,1,0:T(8,128)(2,1)} %bitcast.18), channel_id=1, source_target_pairs={{0,16},{16,32},{32,48},{48,64},{64,80},{80,96},{96,112},{1,17},{17... | collective-permute-start | bytes 1572872 | tf_op jit(solution)/shard_map/ppermute | solution.py:148
  75.1 1.1 bitcast_dynamic-update-slice_fusion.10
  76.3 1.1 bitcast_dynamic-update-slice_fusion.8
  77.5 8.0 %collective-permute-done.3 = bf16[2,1024,128]{2,1,0:T(8,128)(2,1)S(1)} collective-permute-done((bf16[2,1024,128]{2,1,0:T(8,128)(2,1)}, bf16[2,1024,128]{2,1,0:T(8,128)(2,1)S(1)}, u32[]{:S(2)}, u32[]{:S(2)}) %collective-permute-start.3) | collective-permute-done | bytes 524320 | tf_op jit(solution)/shard_map/ppermute | solution.py:148
  85.5 11.2 %collective-permute-done.4 = bf16[2,1024,128]{2,1,0:T(8,128)(2,1)S(1)} collective-permute-done((bf16[2,1024,128]{2,1,0:T(8,128)(2,1)}, bf16[2,1024,128]{2,1,0:T(8,128)(2,1)S(1)}, u32[]{:S(2)}, u32[]{:S(2)}) %collective-permute-start.4) | collective-permute-done | bytes 524320 | tf_op jit(solution)/shard_map/ppermute | solution.py:148
  102.0 5.2 %shard_map.157 = bf16[1024,128]{1,0:T(8,128)(2,1)S(1)} custom-call(s32[3]{0:T(128)S(1)} %pad_add_fusion.bounds_ref, bf16[1024,128]{1,0:T(8,128)(2,1)S(1)} %bitcast.126, bf16[8192,128]{1,0:T(8,128)(2,1)S(1)} %bitcast.125, bf16[8192,128]{1,0:T(8,128)(2,1)S(1)} %bitcast.124, s32[1024,1]{1,0:T(8,128)S(1)} %copy-done.1, s32[1,8192]{1,0:T(1,128)S(1)} %bitcast.128), custom_call_target="tpu_custom_call" | custom-call | flops 4294967296 | bytes 4718592 | tf_op jit(solution)/shard_map/pallas_call | solution.py:107
  108.1 8.9 %all_to_all.41 = bf16[4,256,1,128]{1,3,2,0:T(8,128)(2,1)S(1)} all-to-all(bf16[4,256,1,128]{1,3,2,0:T(8,128)(2,1)} %copy.119), channel_id=1, replica_groups=mesh['sh'=8,'sl'=4,'zl'=2,'co'=2] {'sl'}, dimensions={0} | all-to-all | bytes 524288 | tf_op jit(solution)/shard_map/all_to_all | solution.py:265
  117.0 3.3 convolution_convert_fusion.1
  120.3 3.8 collective-permute-start.6
  124.1 2.6 collective-permute-done.6
  126.7 2.2 add_convert_fusion.1
  129.9 12.4 %collective-permute-done.7 = bf16[256,1024]{1,0:T(8,128)(2,1)} collective-permute-done((bf16[256,1024]{1,0:T(8,128)(2,1)}, bf16[256,1024]{1,0:T(8,128)(2,1)}, u32[]{:S(2)}, u32[]{:S(2)}) %collective-permute-start.7) | collective-permute-done | bytes 524320 | tf_op jit(solution)/shard_map/ppermute | solution.py:158
  142.4 2.2 add_convert_fusion
  144.6 1.2 collective-permute-start.8
  146.6 2.6 fusion.5
  149.3 2.4 multiply_reduce_fusion.1
  151.7 1.3 copy-done.3
  153.3 1.3 convolution_convert_fusion
  154.6 82.2 %all_to_all.42 = bf16[32,2,32,1024]{3,2,1,0:T(8,128)(2,1)S(1)} all-to-all(bf16[32,2,32,1024]{3,2,1,0:T(8,128)(2,1)S(1)} %bitcast.129), channel_id=1, replica_groups=mesh['sh'=8,'sl'=4,'zl'=2,'co'=2] {'sh','sl'}, dimensions={0} | all-to-all | bytes 8388608 | tf_op jit(solution)/shard_map/all_to_all | solution.py:301
  236.7 2.4 copy.122
  239.2 22.7 %all-gather.2.cloned.1.call-done = bf16[32,2,32,2048]{3,2,0,1:T(8,128)(2,1)} async-done(((bf16[32,2,32,1024]{3,2,0,1:T(8,128)(2,1)}), bf16[32,2,32,2048]{3,2,0,1:T(8,128)(2,1)}) %all-gather.2.cloned.1.call-update) | async-done | bytes 8388624 | tf_op jit(solution)/shard_map/all_gather | solution.py:300
  261.9 10.1 %fusion.12 = f32[32,2,32,2,352]{4,2,3,0,1:T(8,128)S(1)} fusion(bf16[2,2,2048,352]{2,3,1,0:T(8,128)(2,1)} %param.24, bf16[32,2,32,2048]{3,2,0,1:T(8,128)(2,1)} %all-gather.2.cloned.1.call-done), kind=kOutput, calls=%fused_computation.23 | convolution fusion | flops 5905580032 | bytes 19922944 | tf_op jit(solution)/shard_map/nscd,sgde->nscge/dot_general | solution.py:209
  272.1 6.7 %convert_bitcast_fusion = bf16[32,2,32,2048]{3,2,0,1:T(8,128)(2,1)} fusion(bf16[2,352,2048]{2,1,0:T(8,128)(2,1)S(1)} %copy-done.14, f32[32,2,32,2,352]{4,2,3,0,1:T(8,128)S(1)} %fusion.12), kind=kOutput, calls=%fused_computation.2 | convolution fusion | flops 2961309696 | bytes 17039360 | tf_op jit(solution)/shard_map/nsce,sed->nscd/dot_general | solution.py:215
  278.8 20.4 %reduce-scatter.3.cloned.1.call-done = bf16[32,2,32,1024]{3,2,0,1:T(8,128)(2,1)} async-done(((bf16[32,2,32,2048]{3,2,0,1:T(8,128)(2,1)}), bf16[32,2,32,1024]{3,2,0,1:T(8,128)(2,1)}) %reduce-scatter.3.cloned.1.call-update) | async-done | bytes 4194320 | tf_op jit(solution)/shard_map/reduce_scatter | solution.py:307
  299.2 5.0 %copy.124 = bf16[32,2,32,1024]{3,2,1,0:T(8,128)(2,1)} copy(bf16[32,2,32,1024]{3,2,0,1:T(8,128)(2,1)} %reduce-scatter.3.cloned.1.call-done) | data formatting | bytes 8388608 | tf_op jit(solution)/shard_map/reduce_scatter | solution.py:307
  304.2 9.7 %all-to-all-start.3 = ((bf16[32,2,32,1024]{3,2,1,0:T(8,128)(2,1)}), bf16[32,2,32,1024]{3,2,1,0:T(8,128)(2,1)}, u32[]{:S(2)}, u32[]{:S(2)}) async-start(bf16[32,2,32,1024]{3,2,1,0:T(8,128)(2,1)} %copy.124), calls=%async_computation.4 | async-start | bytes 8388608 | tf_op jit(solution)/shard_map/all_to_all | solution.py:310
  314.2 1.6 fusion.35
  315.8 4.9 %fusion.22 = f32[256,2,768]{2,0,1:T(8,128)S(1)} fusion(bf16[2,2048,768]{2,1,0:T(8,128)(2,1)} %param.21, bf16[256,2048]{1,0:T(8,128)(2,1)} %copy-done.4), kind=kOutput, calls=%fused_computation.31 | convolution fusion | flops 1610612736 | bytes 8912896 | tf_op jit(solution)/shard_map/td,gde->tge/dot_general | solution.py:277
  320.8 2.4 convolution_multiply_fusion
  323.2 51.8 %all-to-all-done.3 = bf16[32,2,32,1024]{3,2,1,0:T(8,128)(2,1)} async-done(((bf16[32,2,32,1024]{3,2,1,0:T(8,128)(2,1)}), bf16[32,2,32,1024]{3,2,1,0:T(8,128)(2,1)}, u32[]{:S(2)}, u32[]{:S(2)}) %all-to-all-start.3) | async-done | bytes 4194336 | tf_op jit(solution)/shard_map/all_to_all | solution.py:310
  375.1 7.2 %multiply_reduce_fusion = f32[256,1024]{1,0:T(8,128)S(1)} fusion(f32[256,4]{0,1:T(4,128)S(1)} %copy-done.15, bf16[2048,1024,1]{1,0,2:T(8,128)(2,1)} %bitcast.51, s32[256,4]{0,1:T(4,128)S(1)} %multiply_add_fusion), kind=kOutput, calls=%fused_computation.10 | convolution fusion | flops 4298899456 | bytes 5251072 | tf_op jit(solution)/shard_map/dot_general | solution.py:314
  382.5 1.1 convert_element_type.130
  384.4 1.8 copy.125
  386.2 1.9 fusion.21
  388.9 16.2 %reduce-scatter.5.cloned.1.call-done = bf16[64,2048]{1,0:T(8,128)(2,1)} async-done(((bf16[256,2048]{1,0:T(8,128)(2,1)}), bf16[64,2048]{1,0:T(8,128)(2,1)}) %reduce-scatter.5.cloned.1.call-update) | async-done | bytes 262160 | tf_op jit(solution)/shard_map/reduce_scatter | solution.py:324
  405.0 1.9 add_convert_fusion.2
  (89 shorter events, 20.7 us)
Async XLA Ops:
  7.2 313.6 %copy-start = (bf16[768,2048]{1,0:T(8,128)(2,1)S(1)}, bf16[768,2048]{1,0:T(8,128)(2,1)}, u32[]{:S(2)}) copy-start(bf16[768,2048]{1,0:T(8,128)(2,1)} %param.22) | copy-start | bytes 9437188
  7.2 254.7 %all-gather.2.cloned.1.call-start = ((), (), s32[]{:S(2)}) async-start(), calls=%async_computation.6 | async-start | bytes 12582912 | tf_op jit(solution)/shard_map/all_gather | solution.py:300
  15.1 29.6 %copy-start.2 = (s32[8192]{0:T(1024)S(1)}, s32[8192]{0:T(1024)}, u32[]{:S(2)}) copy-start(s32[8192]{0:T(1024)} %param.14) | copy-start | bytes 98308
  16.3 0.7 copy-start.7
  16.3 0.7 copy-start.9
  37.7 0.9 copy-start.6
  39.4 22.6 %collective-permute-start = (bf16[2,1024,128]{2,1,0:T(8,128)(2,1)}, bf16[2,1024,128]{2,1,0:T(8,128)(2,1)}, u32[]{:S(2)}, u32[]{:S(2)}) collective-permute-start(bf16[2,1024,128]{2,1,0:T(8,128)(2,1)} %bitcast.18), channel_id=1, source_target_pairs={{0,96},{16,112},{1,97},{17,113},{2,98},{18,114},{3,99},{19,115},{4... | collective-permute-start | bytes 1572872 | tf_op jit(solution)/shard_map/ppermute | solution.py:148
  48.9 27.3 %collective-permute-start.1 = (bf16[2,1024,128]{2,1,0:T(8,128)(2,1)}, bf16[2,1024,128]{2,1,0:T(8,128)(2,1)}, u32[]{:S(2)}, u32[]{:S(2)}) collective-permute-start(bf16[2,1024,128]{2,1,0:T(8,128)(2,1)} %bitcast.18), channel_id=1, source_target_pairs={{0,80},{16,96},{32,112},{1,81},{17,97},{33,113},{2,82},{18,98},{34... | collective-permute-start | bytes 1572872 | tf_op jit(solution)/shard_map/ppermute | solution.py:148
  55.1 22.3 %collective-permute-start.2 = (bf16[2,1024,128]{2,1,0:T(8,128)(2,1)}, bf16[2,1024,128]{2,1,0:T(8,128)(2,1)S(1)}, u32[]{:S(2)}, u32[]{:S(2)}) collective-permute-start(bf16[2,1024,128]{2,1,0:T(8,128)(2,1)} %bitcast.18), channel_id=1, source_target_pairs={{0,64},{16,80},{32,96},{48,112},{1,65},{17,81},{33,97},{49,113},{2... | collective-permute-start | bytes 1572872 | tf_op jit(solution)/shard_map/ppermute | solution.py:148
  58.6 26.9 %collective-permute-start.3 = (bf16[2,1024,128]{2,1,0:T(8,128)(2,1)}, bf16[2,1024,128]{2,1,0:T(8,128)(2,1)S(1)}, u32[]{:S(2)}, u32[]{:S(2)}) collective-permute-start(bf16[2,1024,128]{2,1,0:T(8,128)(2,1)} %bitcast.18), channel_id=1, source_target_pairs={{0,48},{16,64},{32,80},{48,96},{64,112},{1,49},{17,65},{33,81},{49... | collective-permute-start | bytes 1572872 | tf_op jit(solution)/shard_map/ppermute | solution.py:148
  59.9 36.8 %collective-permute-start.4 = (bf16[2,1024,128]{2,1,0:T(8,128)(2,1)}, bf16[2,1024,128]{2,1,0:T(8,128)(2,1)S(1)}, u32[]{:S(2)}, u32[]{:S(2)}) collective-permute-start(bf16[2,1024,128]{2,1,0:T(8,128)(2,1)} %bitcast.18), channel_id=1, source_target_pairs={{0,32},{16,48},{32,64},{48,80},{64,96},{80,112},{1,33},{17,49},{33... | collective-permute-start | bytes 1572872 | tf_op jit(solution)/shard_map/ppermute | solution.py:148
  62.0 34.8 %collective-permute-start.5 = (bf16[2,1024,128]{2,1,0:T(8,128)(2,1)}, bf16[2,1024,128]{2,1,0:T(8,128)(2,1)S(1)}, u32[]{:S(2)}, u32[]{:S(2)}) collective-permute-start(bf16[2,1024,128]{2,1,0:T(8,128)(2,1)} %bitcast.18), channel_id=1, source_target_pairs={{0,16},{16,32},{32,48},{48,64},{64,80},{80,96},{96,112},{1,17},{17... | collective-permute-start | bytes 1572872 | tf_op jit(solution)/shard_map/ppermute | solution.py:148
  100.9 1.0 copy-start.1
  107.2 22.5 %copy-start.11 = (s32[256,4]{0,1:T(4,128)S(1)}, s32[256,4]{0,1:T(4,128)}, u32[]{:S(2)}) copy-start(s32[256,4]{0,1:T(4,128)} %param.26) | copy-start | bytes 12292
  107.2 39.1 %copy-start.12 = (bf16[2048]{0:T(1024)(128)(2,1)S(1)}, bf16[2048]{0:T(1024)(128)(2,1)}, u32[]{:S(2)}) copy-start(bf16[2048]{0:T(1024)(128)(2,1)} %param.20) | copy-start | bytes 12292
  120.3 6.4 %collective-permute-start.6 = (bf16[256,2048]{1,0:T(8,128)(2,1)}, bf16[256,2048]{1,0:T(8,128)(2,1)}, u32[]{:S(2)}, u32[]{:S(2)}) collective-permute-start(bf16[256,2048]{1,0:T(8,128)(2,1)} %convolution_convert_fusion.1), channel_id=1, source_target_pairs={{0,1},{1,0},{2,3},{3,2},{4,5},{5,4},{6,7},{7,6},{8,9},{9,8},{10,11... | collective-permute-start | bytes 3145736 | tf_op jit(solution)/shard_map/ppermute | solution.py:156
  128.9 13.4 %collective-permute-start.7 = (bf16[256,1024]{1,0:T(8,128)(2,1)}, bf16[256,1024]{1,0:T(8,128)(2,1)}, u32[]{:S(2)}, u32[]{:S(2)}) collective-permute-start(bf16[256,1024]{1,0:T(8,128)(2,1)} %add_convert_fusion.1), channel_id=1, source_target_pairs={{0,2},{2,0},{1,3},{3,1},{4,6},{6,4},{5,7},{7,5},{8,10},{10,8},{9,1... | collective-permute-start | bytes 1572872 | tf_op jit(solution)/shard_map/ppermute | solution.py:158
  144.6 4.7 %collective-permute-start.8 = (bf16[256,1024]{1,0:T(8,128)(2,1)}, bf16[256,1024]{1,0:T(8,128)(2,1)}, u32[]{:S(2)}, u32[]{:S(2)}) collective-permute-start(bf16[256,1024]{1,0:T(8,128)(2,1)} %add_convert_fusion), channel_id=1, source_target_pairs={{0,1},{1,0},{2,3},{3,2},{4,5},{5,4},{6,7},{7,6},{8,9},{9,8},{10,11... | collective-permute-start | bytes 1572872 | tf_op jit(solution)/shard_map/ppermute | solution.py:161
  151.7 1.4 copy-start.3
  153.3 1.3 copy-start.4
  239.2 60.1 %reduce-scatter.3.cloned.1.call-start = ((), (), s32[]{:S(2)}) async-start(), calls=%async_computation.7 | async-start | bytes 12582912 | tf_op jit(solution)/shard_map/reduce_scatter | solution.py:307
  261.9 10.2 %copy-start.14 = (bf16[2,352,2048]{2,1,0:T(8,128)(2,1)S(1)}, bf16[2,352,2048]{2,1,0:T(8,128)(2,1)}, u32[]{:S(2)}) copy-start(bf16[2,352,2048]{2,1,0:T(8,128)(2,1)} %param.25) | copy-start | bytes 8650756
  304.2 10.0 %copy-start.13 = (bf16[2048]{0:T(1024)(128)(2,1)S(1)}, bf16[2048]{0:T(1024)(128)(2,1)}, u32[]{:S(2)}) copy-start(bf16[2048]{0:T(1024)(128)(2,1)} %param.23) | copy-start | bytes 12292
  304.2 70.9 %all-to-all-start.3 = ((bf16[32,2,32,1024]{3,2,1,0:T(8,128)(2,1)}), bf16[32,2,32,1024]{3,2,1,0:T(8,128)(2,1)}, u32[]{:S(2)}, u32[]{:S(2)}) async-start(bf16[32,2,32,1024]{3,2,1,0:T(8,128)(2,1)} %copy.124), calls=%async_computation.4 | async-start | bytes 8388608 | tf_op jit(solution)/shard_map/all_to_all | solution.py:310
  313.9 91.1 %reduce-scatter.5.cloned.1.call-start = ((), (), s32[]{:S(2)}) async-start(), calls=%async_computation.8 | async-start | bytes 1310720 | tf_op jit(solution)/shard_map/reduce_scatter | solution.py:324
  320.8 54.3 %copy-start.15 = (f32[256,4]{0,1:T(4,128)S(1)}, f32[256,4]{0,1:T(4,128)}, u32[]{:S(2)}) copy-start(f32[256,4]{0,1:T(4,128)} %param.27) | copy-start | bytes 12292
  375.1 7.2 %copy-start.5 = (f32[256,2048]{1,0:T(8,128)S(1)}, f32[256,2048]{1,0:T(8,128)}, u32[]{:S(2)}) copy-start(f32[256,2048]{1,0:T(8,128)} %convolution_multiply_fusion) | copy-start | bytes 6291460
  382.3 1.4 copy-start.8
  382.3 1.4 copy-start.10
Sparse Core Ops, SparseCore 0:
  239.3 22.5 all-gather.1
  278.9 20.2 reduce-scatter.2
  383.8 21.1 reduce-scatter.4

commit v9 on v8

--- a/solution.py
+++ b/solution.py
@@ -38,11 +38,7 @@
         l_sc[...] = jnp.zeros(l_sc.shape, jnp.float32)
         acc_sc[...] = jnp.zeros(acc_sc.shape, jnp.float32)
 
-    @pl.when(chunk < end_chunk)
-    def _():
-        key_pos = chunk * KEY_TILE + lax.broadcasted_iota(jnp.int32, (1, KEY_TILE), 1)
-        query_pos = query_first + lax.broadcasted_iota(jnp.int32, (rows, 1), 0)
-        visible = (key_pos <= query_pos) & (kseg_ref[...] == qseg_ref[...])
+    def accumulate(visible):
         score_scale = 1.0 / math.sqrt(HD)
         for h in range(heads):
             cols = slice(h * HD, (h + 1) * HD)
@@ -54,16 +50,32 @@
                 * score_scale
             )
             m_old = m_sc[h]
-            m_new = jnp.maximum(
-                m_old, jnp.max(jnp.where(visible, scores, neg_fill), axis=1, keepdims=True)
-            )
-            weights_f = jnp.where(visible, jnp.exp(scores - m_new), 0.0)
+            if visible is None:
+                m_new = jnp.maximum(m_old, jnp.max(scores, axis=1, keepdims=True))
+                weights_f = jnp.exp(scores - m_new)
+            else:
+                m_new = jnp.maximum(
+                    m_old, jnp.max(jnp.where(visible, scores, neg_fill), axis=1, keepdims=True)
+                )
+                weights_f = jnp.where(visible, jnp.exp(scores - m_new), 0.0)
             rescale = jnp.exp(m_old - m_new)
             l_sc[h] = l_sc[h] * rescale + jnp.sum(weights_f, axis=1, keepdims=True)
             acc_sc[h] = acc_sc[h] * rescale + jnp.dot(
                 weights_f.astype(jnp.bfloat16), v_ref[:, cols], preferred_element_type=jnp.float32
             )
             m_sc[h] = m_new
+
+    whole = (chunk >= bounds_ref[3]) & (chunk < bounds_ref[4])
+
+    @pl.when((chunk < end_chunk) & whole)
+    def _():
+        accumulate(None)
+
+    @pl.when((chunk < end_chunk) & jnp.logical_not(whole))
+    def _():
+        key_pos = chunk * KEY_TILE + lax.broadcasted_iota(jnp.int32, (1, KEY_TILE), 1)
+        query_pos = query_first + lax.broadcasted_iota(jnp.int32, (rows, 1), 0)
+        accumulate((key_pos <= query_pos) & (kseg_ref[...] == qseg_ref[...]))
 
     @pl.when(step == pl.num_programs(0) - 1)
     def _():
@@ -78,7 +90,12 @@
     chunks = key_count // KEY_TILE
     first_chunk = seg_first // KEY_TILE
     end_chunk = (query_first + rows + KEY_TILE - 1) // KEY_TILE
-    bounds = jnp.stack([first_chunk, end_chunk, query_first]).astype(jnp.int32)
+    last_start = jnp.sum((segment_ids < query_seg[rows - 1]).astype(jnp.int32))
+    whole_first = (last_start + KEY_TILE - 1) // KEY_TILE
+    whole_end = (query_first + 1) // KEY_TILE
+    bounds = jnp.stack([first_chunk, end_chunk, query_first, whole_first, whole_end]).astype(
+        jnp.int32
+    )
 
     def kv_map(c, b):
         return (jnp.minimum(b[0] + c, b[1] - 1), 0)

time: 414 us -> 419 us (1.012)
  starting transfers between devices: 43.9 us -> 32.1 us
  blocking collectives: 107 us -> 118 us
  waiting for transfers between devices: 145 us -> 152 us
    ppermute x6, starting transfers between devices: 28.1 us -> 16.3 us  [causal_copies(): lax.ppermute(x, axis_name, pairs)]
    all_to_all x1, blocking collectives: 82.2 us -> 92.2 us  [body(): lax.all_to_all(outgoing_part, SEQ, split_axis=0, concat_axis=0, tiled=True)]
    ppermute x6, waiting for transfers between devices: 19.2 us -> 25.8 us  [causal_copies(): lax.ppermute(x, axis_name, pairs)]
  transfers between devices with their start and end apart: 13 -> 13, of which waited for: 8 -> 9; matrix products, arithmetic and copies ran while one was open for 6% -> 6% of each run, Pallas kernels for 0% -> 0%
where the time goes in v9:
time: 419 us; the launch traced here: 420 us
  waiting for transfers between devices  152 us (36%)
  blocking collectives  118 us (28%)
  matrix products  37.6 us (9%)
  local copies, waits for them, and re-layouts  33.7 us (8%)
  starting transfers between devices  32.1 us (8%)
  other arithmetic  24.1 us (6%)
  between operations  17.6 us (4%)
  Pallas kernels  5.38 us (1%)
    all_to_all x1, blocking collectives, body(): lax.all_to_all(outgoing_part, SEQ, split_axis=0, concat_axis=0, tiled=True)  92.2 us
    all_to_all x1, waiting for transfers between devices, body(): lax.all_to_all(summed.astype(jnp.bfloat16), SEQ, split_axis=0, concat_axi...  51.6 us
    ppermute x6, waiting for transfers between devices, causal_copies(): lax.ppermute(x, axis_name, pairs)  25.8 us
    all_gather x1, waiting for transfers between devices, body(): lax.all_gather(lax.all_to_all(outgoing_part, SEQ, split_axis=0, concat_ax...  22.6 us
    reduce_scatter x1, waiting for transfers between devices, body(): lax.psum_scatter(expert_part, 'co', scatter_dimension=3, tiled=True)  20.4 us
    unnamed x53, local copies, waits for them, and re-layouts  17 us
    all_to_all x1, blocking collectives, body(): lax.all_to_all(stacked, 'sl', split_axis=2, concat_axis=1, tiled=True)  16.4 us
    reduce_scatter x1, waiting for transfers between devices, body(): lax.psum_scatter(combined.astype(jnp.bfloat16), EXP, scatter_dimension=0,...  16.4 us
  transfers between devices with their start and end apart: 13, of which 9 were waited for; matrix products, arithmetic and copies ran while one was open for 6% of the time, Pallas kernels for 0%

profile of v9, /device:TPU:1, one launch (start us, length us, event | category | flops | bytes accessed | tf_op | source)
XLA Modules:
  0.0 419.9 jit_solution(9455997613683282546)
XLA Ops:
  7.2 1.9 copy.115
  11.9 1.7 convert_reduce_fusion
  15.1 1.2 fusion.29
  17.0 1.9 pad_maximum_fusion
  18.9 2.3 copy.116
  21.2 16.4 %all_to_all.40 = bf16[3,256,4,128]{3,1,0,2:T(8,128)(2,1)S(1)} all-to-all(bf16[3,256,4,128]{3,1,0,2:T(8,128)(2,1)} %copy.116), channel_id=1, replica_groups=mesh['sh'=8,'sl'=4,'zl'=2,'co'=2] {'sl'}, dimensions={2} | all-to-all | bytes 1572864 | tf_op jit(solution)/shard_map/all_to_all | solution.py:268
  39.5 5.2 %collective-permute-start = (bf16[2,1024,128]{2,1,0:T(8,128)(2,1)}, bf16[2,1024,128]{2,1,0:T(8,128)(2,1)}, u32[]{:S(2)}, u32[]{:S(2)}) collective-permute-start(bf16[2,1024,128]{2,1,0:T(8,128)(2,1)} %bitcast.21), channel_id=1, source_target_pairs={{0,96},{16,112},{1,97},{17,113},{2,98},{18,114},{3,99},{19,115},{4... | collective-permute-start | bytes 1572872 | tf_op jit(solution)/shard_map/ppermute | solution.py:165
  45.3 5.0 %collective-permute-start.1 = (bf16[2,1024,128]{2,1,0:T(8,128)(2,1)}, bf16[2,1024,128]{2,1,0:T(8,128)(2,1)}, u32[]{:S(2)}, u32[]{:S(2)}) collective-permute-start(bf16[2,1024,128]{2,1,0:T(8,128)(2,1)} %bitcast.21), channel_id=1, source_target_pairs={{0,80},{16,96},{32,112},{1,81},{17,97},{33,113},{2,82},{18,98},{34... | collective-permute-start | bytes 1572872 | tf_op jit(solution)/shard_map/ppermute | solution.py:165
  50.3 2.0 convert_reduce_fusion.2
  56.7 1.3 collective-permute-start.2
  60.2 1.3 collective-permute-start.3
  61.5 2.1 collective-permute-start.4
  63.6 12.5 %collective-permute-done = bf16[2,1024,128]{2,1,0:T(8,128)(2,1)} collective-permute-done((bf16[2,1024,128]{2,1,0:T(8,128)(2,1)}, bf16[2,1024,128]{2,1,0:T(8,128)(2,1)}, u32[]{:S(2)}, u32[]{:S(2)}) %collective-permute-start) | collective-permute-done | bytes 524320 | tf_op jit(solution)/shard_map/ppermute | solution.py:165
  76.1 1.3 collective-permute-start.5
  77.4 1.1 bitcast_dynamic-update-slice_fusion.10
  79.7 2.1 collective-permute-done.3
  81.9 11.2 %collective-permute-done.4 = bf16[2,1024,128]{2,1,0:T(8,128)(2,1)S(1)} collective-permute-done((bf16[2,1024,128]{2,1,0:T(8,128)(2,1)}, bf16[2,1024,128]{2,1,0:T(8,128)(2,1)S(1)}, u32[]{:S(2)}, u32[]{:S(2)}) %collective-permute-start.4) | collective-permute-done | bytes 524320 | tf_op jit(solution)/shard_map/ppermute | solution.py:165
  98.4 5.4 %shard_map.157 = bf16[1024,128]{1,0:T(8,128)(2,1)S(1)} custom-call(s32[5]{0:T(128)S(1)} %stack.50.bounds_ref, bf16[1024,128]{1,0:T(8,128)(2,1)S(1)} %bitcast.129, bf16[8192,128]{1,0:T(8,128)(2,1)S(1)} %bitcast.128, bf16[8192,128]{1,0:T(8,128)(2,1)S(1)} %bitcast.127, s32[1024,1]{1,0:T(8,128)S(1)} %copy-done.1, s32[1,8192]{1,0:T(1,128)S(1)} %bitcast.131), custom_call_target="tpu_custom_call" | custom-call | flops 4294967296 | bytes 4718592 | tf_op jit(solution)/shard_map/pallas_call | solution.py:124
  104.6 8.9 %all_to_all.41 = bf16[4,256,1,128]{1,3,2,0:T(8,128)(2,1)S(1)} all-to-all(bf16[4,256,1,128]{1,3,2,0:T(8,128)(2,1)} %copy.119), channel_id=1, replica_groups=mesh['sh'=8,'sl'=4,'zl'=2,'co'=2] {'sl'}, dimensions={0} | all-to-all | bytes 524288 | tf_op jit(solution)/shard_map/all_to_all | solution.py:282
  113.5 3.3 convolution_convert_fusion.1
  116.8 3.8 collective-permute-start.6
  120.7 2.6 collective-permute-done.6
  123.3 2.2 add_convert_fusion.1
  126.5 12.4 %collective-permute-done.7 = bf16[256,1024]{1,0:T(8,128)(2,1)} collective-permute-done((bf16[256,1024]{1,0:T(8,128)(2,1)}, bf16[256,1024]{1,0:T(8,128)(2,1)}, u32[]{:S(2)}, u32[]{:S(2)}) %collective-permute-start.7) | collective-permute-done | bytes 524320 | tf_op jit(solution)/shard_map/ppermute | solution.py:175
  138.9 2.2 add_convert_fusion
  141.1 1.2 collective-permute-start.8
  143.1 2.6 fusion.5
  145.8 2.4 multiply_reduce_fusion.1
  148.2 1.3 copy-done.3
  149.8 1.3 convolution_convert_fusion
  151.1 92.2 %all_to_all.42 = bf16[32,2,32,1024]{3,2,1,0:T(8,128)(2,1)S(1)} all-to-all(bf16[32,2,32,1024]{3,2,1,0:T(8,128)(2,1)S(1)} %bitcast.132), channel_id=1, replica_groups=mesh['sh'=8,'sl'=4,'zl'=2,'co'=2] {'sh','sl'}, dimensions={0} | all-to-all | bytes 8388608 | tf_op jit(solution)/shard_map/all_to_all | solution.py:318
  243.3 2.4 copy.122
  245.8 22.6 %all-gather.2.cloned.1.call-done = bf16[32,2,32,2048]{3,2,0,1:T(8,128)(2,1)} async-done(((bf16[32,2,32,1024]{3,2,0,1:T(8,128)(2,1)}), bf16[32,2,32,2048]{3,2,0,1:T(8,128)(2,1)}) %all-gather.2.cloned.1.call-update) | async-done | bytes 8388624 | tf_op jit(solution)/shard_map/all_gather | solution.py:317
  268.4 10.1 %fusion.12 = f32[32,2,32,2,352]{4,2,3,0,1:T(8,128)S(1)} fusion(bf16[2,2,2048,352]{2,3,1,0:T(8,128)(2,1)} %param.24, bf16[32,2,32,2048]{3,2,0,1:T(8,128)(2,1)} %all-gather.2.cloned.1.call-done), kind=kOutput, calls=%fused_computation.23 | convolution fusion | flops 5905580032 | bytes 19922944 | tf_op jit(solution)/shard_map/nscd,sgde->nscge/dot_general | solution.py:226
  278.5 6.7 %convert_bitcast_fusion = bf16[32,2,32,2048]{3,2,0,1:T(8,128)(2,1)} fusion(bf16[2,352,2048]{2,1,0:T(8,128)(2,1)S(1)} %copy-done.14, f32[32,2,32,2,352]{4,2,3,0,1:T(8,128)S(1)} %fusion.12), kind=kOutput, calls=%fused_computation.2 | convolution fusion | flops 2961309696 | bytes 17039360 | tf_op jit(solution)/shard_map/nsce,sed->nscd/dot_general | solution.py:232
  285.3 20.4 %reduce-scatter.3.cloned.1.call-done = bf16[32,2,32,1024]{3,2,0,1:T(8,128)(2,1)} async-done(((bf16[32,2,32,2048]{3,2,0,1:T(8,128)(2,1)}), bf16[32,2,32,1024]{3,2,0,1:T(8,128)(2,1)}) %reduce-scatter.3.cloned.1.call-update) | async-done | bytes 4194320 | tf_op jit(solution)/shard_map/reduce_scatter | solution.py:324
  305.7 5.0 %copy.124 = bf16[32,2,32,1024]{3,2,1,0:T(8,128)(2,1)} copy(bf16[32,2,32,1024]{3,2,0,1:T(8,128)(2,1)} %reduce-scatter.3.cloned.1.call-done) | data formatting | bytes 8388608 | tf_op jit(solution)/shard_map/reduce_scatter | solution.py:324
  310.6 9.8 %all-to-all-start.3 = ((bf16[32,2,32,1024]{3,2,1,0:T(8,128)(2,1)}), bf16[32,2,32,1024]{3,2,1,0:T(8,128)(2,1)}, u32[]{:S(2)}, u32[]{:S(2)}) async-start(bf16[32,2,32,1024]{3,2,1,0:T(8,128)(2,1)} %copy.124), calls=%async_computation.4 | async-start | bytes 8388608 | tf_op jit(solution)/shard_map/all_to_all | solution.py:327
  320.7 1.6 fusion.36
  322.3 4.9 %fusion.22 = f32[256,2,768]{2,0,1:T(8,128)S(1)} fusion(bf16[2,2048,768]{2,1,0:T(8,128)(2,1)} %param.21, bf16[256,2048]{1,0:T(8,128)(2,1)} %copy-done.4), kind=kOutput, calls=%fused_computation.31 | convolution fusion | flops 1610612736 | bytes 8912896 | tf_op jit(solution)/shard_map/td,gde->tge/dot_general | solution.py:294
  327.2 2.4 convolution_multiply_fusion
  329.7 51.6 %all-to-all-done.3 = bf16[32,2,32,1024]{3,2,1,0:T(8,128)(2,1)} async-done(((bf16[32,2,32,1024]{3,2,1,0:T(8,128)(2,1)}), bf16[32,2,32,1024]{3,2,1,0:T(8,128)(2,1)}, u32[]{:S(2)}, u32[]{:S(2)}) %all-to-all-start.3) | async-done | bytes 4194336 | tf_op jit(solution)/shard_map/all_to_all | solution.py:327
  381.3 7.2 %multiply_reduce_fusion = f32[256,1024]{1,0:T(8,128)S(1)} fusion(f32[256,4]{0,1:T(4,128)S(1)} %copy-done.15, bf16[2048,1024,1]{1,0,2:T(8,128)(2,1)} %bitcast.54, s32[256,4]{0,1:T(4,128)S(1)} %multiply_add_fusion), kind=kOutput, calls=%fused_computation.10 | convolution fusion | flops 4298899456 | bytes 5251072 | tf_op jit(solution)/shard_map/dot_general | solution.py:331
  388.7 1.1 convert_element_type.134
  390.7 1.8 copy.125
  392.4 1.9 fusion.21
  395.1 16.4 %reduce-scatter.5.cloned.1.call-done = bf16[64,2048]{1,0:T(8,128)(2,1)} async-done(((bf16[256,2048]{1,0:T(8,128)(2,1)}), bf16[64,2048]{1,0:T(8,128)(2,1)}) %reduce-scatter.5.cloned.1.call-update) | async-done | bytes 262160 | tf_op jit(solution)/shard_map/reduce_scatter | solution.py:341
  411.5 1.9 add_convert_fusion.2
  (89 shorter events, 21.9 us)
Async XLA Ops:
  7.2 320.1 %copy-start = (bf16[768,2048]{1,0:T(8,128)(2,1)S(1)}, bf16[768,2048]{1,0:T(8,128)(2,1)}, u32[]{:S(2)}) copy-start(bf16[768,2048]{1,0:T(8,128)(2,1)} %param.22) | copy-start | bytes 9437188
  7.2 261.2 %all-gather.2.cloned.1.call-start = ((), (), s32[]{:S(2)}) async-start(), calls=%async_computation.6 | async-start | bytes 12582912 | tf_op jit(solution)/shard_map/all_gather | solution.py:317
  15.1 29.6 %copy-start.2 = (s32[8192]{0:T(1024)S(1)}, s32[8192]{0:T(1024)}, u32[]{:S(2)}) copy-start(s32[8192]{0:T(1024)} %param.14) | copy-start | bytes 98308
  16.3 0.7 copy-start.7
  16.3 0.7 copy-start.9
  37.7 0.9 copy-start.6
  39.5 36.6 %collective-permute-start = (bf16[2,1024,128]{2,1,0:T(8,128)(2,1)}, bf16[2,1024,128]{2,1,0:T(8,128)(2,1)}, u32[]{:S(2)}, u32[]{:S(2)}) collective-permute-start(bf16[2,1024,128]{2,1,0:T(8,128)(2,1)} %bitcast.21), channel_id=1, source_target_pairs={{0,96},{16,112},{1,97},{17,113},{2,98},{18,114},{3,99},{19,115},{4... | collective-permute-start | bytes 1572872 | tf_op jit(solution)/shard_map/ppermute | solution.py:165
  45.3 33.2 %collective-permute-start.1 = (bf16[2,1024,128]{2,1,0:T(8,128)(2,1)}, bf16[2,1024,128]{2,1,0:T(8,128)(2,1)}, u32[]{:S(2)}, u32[]{:S(2)}) collective-permute-start(bf16[2,1024,128]{2,1,0:T(8,128)(2,1)} %bitcast.21), channel_id=1, source_target_pairs={{0,80},{16,96},{32,112},{1,81},{17,97},{33,113},{2,82},{18,98},{34... | collective-permute-start | bytes 1572872 | tf_op jit(solution)/shard_map/ppermute | solution.py:165
  56.7 22.9 %collective-permute-start.2 = (bf16[2,1024,128]{2,1,0:T(8,128)(2,1)}, bf16[2,1024,128]{2,1,0:T(8,128)(2,1)S(1)}, u32[]{:S(2)}, u32[]{:S(2)}) collective-permute-start(bf16[2,1024,128]{2,1,0:T(8,128)(2,1)} %bitcast.21), channel_id=1, source_target_pairs={{0,64},{16,80},{32,96},{48,112},{1,65},{17,81},{33,97},{49,113},{2... | collective-permute-start | bytes 1572872 | tf_op jit(solution)/shard_map/ppermute | solution.py:165
  60.2 21.7 %collective-permute-start.3 = (bf16[2,1024,128]{2,1,0:T(8,128)(2,1)}, bf16[2,1024,128]{2,1,0:T(8,128)(2,1)S(1)}, u32[]{:S(2)}, u32[]{:S(2)}) collective-permute-start(bf16[2,1024,128]{2,1,0:T(8,128)(2,1)} %bitcast.21), channel_id=1, source_target_pairs={{0,48},{16,64},{32,80},{48,96},{64,112},{1,49},{17,65},{33,81},{49... | collective-permute-start | bytes 1572872 | tf_op jit(solution)/shard_map/ppermute | solution.py:165
  61.5 31.6 %collective-permute-start.4 = (bf16[2,1024,128]{2,1,0:T(8,128)(2,1)}, bf16[2,1024,128]{2,1,0:T(8,128)(2,1)S(1)}, u32[]{:S(2)}, u32[]{:S(2)}) collective-permute-start(bf16[2,1024,128]{2,1,0:T(8,128)(2,1)} %bitcast.21), channel_id=1, source_target_pairs={{0,32},{16,48},{32,64},{48,80},{64,96},{80,112},{1,33},{17,49},{33... | collective-permute-start | bytes 1572872 | tf_op jit(solution)/shard_map/ppermute | solution.py:165
  76.1 17.1 %collective-permute-start.5 = (bf16[2,1024,128]{2,1,0:T(8,128)(2,1)}, bf16[2,1024,128]{2,1,0:T(8,128)(2,1)S(1)}, u32[]{:S(2)}, u32[]{:S(2)}) collective-permute-start(bf16[2,1024,128]{2,1,0:T(8,128)(2,1)} %bitcast.21), channel_id=1, source_target_pairs={{0,16},{16,32},{32,48},{48,64},{64,80},{80,96},{96,112},{1,17},{17... | collective-permute-start | bytes 1572872 | tf_op jit(solution)/shard_map/ppermute | solution.py:165
  97.3 1.0 copy-start.1
  103.8 22.5 %copy-start.11 = (s32[256,4]{0,1:T(4,128)S(1)}, s32[256,4]{0,1:T(4,128)}, u32[]{:S(2)}) copy-start(s32[256,4]{0,1:T(4,128)} %param.26) | copy-start | bytes 12292
  103.8 39.1 %copy-start.12 = (bf16[2048]{0:T(1024)(128)(2,1)S(1)}, bf16[2048]{0:T(1024)(128)(2,1)}, u32[]{:S(2)}) copy-start(bf16[2048]{0:T(1024)(128)(2,1)} %param.20) | copy-start | bytes 12292
  116.8 6.4 %collective-permute-start.6 = (bf16[256,2048]{1,0:T(8,128)(2,1)}, bf16[256,2048]{1,0:T(8,128)(2,1)}, u32[]{:S(2)}, u32[]{:S(2)}) collective-permute-start(bf16[256,2048]{1,0:T(8,128)(2,1)} %convolution_convert_fusion.1), channel_id=1, source_target_pairs={{0,1},{1,0},{2,3},{3,2},{4,5},{5,4},{6,7},{7,6},{8,9},{9,8},{10,11... | collective-permute-start | bytes 3145736 | tf_op jit(solution)/shard_map/ppermute | solution.py:173
  125.5 13.4 %collective-permute-start.7 = (bf16[256,1024]{1,0:T(8,128)(2,1)}, bf16[256,1024]{1,0:T(8,128)(2,1)}, u32[]{:S(2)}, u32[]{:S(2)}) collective-permute-start(bf16[256,1024]{1,0:T(8,128)(2,1)} %add_convert_fusion.1), channel_id=1, source_target_pairs={{0,2},{2,0},{1,3},{3,1},{4,6},{6,4},{5,7},{7,5},{8,10},{10,8},{9,1... | collective-permute-start | bytes 1572872 | tf_op jit(solution)/shard_map/ppermute | solution.py:175
  141.1 4.7 %collective-permute-start.8 = (bf16[256,1024]{1,0:T(8,128)(2,1)}, bf16[256,1024]{1,0:T(8,128)(2,1)}, u32[]{:S(2)}, u32[]{:S(2)}) collective-permute-start(bf16[256,1024]{1,0:T(8,128)(2,1)} %add_convert_fusion), channel_id=1, source_target_pairs={{0,1},{1,0},{2,3},{3,2},{4,5},{5,4},{6,7},{7,6},{8,9},{9,8},{10,11... | collective-permute-start | bytes 1572872 | tf_op jit(solution)/shard_map/ppermute | solution.py:178
  148.2 1.3 copy-start.3
  149.8 1.3 copy-start.4
  245.7 59.9 %reduce-scatter.3.cloned.1.call-start = ((), (), s32[]{:S(2)}) async-start(), calls=%async_computation.7 | async-start | bytes 12582912 | tf_op jit(solution)/shard_map/reduce_scatter | solution.py:324
  268.4 10.2 %copy-start.14 = (bf16[2,352,2048]{2,1,0:T(8,128)(2,1)S(1)}, bf16[2,352,2048]{2,1,0:T(8,128)(2,1)}, u32[]{:S(2)}) copy-start(bf16[2,352,2048]{2,1,0:T(8,128)(2,1)} %param.25) | copy-start | bytes 8650756
  310.6 10.0 %copy-start.13 = (bf16[2048]{0:T(1024)(128)(2,1)S(1)}, bf16[2048]{0:T(1024)(128)(2,1)}, u32[]{:S(2)}) copy-start(bf16[2048]{0:T(1024)(128)(2,1)} %param.23) | copy-start | bytes 12292
  310.6 70.7 %all-to-all-start.3 = ((bf16[32,2,32,1024]{3,2,1,0:T(8,128)(2,1)}), bf16[32,2,32,1024]{3,2,1,0:T(8,128)(2,1)}, u32[]{:S(2)}, u32[]{:S(2)}) async-start(bf16[32,2,32,1024]{3,2,1,0:T(8,128)(2,1)} %copy.124), calls=%async_computation.4 | async-start | bytes 8388608 | tf_op jit(solution)/shard_map/all_to_all | solution.py:327
  320.4 91.1 %reduce-scatter.5.cloned.1.call-start = ((), (), s32[]{:S(2)}) async-start(), calls=%async_computation.8 | async-start | bytes 1310720 | tf_op jit(solution)/shard_map/reduce_scatter | solution.py:341
  327.2 54.1 %copy-start.15 = (f32[256,4]{0,1:T(4,128)S(1)}, f32[256,4]{0,1:T(4,128)}, u32[]{:S(2)}) copy-start(f32[256,4]{0,1:T(4,128)} %param.27) | copy-start | bytes 12292
  381.3 7.2 %copy-start.5 = (f32[256,2048]{1,0:T(8,128)S(1)}, f32[256,2048]{1,0:T(8,128)}, u32[]{:S(2)}) copy-start(f32[256,2048]{1,0:T(8,128)} %convolution_multiply_fusion) | copy-start | bytes 6291460
  388.5 1.4 copy-start.8
  388.5 1.4 copy-start.10
Sparse Core Ops, SparseCore 0:
  245.9 22.4 all-gather.1
  285.4 20.2 reduce-scatter.2
  390.0 21.3 reduce-scatter.4
